TPU v7x, 512 devices: a whole 4x4x16 slice. The times are simulated.
512 devices in a mesh: ta: 32 (over x_hi, z), gz: 8 (over y, x_lo), gy: 2 (over core).
Axes of the slice: x: 4 (x_hi: 2, x_lo: 2; x = x_hi * 2 + x_lo), y: 4, z: 16, core: 2. Of those that a mesh axis runs over, the one named last changes fastest.
Arguments:
- source_field: bfloat16 [32, 16, 4, 2, 256, 128], P('ta', 'gz', 'gy'), may hold values from -6 to 6
- clover: bfloat16 [32, 16, 4, 2, 128, 128], P('ta', 'gz', 'gy'), may hold values from -0.1875 to 0.1875
- forward: bfloat16 [4, 32, 16, 4, 2, 128, 128], P(None, 'ta', 'gz', 'gy'), may hold values from -0.1875 to 0.1875
- backward: bfloat16 [4, 32, 16, 4, 2, 128, 128], P(None, 'ta', 'gz', 'gy'), may hold values from -0.1875 to 0.1875
- restrict_blocks: bfloat16 [32, 16, 4, 2, 128, 128], P('ta', 'gz', 'gy'), may hold values from -0.1875 to 0.1875
Outputs:
- second_image: bfloat16 [32, 16, 4, 2, 256, 128], P('ta', 'gz', 'gy')
- restricted: bfloat16 [32, 16, 256, 128], P('ta')
All inputs are finite; a program needn't handle non-finite values.
Results may differ from a plain program's by a relative error of at most 0.0064.
Values may be sent and summed in bfloat16 or wider, within the bound.
No kernel may reach another device: no remote copies, remote signals or barrier semaphores. Data moves between devices by JAX's collectives and lax.ppermute only.
A program may use at most 64 MiB of HBM per device.

v0:
```python
import jax
import jax.numpy as jnp
from jax import lax
from jax.sharding import PartitionSpec as P


def apply_block(blocks, vector):
    return jnp.einsum("tzyxij,tzyxrj->tzyxri", blocks, vector, preferred_element_type=jnp.float32)


def formed(blocks, vector):
    return lax.optimization_barrier(apply_block(blocks, vector).astype(jnp.bfloat16))


def ring(n, step):
    return [(i, (i + step) % n) for i in range(n)]


def take(block, dim, start, stop):
    return lax.slice_in_dim(block, start, stop, axis=dim)


def neighbours(vector, pulled, dim, axis):
    count = lax.axis_size(axis)
    size = vector.shape[dim]
    first = take(vector, dim, 0, 1)
    last = take(pulled, dim, size - 1, size)
    if count == 2:
        both = lax.ppermute(jnp.stack([first, last]), axis, ring(2, 1))
        got_v, got_p = both[0], both[1]
    else:
        got_v = lax.ppermute(first, axis, ring(count, -1))
        got_p = lax.ppermute(last, axis, ring(count, 1))
    ahead = jnp.concatenate([take(vector, dim, 1, size), got_v], axis=dim)
    behind = jnp.concatenate([got_p, take(pulled, dim, 0, size - 1)], axis=dim)
    return ahead, behind


AXES = ((0, "ta"), (1, "gz"), (2, "gy"))


def operate(vector, clover, forward, backward):
    pulled = [formed(backward[m], vector) for m in range(4)]
    terms = []
    pulls = []
    for m, axis in AXES:
        ahead, behind = neighbours(vector, pulled[m], m, axis)
        terms.append(apply_block(forward[m], ahead))
        pulls.append(behind)
    terms.append(apply_block(forward[3], jnp.roll(vector, -1, axis=3)))
    pulls.append(jnp.roll(pulled[3], 1, axis=3))
    total = apply_block(clover, vector)
    for term in terms:
        total = total + term
    for pull in pulls:
        total = total + pull.astype(jnp.float32)
    return total.astype(jnp.bfloat16)


def gather_pieces(piece):
    nz = lax.axis_size("gz")
    ny = lax.axis_size("gy")
    assert nz == 8 and ny == 2
    g = lax.axis_index("gz")
    c = lax.axis_index("gy")
    other = lax.ppermute(piece, "gz", [(i, i ^ 1) for i in range(nz)])
    pair = jnp.where(g % 2 == 1, jnp.stack([other, piece]), jnp.stack([piece, other]))
    from_far = lax.ppermute(pair, "gz", ring(nz, 4))
    from_prev = lax.ppermute(pair, "gz", ring(nz, 2))
    from_next = lax.ppermute(pair, "gz", ring(nz, -2))
    rel = jnp.stack([pair, from_next, from_far, from_prev])
    pairs = nz // 2
    doubled = jnp.concatenate([rel, rel], axis=0)
    absolute = lax.dynamic_slice_in_dim(doubled, pairs - g // 2, pairs, axis=0)
    absolute = absolute.reshape(nz, *piece.shape)
    partner = lax.ppermute(absolute, "gy", ring(2, 1))
    full = jnp.where(
        c == 0, jnp.stack([absolute, partner], axis=1), jnp.stack([partner, absolute], axis=1)
    )
    return full.reshape(1, nz * ny, *piece.shape)


def per_device_body(source_field, clover, forward, backward, restrict_blocks):
    first_image = operate(source_field, clover, forward, backward)
    second_image = operate(first_image, clover, forward, backward)
    partial_sum = jnp.einsum(
        "tzyxij,tzyxrj->ri", restrict_blocks, second_image, preferred_element_type=jnp.float32
    )
    restricted = gather_pieces(partial_sum.astype(jnp.bfloat16))
    return (second_image, restricted)


def solution(mesh):
    return jax.shard_map(
        per_device_body,
        mesh=mesh,
        in_specs=(
            P("ta", "gz", "gy", None, None, None),
            P("ta", "gz", "gy", None, None, None),
            P(None, "ta", "gz", "gy", None, None, None),
            P(None, "ta", "gz", "gy", None, None, None),
            P("ta", "gz", "gy", None, None, None),
        ),
        out_specs=(P("ta", "gz", "gy", None, None, None), P("ta", None, None, None)),
        check_vma=False,
    )
```

profile of v0, /device:TPU:1, one launch (start us, length us, event | category | flops | bytes accessed | tf_op | source)
XLA Modules:
  0.0 108.4 jit_solution(13285694534187286118)
XLA Ops:
  0.7 14.5 %collective-permute-start = (bf16[1,2,2,2,256,128]{5,4,3,2,1,0:T(8,128)(2,1)}, bf16[1,2,2,2,256,128]{5,4,3,2,1,0:T(8,128)(2,1)S(1)}, u32[]{:S(2)}, u32[]{:S(2)}) collective-permute-start(bf16[1,2,2,2,256,128]{5,4,3,2,1,0:T(8,128)(2,1)} %param.5), channel_id=1, source_target_pairs={{0,496},{16,0},{32,16},{48,32},{64,48},{80,64},{96,80},{112,96},{1... | collective-permute-start | bytes 1572872 | tf_op jit(solution)/shard_map/ppermute | solution.py:32
  15.2 1.1 slice_bitcast_fusion.15
  16.3 1.2 %fusion.3 = bf16[1,2,2,2,256,128]{5,4,3,2,1,0:T(8,128)(2,1)S(1)} fusion(bf16[1,2,2,2,256,128]{5,4,3,2,1,0:T(8,128)(2,1)S(1)} %copy-done.1, bf16[4,1,2,2,2,128,128]{6,5,4,3,2,1,0:T(8,128)(2,1)} %param.8), kind=kOutput, calls=%fused_computation.18 | convolution fusion | flops 67371008 | bytes 1310720 | tf_op jit(solution)/shard_map/tzyxij,tzyxrj->tzyxri/dot_general | solution.py:8
  17.6 3.0 %collective-permute-start.2 = (bf16[2,1,2,1,2,256,128]{6,5,4,2,3,1,0:T(8,128)(2,1)S(1)}, bf16[2,1,2,1,2,256,128]{6,5,4,2,3,1,0:T(8,128)(2,1)S(1)}, u32[]{:S(2)}, u32[]{:S(2)}) collective-permute-start(bf16[2,1,2,1,2,256,128]{6,5,4,2,3,1,0:T(8,128)(2,1)S(1)} %pad_maximum_fusion), channel_id=1, source_target_pairs={{0,1},{1,0},{2,3},{3,2},{4,5},{5,4},{6,7},{7,6},{8,9},{9,8},{10,11... | collective-permute-start | bytes 1572872 | tf_op jit(solution)/shard_map/ppermute | solution.py:29
  20.7 4.7 %collective-permute-start.1 = (bf16[1,1,2,2,256,128]{5,4,3,2,1,0:T(8,128)(2,1)S(1)}, bf16[1,1,2,2,256,128]{5,4,3,2,1,0:T(8,128)(2,1)S(1)}, u32[]{:S(2)}, u32[]{:S(2)}) collective-permute-start(bf16[1,1,2,2,256,128]{5,4,3,2,1,0:T(8,128)(2,1)S(1)} %get-tuple-element.29), channel_id=1, source_target_pairs={{0,14},{2,0},{4,2},{6,4},{8,6},{10,8},{12,10},{14,12},{1,15},{3,1}... | collective-permute-start | bytes 786440 | tf_op jit(solution)/shard_map/ppermute | solution.py:32
  25.4 0.3 fusion.5
  25.7 1.9 %collective-permute-start.4 = (bf16[1,1,2,2,256,128]{5,4,3,2,1,0:T(8,128)(2,1)S(1)}, bf16[1,1,2,2,256,128]{5,4,3,2,1,0:T(8,128)(2,1)S(1)}, u32[]{:S(2)}, u32[]{:S(2)}) collective-permute-start(bf16[1,1,2,2,256,128]{5,4,3,2,1,0:T(8,128)(2,1)S(1)} %get-tuple-element.38), channel_id=1, source_target_pairs={{0,2},{2,4},{4,6},{6,8},{8,10},{10,12},{12,14},{14,0},{1,3},{3,5},... | collective-permute-start | bytes 786440 | tf_op jit(solution)/shard_map/ppermute | solution.py:33
  27.7 0.3 fusion.4
  28.0 1.9 %collective-permute-start.3 = (bf16[1,2,2,2,256,128]{5,4,3,2,1,0:T(8,128)(2,1)S(1)}, bf16[1,2,2,2,256,128]{5,4,3,2,1,0:T(8,128)(2,1)S(1)}, u32[]{:S(2)}, u32[]{:S(2)}) collective-permute-start(bf16[1,2,2,2,256,128]{5,4,3,2,1,0:T(8,128)(2,1)S(1)} %fusion.4), channel_id=1, source_target_pairs={{0,16},{16,32},{32,48},{48,64},{64,80},{80,96},{96,112},{112,128},... | collective-permute-start | bytes 1572872 | tf_op jit(solution)/shard_map/ppermute | solution.py:33
  29.9 0.1 slice_bitcast_fusion.8
  30.0 0.3 fusion.23
  30.3 0.3 fusion.6
  30.7 1.1 %copy-done.3 = bf16[4,1,2,2,2,128,128]{6,5,4,3,2,1,0:T(8,128)(2,1)S(1)} copy-done((bf16[4,1,2,2,2,128,128]{6,5,4,3,2,1,0:T(8,128)(2,1)S(1)}, bf16[4,1,2,2,2,128,128]{6,5,4,3,2,1,0:T(8,128)(2,1)}, u32[]{:S(2)}) %copy-start.3) | copy-done | bytes 1048600
  31.8 0.1 slice_bitcast_fusion.11
  32.0 0.3 convolution_add_fusion.6
  32.3 0.3 fusion.31
  32.6 0.3 fusion.2
  32.9 16.8 %collective-permute-done.4 = bf16[1,1,2,2,256,128]{5,4,3,2,1,0:T(8,128)(2,1)S(1)} collective-permute-done((bf16[1,1,2,2,256,128]{5,4,3,2,1,0:T(8,128)(2,1)S(1)}, bf16[1,1,2,2,256,128]{5,4,3,2,1,0:T(8,128)(2,1)S(1)}, u32[]{:S(2)}, u32[]{:S(2)}) %collective-permute-start.4) | collective-permute-done | bytes 262176 | tf_op jit(solution)/shard_map/ppermute | solution.py:33
  49.8 0.5 add_convert_fusion.1
  50.3 1.9 %collective-permute-start.5 = (bf16[1,2,2,2,256,128]{5,4,3,2,1,0:T(8,128)(2,1)S(1)}, bf16[1,2,2,2,256,128]{5,4,3,2,1,0:T(8,128)(2,1)S(1)}, u32[]{:S(2)}, u32[]{:S(2)}) collective-permute-start(bf16[1,2,2,2,256,128]{5,4,3,2,1,0:T(8,128)(2,1)S(1)} %add_convert_fusion.1), channel_id=1, source_target_pairs={{0,496},{16,0},{32,16},{48,32},{64,48},{80,64},{96,80},{112,96},{1... | collective-permute-start | bytes 1572872 | tf_op jit(solution)/shard_map/ppermute | solution.py:32
  52.3 2.4 %collective-permute-start.6 = (bf16[1,1,2,2,256,128]{5,4,3,2,1,0:T(8,128)(2,1)S(1)}, bf16[1,1,2,2,256,128]{5,4,3,2,1,0:T(8,128)(2,1)S(1)}, u32[]{:S(2)}, u32[]{:S(2)}) collective-permute-start(bf16[1,1,2,2,256,128]{5,4,3,2,1,0:T(8,128)(2,1)S(1)} %get-tuple-element.19), channel_id=1, source_target_pairs={{0,14},{2,0},{4,2},{6,4},{8,6},{10,8},{12,10},{14,12},{1,15},{3,1}... | collective-permute-start | bytes 786440 | tf_op jit(solution)/shard_map/ppermute | solution.py:32
  54.7 0.3 fusion.7
  55.2 3.3 %collective-permute-start.7 = (bf16[2,1,2,1,2,256,128]{6,5,4,2,3,1,0:T(8,128)(2,1)S(1)}, bf16[2,1,2,1,2,256,128]{6,5,4,2,3,1,0:T(8,128)(2,1)S(1)}, u32[]{:S(2)}, u32[]{:S(2)}) collective-permute-start(bf16[2,1,2,1,2,256,128]{6,5,4,2,3,1,0:T(8,128)(2,1)S(1)} %pad_maximum_fusion.1), channel_id=1, source_target_pairs={{0,1},{1,0},{2,3},{3,2},{4,5},{5,4},{6,7},{7,6},{8,9},{9,8},{10,11... | collective-permute-start | bytes 1572872 | tf_op jit(solution)/shard_map/ppermute | solution.py:29
  58.5 0.3 fusion.9
  58.8 2.6 %collective-permute-start.9 = (bf16[1,1,2,2,256,128]{5,4,3,1,2,0:T(8,128)(2,1)S(1)}, bf16[1,1,2,2,256,128]{5,4,3,1,2,0:T(8,128)(2,1)S(1)}, u32[]{:S(2)}, u32[]{:S(2)}) collective-permute-start(bf16[1,1,2,2,256,128]{5,4,3,1,2,0:T(8,128)(2,1)S(1)} %get-tuple-element.24), channel_id=1, source_target_pairs={{0,2},{2,4},{4,6},{6,8},{8,10},{10,12},{12,14},{14,0},{1,3},{3,5},... | collective-permute-start | bytes 786440 | tf_op jit(solution)/shard_map/ppermute | solution.py:33
  61.5 0.3 fusion.10
  61.8 0.3 fusion.8
  62.1 3.6 %collective-permute-start.8 = (bf16[1,2,2,2,256,128]{5,4,3,1,2,0:T(8,128)(2,1)S(1)}, bf16[1,2,2,2,256,128]{5,4,3,1,2,0:T(8,128)(2,1)S(1)}, u32[]{:S(2)}, u32[]{:S(2)}) collective-permute-start(bf16[1,2,2,2,256,128]{5,4,3,1,2,0:T(8,128)(2,1)S(1)} %fusion.8), channel_id=1, source_target_pairs={{0,16},{16,32},{32,48},{48,64},{64,80},{80,96},{96,112},{112,128},... | collective-permute-start | bytes 1572872 | tf_op jit(solution)/shard_map/ppermute | solution.py:33
  65.8 0.3 fusion.37
  66.1 0.3 convolution_add_fusion.3
  66.4 0.3 convolution_add_fusion.2
  66.8 0.3 convolution_add_fusion.1
  67.1 3.6 %collective-permute-done.9 = bf16[1,1,2,2,256,128]{5,4,3,1,2,0:T(8,128)(2,1)S(1)} collective-permute-done((bf16[1,1,2,2,256,128]{5,4,3,1,2,0:T(8,128)(2,1)S(1)}, bf16[1,1,2,2,256,128]{5,4,3,1,2,0:T(8,128)(2,1)S(1)}, u32[]{:S(2)}, u32[]{:S(2)}) %collective-permute-start.9) | collective-permute-done | bytes 262176 | tf_op jit(solution)/shard_map/ppermute | solution.py:33
  70.7 10.1 %collective-permute-done.8 = bf16[1,2,2,2,256,128]{5,4,3,1,2,0:T(8,128)(2,1)S(1)} collective-permute-done((bf16[1,2,2,2,256,128]{5,4,3,1,2,0:T(8,128)(2,1)S(1)}, bf16[1,2,2,2,256,128]{5,4,3,1,2,0:T(8,128)(2,1)S(1)}, u32[]{:S(2)}, u32[]{:S(2)}) %collective-permute-start.8) | collective-permute-done | bytes 524320 | tf_op jit(solution)/shard_map/ppermute | solution.py:33
  80.8 0.5 add_convert_fusion
  81.3 0.4 copy-done.4
  81.7 0.3 fusion.11
  82.0 3.1 %collective-permute-start.10 = (bf16[256,128]{1,0:T(8,128)(2,1)S(1)}, bf16[256,128]{1,0:T(8,128)(2,1)S(1)}, u32[]{:S(2)}, u32[]{:S(2)}) collective-permute-start(bf16[256,128]{1,0:T(8,128)(2,1)S(1)} %fusion.11), channel_id=1, source_target_pairs={{0,2},{2,0},{4,6},{6,4},{8,10},{10,8},{12,14},{14,12},{1,3},{3,1},... | collective-permute-start | bytes 196616 | tf_op jit(solution)/shard_map/ppermute | solution.py:66
  85.2 1.9 %collective-permute-done.10 = bf16[256,128]{1,0:T(8,128)(2,1)S(1)} collective-permute-done((bf16[256,128]{1,0:T(8,128)(2,1)S(1)}, bf16[256,128]{1,0:T(8,128)(2,1)S(1)}, u32[]{:S(2)}, u32[]{:S(2)}) %collective-permute-start.10) | collective-permute-done | bytes 65568 | tf_op jit(solution)/shard_map/ppermute | solution.py:66
  87.0 3.6 %collective-permute-start.11 = (bf16[2,256,128]{2,1,0:T(8,128)(2,1)S(1)}, bf16[2,256,128]{2,1,0:T(8,128)(2,1)S(1)}, u32[]{:S(2)}, u32[]{:S(2)}) collective-permute-start(bf16[2,256,128]{2,1,0:T(8,128)(2,1)S(1)} %maximum_select_fusion.2), channel_id=1, source_target_pairs={{0,12},{2,14},{4,0},{6,2},{8,4},{10,6},{12,8},{14,10},{1,13},{3,15... | collective-permute-start | bytes 393224 | tf_op jit(solution)/shard_map/ppermute | solution.py:70
  90.7 2.3 %collective-permute-start.12 = (bf16[2,256,128]{2,1,0:T(8,128)(2,1)S(1)}, bf16[2,256,128]{2,1,0:T(8,128)(2,1)S(1)}, u32[]{:S(2)}, u32[]{:S(2)}) collective-permute-start(bf16[2,256,128]{2,1,0:T(8,128)(2,1)S(1)} %maximum_select_fusion.2), channel_id=1, source_target_pairs={{0,8},{2,10},{4,12},{6,14},{8,0},{10,2},{12,4},{14,6},{1,9},{3,11}... | collective-permute-start | bytes 393224 | tf_op jit(solution)/shard_map/ppermute | solution.py:68
  93.0 2.1 %collective-permute-start.13 = (bf16[2,256,128]{2,1,0:T(8,128)(2,1)S(1)}, bf16[2,256,128]{2,1,0:T(8,128)(2,1)S(1)}, u32[]{:S(2)}, u32[]{:S(2)}) collective-permute-start(bf16[2,256,128]{2,1,0:T(8,128)(2,1)S(1)} %maximum_select_fusion.2), channel_id=1, source_target_pairs={{0,4},{2,6},{4,8},{6,10},{8,12},{10,14},{12,0},{14,2},{1,5},{3,7},... | collective-permute-start | bytes 393224 | tf_op jit(solution)/shard_map/ppermute | solution.py:69
  95.2 2.7 %collective-permute-done.12 = bf16[2,256,128]{2,1,0:T(8,128)(2,1)S(1)} collective-permute-done((bf16[2,256,128]{2,1,0:T(8,128)(2,1)S(1)}, bf16[2,256,128]{2,1,0:T(8,128)(2,1)S(1)}, u32[]{:S(2)}, u32[]{:S(2)}) %collective-permute-start.12) | collective-permute-done | bytes 131104 | tf_op jit(solution)/shard_map/ppermute | solution.py:68
  97.9 3.0 %collective-permute-done.13 = bf16[2,256,128]{2,1,0:T(8,128)(2,1)S(1)} collective-permute-done((bf16[2,256,128]{2,1,0:T(8,128)(2,1)S(1)}, bf16[2,256,128]{2,1,0:T(8,128)(2,1)S(1)}, u32[]{:S(2)}, u32[]{:S(2)}) %collective-permute-start.13) | collective-permute-done | bytes 131104 | tf_op jit(solution)/shard_map/ppermute | solution.py:69
  101.1 4.7 %collective-permute-start.14 = (bf16[8,256,128]{2,1,0:T(8,128)(2,1)S(1)}, bf16[8,256,128]{2,1,0:T(8,128)(2,1)S(1)}, u32[]{:S(2)}, u32[]{:S(2)}) collective-permute-start(bf16[8,256,128]{2,1,0:T(8,128)(2,1)S(1)} %bitcast.166), channel_id=1, source_target_pairs={{0,1},{1,0},{2,3},{3,2},{4,5},{5,4},{6,7},{7,6},{8,9},{9,8},{10,11... | collective-permute-start | bytes 1572872 | tf_op jit(solution)/shard_map/ppermute | solution.py:76
  105.8 0.8 copy.24
  106.6 0.7 collective-permute-done.14
  107.3 1.1 maximum_select_fusion
  (40 shorter events, 0.9 us)
Async XLA Ops:
  0.6 29.4 %copy-start = (bf16[1,2,2,2,128,128]{5,4,3,2,1,0:T(8,128)(2,1)S(1)}, bf16[1,2,2,2,128,128]{5,4,3,2,1,0:T(8,128)(2,1)}, u32[]{:S(2)}) copy-start(bf16[1,2,2,2,128,128]{5,4,3,2,1,0:T(8,128)(2,1)} %param.6) | copy-start | bytes 786436
  0.6 15.6 %copy-start.1 = (bf16[1,2,2,2,256,128]{5,4,3,2,1,0:T(8,128)(2,1)S(1)}, bf16[1,2,2,2,256,128]{5,4,3,2,1,0:T(8,128)(2,1)}, u32[]{:S(2)}) copy-start(bf16[1,2,2,2,256,128]{5,4,3,2,1,0:T(8,128)(2,1)} %param.5) | copy-start | bytes 1572868
  0.7 31.3 %collective-permute-start = (bf16[1,2,2,2,256,128]{5,4,3,2,1,0:T(8,128)(2,1)}, bf16[1,2,2,2,256,128]{5,4,3,2,1,0:T(8,128)(2,1)S(1)}, u32[]{:S(2)}, u32[]{:S(2)}) collective-permute-start(bf16[1,2,2,2,256,128]{5,4,3,2,1,0:T(8,128)(2,1)} %param.5), channel_id=1, source_target_pairs={{0,496},{16,0},{32,16},{48,32},{64,48},{80,64},{96,80},{112,96},{1... | collective-permute-start | bytes 1572872 | tf_op jit(solution)/shard_map/ppermute | solution.py:32
  17.6 7.8 %copy-start.2 = (bf16[4,1,2,2,2,128,128]{6,5,4,3,2,1,0:T(8,128)(2,1)S(1)}, bf16[4,1,2,2,2,128,128]{6,5,4,3,2,1,0:T(8,128)(2,1)}, u32[]{:S(2)}) copy-start(bf16[4,1,2,2,2,128,128]{6,5,4,3,2,1,0:T(8,128)(2,1)} %param.8) | copy-start | bytes 3145732
  17.6 14.6 %collective-permute-start.2 = (bf16[2,1,2,1,2,256,128]{6,5,4,2,3,1,0:T(8,128)(2,1)S(1)}, bf16[2,1,2,1,2,256,128]{6,5,4,2,3,1,0:T(8,128)(2,1)S(1)}, u32[]{:S(2)}, u32[]{:S(2)}) collective-permute-start(bf16[2,1,2,1,2,256,128]{6,5,4,2,3,1,0:T(8,128)(2,1)S(1)} %pad_maximum_fusion), channel_id=1, source_target_pairs={{0,1},{1,0},{2,3},{3,2},{4,5},{5,4},{6,7},{7,6},{8,9},{9,8},{10,11... | collective-permute-start | bytes 1572872 | tf_op jit(solution)/shard_map/ppermute | solution.py:29
  20.7 11.9 %collective-permute-start.1 = (bf16[1,1,2,2,256,128]{5,4,3,2,1,0:T(8,128)(2,1)S(1)}, bf16[1,1,2,2,256,128]{5,4,3,2,1,0:T(8,128)(2,1)S(1)}, u32[]{:S(2)}, u32[]{:S(2)}) collective-permute-start(bf16[1,1,2,2,256,128]{5,4,3,2,1,0:T(8,128)(2,1)S(1)} %get-tuple-element.29), channel_id=1, source_target_pairs={{0,14},{2,0},{4,2},{6,4},{8,6},{10,8},{12,10},{14,12},{1,15},{3,1}... | collective-permute-start | bytes 786440 | tf_op jit(solution)/shard_map/ppermute | solution.py:32
  25.7 24.0 %collective-permute-start.4 = (bf16[1,1,2,2,256,128]{5,4,3,2,1,0:T(8,128)(2,1)S(1)}, bf16[1,1,2,2,256,128]{5,4,3,2,1,0:T(8,128)(2,1)S(1)}, u32[]{:S(2)}, u32[]{:S(2)}) collective-permute-start(bf16[1,1,2,2,256,128]{5,4,3,2,1,0:T(8,128)(2,1)S(1)} %get-tuple-element.38), channel_id=1, source_target_pairs={{0,2},{2,4},{4,6},{6,8},{8,10},{10,12},{12,14},{14,0},{1,3},{3,5},... | collective-permute-start | bytes 786440 | tf_op jit(solution)/shard_map/ppermute | solution.py:33
  28.0 21.8 %collective-permute-start.3 = (bf16[1,2,2,2,256,128]{5,4,3,2,1,0:T(8,128)(2,1)S(1)}, bf16[1,2,2,2,256,128]{5,4,3,2,1,0:T(8,128)(2,1)S(1)}, u32[]{:S(2)}, u32[]{:S(2)}) collective-permute-start(bf16[1,2,2,2,256,128]{5,4,3,2,1,0:T(8,128)(2,1)S(1)} %fusion.4), channel_id=1, source_target_pairs={{0,16},{16,32},{32,48},{48,64},{64,80},{80,96},{96,112},{112,128},... | collective-permute-start | bytes 1572872 | tf_op jit(solution)/shard_map/ppermute | solution.py:33
  30.6 1.2 %copy-start.3 = (bf16[4,1,2,2,2,128,128]{6,5,4,3,2,1,0:T(8,128)(2,1)S(1)}, bf16[4,1,2,2,2,128,128]{6,5,4,3,2,1,0:T(8,128)(2,1)}, u32[]{:S(2)}) copy-start(bf16[4,1,2,2,2,128,128]{6,5,4,3,2,1,0:T(8,128)(2,1)} %param.7) | copy-start | bytes 3145732
  50.3 15.8 %collective-permute-start.5 = (bf16[1,2,2,2,256,128]{5,4,3,2,1,0:T(8,128)(2,1)S(1)}, bf16[1,2,2,2,256,128]{5,4,3,2,1,0:T(8,128)(2,1)S(1)}, u32[]{:S(2)}, u32[]{:S(2)}) collective-permute-start(bf16[1,2,2,2,256,128]{5,4,3,2,1,0:T(8,128)(2,1)S(1)} %add_convert_fusion.1), channel_id=1, source_target_pairs={{0,496},{16,0},{32,16},{48,32},{64,48},{80,64},{96,80},{112,96},{1... | collective-permute-start | bytes 1572872 | tf_op jit(solution)/shard_map/ppermute | solution.py:32
  52.3 14.1 %collective-permute-start.6 = (bf16[1,1,2,2,256,128]{5,4,3,2,1,0:T(8,128)(2,1)S(1)}, bf16[1,1,2,2,256,128]{5,4,3,2,1,0:T(8,128)(2,1)S(1)}, u32[]{:S(2)}, u32[]{:S(2)}) collective-permute-start(bf16[1,1,2,2,256,128]{5,4,3,2,1,0:T(8,128)(2,1)S(1)} %get-tuple-element.19), channel_id=1, source_target_pairs={{0,14},{2,0},{4,2},{6,4},{8,6},{10,8},{12,10},{14,12},{1,15},{3,1}... | collective-permute-start | bytes 786440 | tf_op jit(solution)/shard_map/ppermute | solution.py:32
  55.2 11.6 %collective-permute-start.7 = (bf16[2,1,2,1,2,256,128]{6,5,4,2,3,1,0:T(8,128)(2,1)S(1)}, bf16[2,1,2,1,2,256,128]{6,5,4,2,3,1,0:T(8,128)(2,1)S(1)}, u32[]{:S(2)}, u32[]{:S(2)}) collective-permute-start(bf16[2,1,2,1,2,256,128]{6,5,4,2,3,1,0:T(8,128)(2,1)S(1)} %pad_maximum_fusion.1), channel_id=1, source_target_pairs={{0,1},{1,0},{2,3},{3,2},{4,5},{5,4},{6,7},{7,6},{8,9},{9,8},{10,11... | collective-permute-start | bytes 1572872 | tf_op jit(solution)/shard_map/ppermute | solution.py:29
  58.8 11.9 %collective-permute-start.9 = (bf16[1,1,2,2,256,128]{5,4,3,1,2,0:T(8,128)(2,1)S(1)}, bf16[1,1,2,2,256,128]{5,4,3,1,2,0:T(8,128)(2,1)S(1)}, u32[]{:S(2)}, u32[]{:S(2)}) collective-permute-start(bf16[1,1,2,2,256,128]{5,4,3,1,2,0:T(8,128)(2,1)S(1)} %get-tuple-element.24), channel_id=1, source_target_pairs={{0,2},{2,4},{4,6},{6,8},{8,10},{10,12},{12,14},{14,0},{1,3},{3,5},... | collective-permute-start | bytes 786440 | tf_op jit(solution)/shard_map/ppermute | solution.py:33
  62.1 18.7 %collective-permute-start.8 = (bf16[1,2,2,2,256,128]{5,4,3,1,2,0:T(8,128)(2,1)S(1)}, bf16[1,2,2,2,256,128]{5,4,3,1,2,0:T(8,128)(2,1)S(1)}, u32[]{:S(2)}, u32[]{:S(2)}) collective-permute-start(bf16[1,2,2,2,256,128]{5,4,3,1,2,0:T(8,128)(2,1)S(1)} %fusion.8), channel_id=1, source_target_pairs={{0,16},{16,32},{32,48},{48,64},{64,80},{80,96},{96,112},{112,128},... | collective-permute-start | bytes 1572872 | tf_op jit(solution)/shard_map/ppermute | solution.py:33
  80.8 1.0 copy-start.4
  82.0 5.0 %collective-permute-start.10 = (bf16[256,128]{1,0:T(8,128)(2,1)S(1)}, bf16[256,128]{1,0:T(8,128)(2,1)S(1)}, u32[]{:S(2)}, u32[]{:S(2)}) collective-permute-start(bf16[256,128]{1,0:T(8,128)(2,1)S(1)} %fusion.11), channel_id=1, source_target_pairs={{0,2},{2,0},{4,6},{6,4},{8,10},{10,8},{12,14},{14,12},{1,3},{3,1},... | collective-permute-start | bytes 196616 | tf_op jit(solution)/shard_map/ppermute | solution.py:66
  87.0 8.1 %collective-permute-start.11 = (bf16[2,256,128]{2,1,0:T(8,128)(2,1)S(1)}, bf16[2,256,128]{2,1,0:T(8,128)(2,1)S(1)}, u32[]{:S(2)}, u32[]{:S(2)}) collective-permute-start(bf16[2,256,128]{2,1,0:T(8,128)(2,1)S(1)} %maximum_select_fusion.2), channel_id=1, source_target_pairs={{0,12},{2,14},{4,0},{6,2},{8,4},{10,6},{12,8},{14,10},{1,13},{3,15... | collective-permute-start | bytes 393224 | tf_op jit(solution)/shard_map/ppermute | solution.py:70
  90.7 7.2 %collective-permute-start.12 = (bf16[2,256,128]{2,1,0:T(8,128)(2,1)S(1)}, bf16[2,256,128]{2,1,0:T(8,128)(2,1)S(1)}, u32[]{:S(2)}, u32[]{:S(2)}) collective-permute-start(bf16[2,256,128]{2,1,0:T(8,128)(2,1)S(1)} %maximum_select_fusion.2), channel_id=1, source_target_pairs={{0,8},{2,10},{4,12},{6,14},{8,0},{10,2},{12,4},{14,6},{1,9},{3,11}... | collective-permute-start | bytes 393224 | tf_op jit(solution)/shard_map/ppermute | solution.py:68
  93.0 7.9 %collective-permute-start.13 = (bf16[2,256,128]{2,1,0:T(8,128)(2,1)S(1)}, bf16[2,256,128]{2,1,0:T(8,128)(2,1)S(1)}, u32[]{:S(2)}, u32[]{:S(2)}) collective-permute-start(bf16[2,256,128]{2,1,0:T(8,128)(2,1)S(1)} %maximum_select_fusion.2), channel_id=1, source_target_pairs={{0,4},{2,6},{4,8},{6,10},{8,12},{10,14},{12,0},{14,2},{1,5},{3,7},... | collective-permute-start | bytes 393224 | tf_op jit(solution)/shard_map/ppermute | solution.py:69
  101.1 6.2 %collective-permute-start.14 = (bf16[8,256,128]{2,1,0:T(8,128)(2,1)S(1)}, bf16[8,256,128]{2,1,0:T(8,128)(2,1)S(1)}, u32[]{:S(2)}, u32[]{:S(2)}) collective-permute-start(bf16[8,256,128]{2,1,0:T(8,128)(2,1)S(1)} %bitcast.166), channel_id=1, source_target_pairs={{0,1},{1,0},{2,3},{3,2},{4,5},{5,4},{6,7},{7,6},{8,9},{9,8},{10,11... | collective-permute-start | bytes 1572872 | tf_op jit(solution)/shard_map/ppermute | solution.py:76
where the time goes:
time: 109 us; the launch traced here: 108 us
  starting transfers between devices  55.8 us (51%)
  waiting for transfers between devices  38.7 us (36%)
  matrix products  7.08 us (6%)
  local copies, waits for them, and re-layouts  4.28 us (4%)
  other arithmetic  1.26 us (1%)
  between operations  1.22 us (1%)
    ppermute x4, waiting for transfers between devices, neighbours(): got_p = lax.ppermute(last, axis, ring(count, 1))  30.5 us
    ppermute x4, starting transfers between devices, neighbours(): got_v = lax.ppermute(first, axis, ring(count, -1))  23.5 us
    ppermute x4, starting transfers between devices, neighbours(): got_p = lax.ppermute(last, axis, ring(count, 1))  10.1 us
    dot_general x18, matrix products, apply_block(): jnp.einsum('tzyxij,tzyxrj->tzyxri', blocks, vector, preferred_element_typ...  6.79 us
    ppermute x2, starting transfers between devices, neighbours(): both = lax.ppermute(jnp.stack([first, last]), axis, ring(2, 1))  6.32 us
    ppermute x1, starting transfers between devices, gather_pieces(): partner = lax.ppermute(absolute, 'gy', ring(2, 1))  4.7 us
    ppermute x1, starting transfers between devices, gather_pieces(): from_next = lax.ppermute(pair, 'gz', ring(nz, -2))  3.61 us
    unnamed x18, local copies, waits for them, and re-layouts  3.59 us
  transfers between devices with their start and end apart: 15, of which 7 were waited for; matrix products, arithmetic and copies ran while one was open for 8% of the time, Pallas kernels for 0%

commit v1 on v0

--- a/solution.py
+++ b/solution.py
@@ -58,26 +58,10 @@
 
 
 def gather_pieces(piece):
-    nz = lax.axis_size("gz")
-    ny = lax.axis_size("gy")
-    assert nz == 8 and ny == 2
-    g = lax.axis_index("gz")
-    c = lax.axis_index("gy")
-    other = lax.ppermute(piece, "gz", [(i, i ^ 1) for i in range(nz)])
-    pair = jnp.where(g % 2 == 1, jnp.stack([other, piece]), jnp.stack([piece, other]))
-    from_far = lax.ppermute(pair, "gz", ring(nz, 4))
-    from_prev = lax.ppermute(pair, "gz", ring(nz, 2))
-    from_next = lax.ppermute(pair, "gz", ring(nz, -2))
-    rel = jnp.stack([pair, from_next, from_far, from_prev])
-    pairs = nz // 2
-    doubled = jnp.concatenate([rel, rel], axis=0)
-    absolute = lax.dynamic_slice_in_dim(doubled, pairs - g // 2, pairs, axis=0)
-    absolute = absolute.reshape(nz, *piece.shape)
-    partner = lax.ppermute(absolute, "gy", ring(2, 1))
-    full = jnp.where(
-        c == 0, jnp.stack([absolute, partner], axis=1), jnp.stack([partner, absolute], axis=1)
-    )
-    return full.reshape(1, nz * ny, *piece.shape)
+    count = lax.axis_size("gz") * lax.axis_size("gy")
+    copies = jnp.broadcast_to(piece[None], (count, *piece.shape))
+    gathered = lax.all_to_all(copies, ("gz", "gy"), 0, 0, tiled=True)
+    return gathered.reshape(1, count, *piece.shape)
 
 
 def per_device_body(source_field, clover, forward, backward, restrict_blocks):

time: 109 us -> 106 us (0.972)
  starting transfers between devices: 55.8 us -> 45.5 us
  waiting for transfers between devices: 38.7 us -> 45.3 us
  local copies, waits for them, and re-layouts: 4.28 us -> 6.26 us
  other arithmetic: 1.26 us -> 0.1 us
    ppermute x5 -> x0, starting transfers between devices: 15.8 us -> none  [the longest x1 4.7 us: gather_pieces(): partner = lax.ppermute(absolute, 'gy', ring(2, 1))]
    all_to_all x0 -> x1, waiting for transfers between devices: none -> 14.8 us  [gather_pieces(): gathered = lax.all_to_all(copies, ('gz', 'gy'), 0, 0, tiled=True)]
    ppermute x5 -> x0, waiting for transfers between devices: 8.23 us -> none  [the longest x1 2.97 us: gather_pieces(): from_prev = lax.ppermute(pair, 'gz', ring(nz, 2))]
    all_to_all x0 -> x1, starting transfers between devices: none -> 5.59 us  [gather_pieces(): gathered = lax.all_to_all(copies, ('gz', 'gy'), 0, 0, tiled=True)]
    broadcast_in_dim x0 -> x1, local copies, waits for them, and re-layouts: none -> 1.17 us  [gather_pieces(): copies = jnp.broadcast_to(piece[None], (count, *piece.shape))]
    unnamed x18 -> x14, local copies, waits for them, and re-layouts: 3.59 us -> 4.46 us
  transfers between devices with their start and end apart: 15 -> 11, of which waited for: 7 -> 4; matrix products, arithmetic and copies ran while one was open for 8% -> 8% of each run, Pallas kernels for 0% -> 0%
where the time goes in v1:
time: 106 us; the launch traced here: 105 us
  starting transfers between devices  45.5 us (43%)
  waiting for transfers between devices  45.3 us (43%)
  matrix products  7.08 us (7%)
  local copies, waits for them, and re-layouts  6.26 us (6%)
  between operations  1.09 us (1%)
    ppermute x4, waiting for transfers between devices, neighbours(): got_p = lax.ppermute(last, axis, ring(count, 1))  30.5 us
    ppermute x4, starting transfers between devices, neighbours(): got_v = lax.ppermute(first, axis, ring(count, -1))  23.5 us
    all_to_all x1, waiting for transfers between devices, gather_pieces(): gathered = lax.all_to_all(copies, ('gz', 'gy'), 0, 0, tiled=True)  14.8 us
    ppermute x4, starting transfers between devices, neighbours(): got_p = lax.ppermute(last, axis, ring(count, 1))  10.1 us
    dot_general x18, matrix products, apply_block(): jnp.einsum('tzyxij,tzyxrj->tzyxri', blocks, vector, preferred_element_typ...  6.79 us
    ppermute x2, starting transfers between devices, neighbours(): both = lax.ppermute(jnp.stack([first, last]), axis, ring(2, 1))  6.32 us
    all_to_all x1, starting transfers between devices, gather_pieces(): gathered = lax.all_to_all(copies, ('gz', 'gy'), 0, 0, tiled=True)  5.59 us
    unnamed x14, local copies, waits for them, and re-layouts  4.46 us
  transfers between devices with their start and end apart: 11, of which 4 were waited for; matrix products, arithmetic and copies ran while one was open for 8% of the time, Pallas kernels for 0%

profile of v1, /device:TPU:1, one launch (start us, length us, event | category | flops | bytes accessed | tf_op | source)
XLA Modules:
  0.0 105.4 jit_solution(10053488846533295364)
XLA Ops:
  0.6 0.0 copy-start
  0.7 14.5 %collective-permute-start = (bf16[1,2,2,2,256,128]{5,4,3,2,1,0:T(8,128)(2,1)}, bf16[1,2,2,2,256,128]{5,4,3,2,1,0:T(8,128)(2,1)S(1)}, u32[]{:S(2)}, u32[]{:S(2)}) collective-permute-start(bf16[1,2,2,2,256,128]{5,4,3,2,1,0:T(8,128)(2,1)} %param.5), channel_id=1, source_target_pairs={{0,496},{16,0},{32,16},{48,32},{64,48},{80,64},{96,80},{112,96},{1... | collective-permute-start | bytes 1572872 | tf_op jit(solution)/shard_map/ppermute | solution.py:32
  15.2 1.1 %slice_bitcast_fusion.15 = (bf16[1,2,1,2,256,128]{5,4,3,1,2,0:T(8,128)(2,1)S(1)}, bf16[1,1,2,1,2,256,128]{6,5,4,2,3,1,0:T(8,128)(2,1)S(1)}) fusion(bf16[1,2,2,2,256,128]{5,4,3,2,1,0:T(8,128)(2,1)} %param.5), kind=kLoop, calls=%fused_computation.88 | loop fusion | bytes 1048576
  16.3 1.2 %fusion.3 = bf16[1,2,2,2,256,128]{5,4,3,2,1,0:T(8,128)(2,1)S(1)} fusion(bf16[1,2,2,2,256,128]{5,4,3,2,1,0:T(8,128)(2,1)S(1)} %copy-done.1, bf16[4,1,2,2,2,128,128]{6,5,4,3,2,1,0:T(8,128)(2,1)} %param.8), kind=kOutput, calls=%fused_computation.18 | convolution fusion | flops 67371008 | bytes 1310720 | tf_op jit(solution)/shard_map/tzyxij,tzyxrj->tzyxri/dot_general | solution.py:8
  17.6 0.0 copy-start.2
  17.6 0.1 pad_maximum_fusion
  17.6 3.0 %collective-permute-start.2 = (bf16[2,1,2,1,2,256,128]{6,5,4,2,3,1,0:T(8,128)(2,1)S(1)}, bf16[2,1,2,1,2,256,128]{6,5,4,2,3,1,0:T(8,128)(2,1)S(1)}, u32[]{:S(2)}, u32[]{:S(2)}) collective-permute-start(bf16[2,1,2,1,2,256,128]{6,5,4,2,3,1,0:T(8,128)(2,1)S(1)} %pad_maximum_fusion), channel_id=1, source_target_pairs={{0,1},{1,0},{2,3},{3,2},{4,5},{5,4},{6,7},{7,6},{8,9},{9,8},{10,11... | collective-permute-start | bytes 1572872 | tf_op jit(solution)/shard_map/ppermute | solution.py:29
  20.7 4.7 %collective-permute-start.1 = (bf16[1,1,2,2,256,128]{5,4,3,2,1,0:T(8,128)(2,1)S(1)}, bf16[1,1,2,2,256,128]{5,4,3,2,1,0:T(8,128)(2,1)S(1)}, u32[]{:S(2)}, u32[]{:S(2)}) collective-permute-start(bf16[1,1,2,2,256,128]{5,4,3,2,1,0:T(8,128)(2,1)S(1)} %get-tuple-element.29), channel_id=1, source_target_pairs={{0,14},{2,0},{4,2},{6,4},{8,6},{10,8},{12,10},{14,12},{1,15},{3,1}... | collective-permute-start | bytes 786440 | tf_op jit(solution)/shard_map/ppermute | solution.py:32
  25.4 0.3 fusion.5
  25.7 1.9 %collective-permute-start.4 = (bf16[1,1,2,2,256,128]{5,4,3,2,1,0:T(8,128)(2,1)S(1)}, bf16[1,1,2,2,256,128]{5,4,3,2,1,0:T(8,128)(2,1)S(1)}, u32[]{:S(2)}, u32[]{:S(2)}) collective-permute-start(bf16[1,1,2,2,256,128]{5,4,3,2,1,0:T(8,128)(2,1)S(1)} %get-tuple-element.38), channel_id=1, source_target_pairs={{0,2},{2,4},{4,6},{6,8},{8,10},{10,12},{12,14},{14,0},{1,3},{3,5},... | collective-permute-start | bytes 786440 | tf_op jit(solution)/shard_map/ppermute | solution.py:33
  27.7 0.3 fusion.4
  28.0 1.9 %collective-permute-start.3 = (bf16[1,2,2,2,256,128]{5,4,3,2,1,0:T(8,128)(2,1)S(1)}, bf16[1,2,2,2,256,128]{5,4,3,2,1,0:T(8,128)(2,1)S(1)}, u32[]{:S(2)}, u32[]{:S(2)}) collective-permute-start(bf16[1,2,2,2,256,128]{5,4,3,2,1,0:T(8,128)(2,1)S(1)} %fusion.4), channel_id=1, source_target_pairs={{0,16},{16,32},{32,48},{48,64},{64,80},{80,96},{96,112},{112,128},... | collective-permute-start | bytes 1572872 | tf_op jit(solution)/shard_map/ppermute | solution.py:33
  29.9 0.1 slice_bitcast_fusion.8
  30.0 0.3 fusion.23
  30.3 0.3 fusion.6
  30.6 0.0 copy-start.3
  30.6 0.1 fusion.57
  30.7 1.1 %copy-done.3 = bf16[4,1,2,2,2,128,128]{6,5,4,3,2,1,0:T(8,128)(2,1)S(1)} copy-done((bf16[4,1,2,2,2,128,128]{6,5,4,3,2,1,0:T(8,128)(2,1)S(1)}, bf16[4,1,2,2,2,128,128]{6,5,4,3,2,1,0:T(8,128)(2,1)}, u32[]{:S(2)}) %copy-start.3) | copy-done | bytes 1048600
  31.8 0.1 slice_bitcast_fusion.11
  32.0 0.3 convolution_add_fusion.6
  32.3 0.3 fusion.31
  32.6 0.3 fusion.2
  32.9 16.8 %collective-permute-done.4 = bf16[1,1,2,2,256,128]{5,4,3,2,1,0:T(8,128)(2,1)S(1)} collective-permute-done((bf16[1,1,2,2,256,128]{5,4,3,2,1,0:T(8,128)(2,1)S(1)}, bf16[1,1,2,2,256,128]{5,4,3,2,1,0:T(8,128)(2,1)S(1)}, u32[]{:S(2)}, u32[]{:S(2)}) %collective-permute-start.4) | collective-permute-done | bytes 262176 | tf_op jit(solution)/shard_map/ppermute | solution.py:33
  49.8 0.5 add_convert_fusion.1
  50.3 1.9 %collective-permute-start.5 = (bf16[1,2,2,2,256,128]{5,4,3,2,1,0:T(8,128)(2,1)S(1)}, bf16[1,2,2,2,256,128]{5,4,3,2,1,0:T(8,128)(2,1)S(1)}, u32[]{:S(2)}, u32[]{:S(2)}) collective-permute-start(bf16[1,2,2,2,256,128]{5,4,3,2,1,0:T(8,128)(2,1)S(1)} %add_convert_fusion.1), channel_id=1, source_target_pairs={{0,496},{16,0},{32,16},{48,32},{64,48},{80,64},{96,80},{112,96},{1... | collective-permute-start | bytes 1572872 | tf_op jit(solution)/shard_map/ppermute | solution.py:32
  52.3 2.4 %collective-permute-start.6 = (bf16[1,1,2,2,256,128]{5,4,3,2,1,0:T(8,128)(2,1)S(1)}, bf16[1,1,2,2,256,128]{5,4,3,2,1,0:T(8,128)(2,1)S(1)}, u32[]{:S(2)}, u32[]{:S(2)}) collective-permute-start(bf16[1,1,2,2,256,128]{5,4,3,2,1,0:T(8,128)(2,1)S(1)} %get-tuple-element.19), channel_id=1, source_target_pairs={{0,14},{2,0},{4,2},{6,4},{8,6},{10,8},{12,10},{14,12},{1,15},{3,1}... | collective-permute-start | bytes 786440 | tf_op jit(solution)/shard_map/ppermute | solution.py:32
  54.7 0.3 fusion.7
  55.1 0.1 pad_maximum_fusion.1
  55.2 3.3 %collective-permute-start.7 = (bf16[2,1,2,1,2,256,128]{6,5,4,2,3,1,0:T(8,128)(2,1)S(1)}, bf16[2,1,2,1,2,256,128]{6,5,4,2,3,1,0:T(8,128)(2,1)S(1)}, u32[]{:S(2)}, u32[]{:S(2)}) collective-permute-start(bf16[2,1,2,1,2,256,128]{6,5,4,2,3,1,0:T(8,128)(2,1)S(1)} %pad_maximum_fusion.1), channel_id=1, source_target_pairs={{0,1},{1,0},{2,3},{3,2},{4,5},{5,4},{6,7},{7,6},{8,9},{9,8},{10,11... | collective-permute-start | bytes 1572872 | tf_op jit(solution)/shard_map/ppermute | solution.py:29
  58.5 0.3 fusion.9
  58.8 2.6 %collective-permute-start.9 = (bf16[1,1,2,2,256,128]{5,4,3,1,2,0:T(8,128)(2,1)S(1)}, bf16[1,1,2,2,256,128]{5,4,3,1,2,0:T(8,128)(2,1)S(1)}, u32[]{:S(2)}, u32[]{:S(2)}) collective-permute-start(bf16[1,1,2,2,256,128]{5,4,3,1,2,0:T(8,128)(2,1)S(1)} %get-tuple-element.24), channel_id=1, source_target_pairs={{0,2},{2,4},{4,6},{6,8},{8,10},{10,12},{12,14},{14,0},{1,3},{3,5},... | collective-permute-start | bytes 786440 | tf_op jit(solution)/shard_map/ppermute | solution.py:33
  61.5 0.3 fusion.10
  61.8 0.3 fusion.8
  62.1 3.6 %collective-permute-start.8 = (bf16[1,2,2,2,256,128]{5,4,3,1,2,0:T(8,128)(2,1)S(1)}, bf16[1,2,2,2,256,128]{5,4,3,1,2,0:T(8,128)(2,1)S(1)}, u32[]{:S(2)}, u32[]{:S(2)}) collective-permute-start(bf16[1,2,2,2,256,128]{5,4,3,1,2,0:T(8,128)(2,1)S(1)} %fusion.8), channel_id=1, source_target_pairs={{0,16},{16,32},{32,48},{48,64},{64,80},{80,96},{96,112},{112,128},... | collective-permute-start | bytes 1572872 | tf_op jit(solution)/shard_map/ppermute | solution.py:33
  65.8 0.3 fusion.37
  66.1 0.3 convolution_add_fusion.3
  66.4 0.3 convolution_add_fusion.2
  66.8 0.3 convolution_add_fusion.1
  67.1 3.6 %collective-permute-done.9 = bf16[1,1,2,2,256,128]{5,4,3,1,2,0:T(8,128)(2,1)S(1)} collective-permute-done((bf16[1,1,2,2,256,128]{5,4,3,1,2,0:T(8,128)(2,1)S(1)}, bf16[1,1,2,2,256,128]{5,4,3,1,2,0:T(8,128)(2,1)S(1)}, u32[]{:S(2)}, u32[]{:S(2)}) %collective-permute-start.9) | collective-permute-done | bytes 262176 | tf_op jit(solution)/shard_map/ppermute | solution.py:33
  70.7 10.1 %collective-permute-done.8 = bf16[1,2,2,2,256,128]{5,4,3,1,2,0:T(8,128)(2,1)S(1)} collective-permute-done((bf16[1,2,2,2,256,128]{5,4,3,1,2,0:T(8,128)(2,1)S(1)}, bf16[1,2,2,2,256,128]{5,4,3,1,2,0:T(8,128)(2,1)S(1)}, u32[]{:S(2)}, u32[]{:S(2)}) %collective-permute-start.8) | collective-permute-done | bytes 524320 | tf_op jit(solution)/shard_map/ppermute | solution.py:33
  80.8 0.5 add_convert_fusion
  81.3 0.4 copy-done.4
  81.7 0.3 fusion.11
  82.0 1.2 %broadcast_in_dim.2 = bf16[16,256,128]{2,1,0:T(8,128)(2,1)} broadcast(bf16[256,128]{1,0:T(8,128)(2,1)S(1)} %fusion.11), dimensions={1,2} | broadcast | bytes 1114112 | tf_op jit(solution)/shard_map/broadcast_in_dim | solution.py:62
  83.2 5.6 %all-to-all-start = ((bf16[16,256,128]{2,1,0:T(8,128)(2,1)}), bf16[16,256,128]{2,1,0:T(8,128)(2,1)S(1)}, u32[]{:S(2)}, u32[]{:S(2)}) async-start(bf16[16,256,128]{2,1,0:T(8,128)(2,1)} %broadcast_in_dim.2), calls=%async_computation | async-start | bytes 2097152 | tf_op jit(solution)/shard_map/all_to_all | solution.py:63
  88.8 0.8 copy.24
  89.6 14.8 %all-to-all-done = bf16[16,256,128]{2,1,0:T(8,128)(2,1)S(1)} async-done(((bf16[16,256,128]{2,1,0:T(8,128)(2,1)}), bf16[16,256,128]{2,1,0:T(8,128)(2,1)S(1)}, u32[]{:S(2)}, u32[]{:S(2)}) %all-to-all-start) | async-done | bytes 1048608 | tf_op jit(solution)/shard_map/all_to_all | solution.py:63
  104.4 1.0 copy.95
  (23 shorter events, 0.4 us)
Async XLA Ops:
  0.6 29.4 %copy-start = (bf16[1,2,2,2,128,128]{5,4,3,2,1,0:T(8,128)(2,1)S(1)}, bf16[1,2,2,2,128,128]{5,4,3,2,1,0:T(8,128)(2,1)}, u32[]{:S(2)}) copy-start(bf16[1,2,2,2,128,128]{5,4,3,2,1,0:T(8,128)(2,1)} %param.6) | copy-start | bytes 786436
  0.6 15.6 %copy-start.1 = (bf16[1,2,2,2,256,128]{5,4,3,2,1,0:T(8,128)(2,1)S(1)}, bf16[1,2,2,2,256,128]{5,4,3,2,1,0:T(8,128)(2,1)}, u32[]{:S(2)}) copy-start(bf16[1,2,2,2,256,128]{5,4,3,2,1,0:T(8,128)(2,1)} %param.5) | copy-start | bytes 1572868
  0.7 31.3 %collective-permute-start = (bf16[1,2,2,2,256,128]{5,4,3,2,1,0:T(8,128)(2,1)}, bf16[1,2,2,2,256,128]{5,4,3,2,1,0:T(8,128)(2,1)S(1)}, u32[]{:S(2)}, u32[]{:S(2)}) collective-permute-start(bf16[1,2,2,2,256,128]{5,4,3,2,1,0:T(8,128)(2,1)} %param.5), channel_id=1, source_target_pairs={{0,496},{16,0},{32,16},{48,32},{64,48},{80,64},{96,80},{112,96},{1... | collective-permute-start | bytes 1572872 | tf_op jit(solution)/shard_map/ppermute | solution.py:32
  17.6 7.8 %copy-start.2 = (bf16[4,1,2,2,2,128,128]{6,5,4,3,2,1,0:T(8,128)(2,1)S(1)}, bf16[4,1,2,2,2,128,128]{6,5,4,3,2,1,0:T(8,128)(2,1)}, u32[]{:S(2)}) copy-start(bf16[4,1,2,2,2,128,128]{6,5,4,3,2,1,0:T(8,128)(2,1)} %param.8) | copy-start | bytes 3145732
  17.6 14.6 %collective-permute-start.2 = (bf16[2,1,2,1,2,256,128]{6,5,4,2,3,1,0:T(8,128)(2,1)S(1)}, bf16[2,1,2,1,2,256,128]{6,5,4,2,3,1,0:T(8,128)(2,1)S(1)}, u32[]{:S(2)}, u32[]{:S(2)}) collective-permute-start(bf16[2,1,2,1,2,256,128]{6,5,4,2,3,1,0:T(8,128)(2,1)S(1)} %pad_maximum_fusion), channel_id=1, source_target_pairs={{0,1},{1,0},{2,3},{3,2},{4,5},{5,4},{6,7},{7,6},{8,9},{9,8},{10,11... | collective-permute-start | bytes 1572872 | tf_op jit(solution)/shard_map/ppermute | solution.py:29
  20.7 11.9 %collective-permute-start.1 = (bf16[1,1,2,2,256,128]{5,4,3,2,1,0:T(8,128)(2,1)S(1)}, bf16[1,1,2,2,256,128]{5,4,3,2,1,0:T(8,128)(2,1)S(1)}, u32[]{:S(2)}, u32[]{:S(2)}) collective-permute-start(bf16[1,1,2,2,256,128]{5,4,3,2,1,0:T(8,128)(2,1)S(1)} %get-tuple-element.29), channel_id=1, source_target_pairs={{0,14},{2,0},{4,2},{6,4},{8,6},{10,8},{12,10},{14,12},{1,15},{3,1}... | collective-permute-start | bytes 786440 | tf_op jit(solution)/shard_map/ppermute | solution.py:32
  25.7 24.0 %collective-permute-start.4 = (bf16[1,1,2,2,256,128]{5,4,3,2,1,0:T(8,128)(2,1)S(1)}, bf16[1,1,2,2,256,128]{5,4,3,2,1,0:T(8,128)(2,1)S(1)}, u32[]{:S(2)}, u32[]{:S(2)}) collective-permute-start(bf16[1,1,2,2,256,128]{5,4,3,2,1,0:T(8,128)(2,1)S(1)} %get-tuple-element.38), channel_id=1, source_target_pairs={{0,2},{2,4},{4,6},{6,8},{8,10},{10,12},{12,14},{14,0},{1,3},{3,5},... | collective-permute-start | bytes 786440 | tf_op jit(solution)/shard_map/ppermute | solution.py:33
  28.0 21.8 %collective-permute-start.3 = (bf16[1,2,2,2,256,128]{5,4,3,2,1,0:T(8,128)(2,1)S(1)}, bf16[1,2,2,2,256,128]{5,4,3,2,1,0:T(8,128)(2,1)S(1)}, u32[]{:S(2)}, u32[]{:S(2)}) collective-permute-start(bf16[1,2,2,2,256,128]{5,4,3,2,1,0:T(8,128)(2,1)S(1)} %fusion.4), channel_id=1, source_target_pairs={{0,16},{16,32},{32,48},{48,64},{64,80},{80,96},{96,112},{112,128},... | collective-permute-start | bytes 1572872 | tf_op jit(solution)/shard_map/ppermute | solution.py:33
  30.6 1.2 %copy-start.3 = (bf16[4,1,2,2,2,128,128]{6,5,4,3,2,1,0:T(8,128)(2,1)S(1)}, bf16[4,1,2,2,2,128,128]{6,5,4,3,2,1,0:T(8,128)(2,1)}, u32[]{:S(2)}) copy-start(bf16[4,1,2,2,2,128,128]{6,5,4,3,2,1,0:T(8,128)(2,1)} %param.7) | copy-start | bytes 3145732
  50.3 15.8 %collective-permute-start.5 = (bf16[1,2,2,2,256,128]{5,4,3,2,1,0:T(8,128)(2,1)S(1)}, bf16[1,2,2,2,256,128]{5,4,3,2,1,0:T(8,128)(2,1)S(1)}, u32[]{:S(2)}, u32[]{:S(2)}) collective-permute-start(bf16[1,2,2,2,256,128]{5,4,3,2,1,0:T(8,128)(2,1)S(1)} %add_convert_fusion.1), channel_id=1, source_target_pairs={{0,496},{16,0},{32,16},{48,32},{64,48},{80,64},{96,80},{112,96},{1... | collective-permute-start | bytes 1572872 | tf_op jit(solution)/shard_map/ppermute | solution.py:32
  52.3 14.1 %collective-permute-start.6 = (bf16[1,1,2,2,256,128]{5,4,3,2,1,0:T(8,128)(2,1)S(1)}, bf16[1,1,2,2,256,128]{5,4,3,2,1,0:T(8,128)(2,1)S(1)}, u32[]{:S(2)}, u32[]{:S(2)}) collective-permute-start(bf16[1,1,2,2,256,128]{5,4,3,2,1,0:T(8,128)(2,1)S(1)} %get-tuple-element.19), channel_id=1, source_target_pairs={{0,14},{2,0},{4,2},{6,4},{8,6},{10,8},{12,10},{14,12},{1,15},{3,1}... | collective-permute-start | bytes 786440 | tf_op jit(solution)/shard_map/ppermute | solution.py:32
  55.2 11.6 %collective-permute-start.7 = (bf16[2,1,2,1,2,256,128]{6,5,4,2,3,1,0:T(8,128)(2,1)S(1)}, bf16[2,1,2,1,2,256,128]{6,5,4,2,3,1,0:T(8,128)(2,1)S(1)}, u32[]{:S(2)}, u32[]{:S(2)}) collective-permute-start(bf16[2,1,2,1,2,256,128]{6,5,4,2,3,1,0:T(8,128)(2,1)S(1)} %pad_maximum_fusion.1), channel_id=1, source_target_pairs={{0,1},{1,0},{2,3},{3,2},{4,5},{5,4},{6,7},{7,6},{8,9},{9,8},{10,11... | collective-permute-start | bytes 1572872 | tf_op jit(solution)/shard_map/ppermute | solution.py:29
  58.8 11.9 %collective-permute-start.9 = (bf16[1,1,2,2,256,128]{5,4,3,1,2,0:T(8,128)(2,1)S(1)}, bf16[1,1,2,2,256,128]{5,4,3,1,2,0:T(8,128)(2,1)S(1)}, u32[]{:S(2)}, u32[]{:S(2)}) collective-permute-start(bf16[1,1,2,2,256,128]{5,4,3,1,2,0:T(8,128)(2,1)S(1)} %get-tuple-element.24), channel_id=1, source_target_pairs={{0,2},{2,4},{4,6},{6,8},{8,10},{10,12},{12,14},{14,0},{1,3},{3,5},... | collective-permute-start | bytes 786440 | tf_op jit(solution)/shard_map/ppermute | solution.py:33
  62.1 18.7 %collective-permute-start.8 = (bf16[1,2,2,2,256,128]{5,4,3,1,2,0:T(8,128)(2,1)S(1)}, bf16[1,2,2,2,256,128]{5,4,3,1,2,0:T(8,128)(2,1)S(1)}, u32[]{:S(2)}, u32[]{:S(2)}) collective-permute-start(bf16[1,2,2,2,256,128]{5,4,3,1,2,0:T(8,128)(2,1)S(1)} %fusion.8), channel_id=1, source_target_pairs={{0,16},{16,32},{32,48},{48,64},{64,80},{80,96},{96,112},{112,128},... | collective-permute-start | bytes 1572872 | tf_op jit(solution)/shard_map/ppermute | solution.py:33
  80.8 1.0 copy-start.4
  83.2 21.3 %all-to-all-start = ((bf16[16,256,128]{2,1,0:T(8,128)(2,1)}), bf16[16,256,128]{2,1,0:T(8,128)(2,1)S(1)}, u32[]{:S(2)}, u32[]{:S(2)}) async-start(bf16[16,256,128]{2,1,0:T(8,128)(2,1)} %broadcast_in_dim.2), calls=%async_computation | async-start | bytes 2097152 | tf_op jit(solution)/shard_map/all_to_all | solution.py:63

commit v2 on v1

--- a/solution.py
+++ b/solution.py
@@ -20,23 +20,68 @@
     return lax.slice_in_dim(block, start, stop, axis=dim)
 
 
+def send(block, axis, perm):
+    return lax.ppermute(block, axis, perm)
+
+
 def neighbours(vector, pulled, dim, axis):
     count = lax.axis_size(axis)
     size = vector.shape[dim]
     first = take(vector, dim, 0, 1)
     last = take(pulled, dim, size - 1, size)
     if count == 2:
-        both = lax.ppermute(jnp.stack([first, last]), axis, ring(2, 1))
+        both = send(jnp.stack([first, last]), axis, ring(2, 1))
         got_v, got_p = both[0], both[1]
     else:
-        got_v = lax.ppermute(first, axis, ring(count, -1))
-        got_p = lax.ppermute(last, axis, ring(count, 1))
+        got_v = send(first, axis, ring(count, -1))
+        got_p = send(last, axis, ring(count, 1))
     ahead = jnp.concatenate([take(vector, dim, 1, size), got_v], axis=dim)
     behind = jnp.concatenate([got_p, take(pulled, dim, 0, size - 1)], axis=dim)
     return ahead, behind
 
 
 AXES = ((0, "ta"), (1, "gz"), (2, "gy"))
+ALL = ("ta", "gz", "gy")
+
+
+def relay_routes(nt, nz, ny):
+    half = nt // 2
+
+    def lin(t, g, c):
+        return (t * nz + g) * ny + c
+
+    first, second = [], []
+    for y in range(nz // 2):
+        for c in range(ny):
+            for src, mid, dst in (
+                ((nt - 1, 0), (half - 1, 1), (0, 0)),
+                ((nt - 1, 1), (nt - 1, 0), (0, 1)),
+                ((half, 0), (0, 1), (half - 1, 0)),
+                ((half, 1), (half, 0), (half - 1, 1)),
+            ):
+                a, b, d = (lin(t, 2 * y + x, c) for t, x in (src, mid, dst))
+                first.append((a, b))
+                second.append((b, d))
+    return first, second
+
+
+def time_neighbours(vector, pulled):
+    nt, nz, ny = (lax.axis_size(a) for a in ALL)
+    size = vector.shape[0]
+    first = take(vector, 0, 0, 1)
+    last = take(pulled, 0, size - 1, size)
+    half = nt // 2
+    t = lax.axis_index("ta")
+    got_v = send(first, "ta", [(i, (i - 1) % nt) for i in range(nt) if i != half])
+    got_p = send(last, "ta", [(i, (i + 1) % nt) for i in range(nt) if i != nt - 1])
+    hop_1, hop_2 = relay_routes(nt, nz, ny)
+    moving = jnp.where(t == nt - 1, last, first)
+    moved = send(send(moving, ALL, hop_1), ALL, hop_2)
+    got_p = jnp.where(t == 0, moved, got_p)
+    got_v = jnp.where(t == half - 1, moved, got_v)
+    ahead = jnp.concatenate([take(vector, 0, 1, size), got_v], axis=0)
+    behind = jnp.concatenate([got_p, take(pulled, 0, 0, size - 1)], axis=0)
+    return ahead, behind
 
 
 def operate(vector, clover, forward, backward):
@@ -44,7 +89,10 @@
     terms = []
     pulls = []
     for m, axis in AXES:
-        ahead, behind = neighbours(vector, pulled[m], m, axis)
+        if axis == "ta":
+            ahead, behind = time_neighbours(vector, pulled[m])
+        else:
+            ahead, behind = neighbours(vector, pulled[m], m, axis)
         terms.append(apply_block(forward[m], ahead))
         pulls.append(behind)
     terms.append(apply_block(forward[3], jnp.roll(vector, -1, axis=3)))

time: 106 us -> 129 us (1.22)
  starting transfers between devices: 45.5 us -> 54.7 us
  local copies, waits for them, and re-layouts: 6.26 us -> 15.2 us
  other arithmetic: 0.1 us -> 3.2 us
    ppermute x10 -> x14, starting transfers between devices: 39.9 us -> 50.7 us  [send(): return lax.ppermute(block, axis, perm)]
    another operation x4 -> x5, local copies, waits for them, and re-layouts: 0.26 us -> 4.03 us
    slice x4 -> x6, local copies, waits for them, and re-layouts: 0.15 us -> 2.86 us  [take(): return lax.slice_in_dim(block, start, stop, axis=dim)]
    another operation x2 -> x3, other arithmetic: 0.1 us -> 2.2 us  [neighbours(): both = lax.ppermute(jnp.stack([first, last]), axis, ring(2, 1))]
    all_to_all x1, starting transfers between devices: 5.59 us -> 3.94 us  [gather_pieces(): gathered = lax.all_to_all(copies, ('gz', 'gy'), 0, 0, tiled=True)]
    unnamed x14 -> x40, local copies, waits for them, and re-layouts: 4.46 us -> 4.98 us
    ppermute x10 -> x14, waiting for transfers between devices: 30.5 us -> 30.9 us  [send(): return lax.ppermute(block, axis, perm)]
  transfers between devices with their start and end apart: 11 -> 15, of which waited for: 4 -> 6; matrix products, arithmetic and copies ran while one was open for 8% -> 12% of each run, Pallas kernels for 0% -> 0%
where the time goes in v2:
time: 129 us; the launch traced here: 128 us
  starting transfers between devices  54.7 us (42%)
  waiting for transfers between devices  45.8 us (36%)
  local copies, waits for them, and re-layouts  15.2 us (12%)
  matrix products  8.05 us (6%)
  other arithmetic  3.2 us (2%)
    ppermute x14, starting transfers between devices, send(): return lax.ppermute(block, axis, perm)  50.7 us
    ppermute x14, waiting for transfers between devices, send(): return lax.ppermute(block, axis, perm)  30.9 us
    all_to_all x1, waiting for transfers between devices, gather_pieces(): gathered = lax.all_to_all(copies, ('gz', 'gy'), 0, 0, tiled=True)  14.9 us
    dot_general x18, matrix products, apply_block(): jnp.einsum('tzyxij,tzyxrj->tzyxri', blocks, vector, preferred_element_typ...  7.76 us
    unnamed x40, local copies, waits for them, and re-layouts  4.98 us
    all_to_all x1, starting transfers between devices, gather_pieces(): gathered = lax.all_to_all(copies, ('gz', 'gy'), 0, 0, tiled=True)  3.94 us
    another operation x2, local copies, waits for them, and re-layouts  3.23 us
    slice x6, local copies, waits for them, and re-layouts, take(): return lax.slice_in_dim(block, start, stop, axis=dim)  2.86 us
  transfers between devices with their start and end apart: 15, of which 6 were waited for; matrix products, arithmetic and copies ran while one was open for 12% of the time, Pallas kernels for 0%

profile of v2, /device:TPU:1, one launch (start us, length us, event | category | flops | bytes accessed | tf_op | source)
XLA Modules:
  0.0 128.1 jit_solution(16513516919841036197)
XLA Ops:
  0.7 2.2 %slice_bitcast_fusion.8 = (bf16[2,2,2,128,128]{4,3,2,1,0:T(8,128)(2,1)}, bf16[2,2,2,128,128]{4,3,2,1,0:T(8,128)(2,1)}, bf16[2,2,2,128,128]{4,3,2,1,0:T(8,128)(2,1)S(1)}, bf16[2,2,2,128,128]{4,3,2,1,0:T(8,128)(2,1)}) fusion(bf16[4,1,2,2,2,128,128]{6,5,4,3,2,1,0:T(8,128)(2,1)} %param.8), kind=kLoop, calls=%fused_computation.85 | loop fusion | bytes 2097152 | tf_op jit(solution)/shard_map/reshape.28
  2.8 1.1 fusion.3
  3.9 5.2 %collective-permute-start.5 = (bf16[1,2,2,2,256,128]{5,4,3,1,2,0:T(8,128)(2,1)}, bf16[1,2,2,2,256,128]{5,4,3,1,2,0:T(8,128)(2,1)}, u32[]{:S(2)}, u32[]{:S(2)}) collective-permute-start(bf16[1,2,2,2,256,128]{5,4,3,1,2,0:T(8,128)(2,1)} %fusion.3), channel_id=1, source_target_pairs={{0,16},{16,32},{32,48},{48,64},{64,80},{80,96},{96,112},{112,128},... | collective-permute-start | bytes 1572872 | tf_op jit(solution)/shard_map/ppermute | solution.py:24
  9.1 0.9 fusion.71
  10.0 11.7 %collective-permute-start.2 = (bf16[1,2,2,2,256,128]{5,4,3,1,2,0:T(8,128)(2,1)}, bf16[1,2,2,2,256,128]{5,4,3,1,2,0:T(8,128)(2,1)}, u32[]{:S(2)}, u32[]{:S(2)}) collective-permute-start(bf16[1,2,2,2,256,128]{5,4,3,1,2,0:T(8,128)(2,1)} %get-tuple-element.38), channel_id=1, source_target_pairs={{0,496},{16,0},{32,16},{48,32},{64,48},{80,64},{96,80},{112,96},{1... | collective-permute-start | bytes 1572872 | tf_op jit(solution)/shard_map/ppermute | solution.py:24
  21.7 1.5 %collective-permute-start = (bf16[1,2,2,2,256,128]{5,4,3,1,2,0:T(8,128)(2,1)S(1)}, bf16[1,2,2,2,256,128]{5,4,3,1,2,0:T(8,128)(2,1)}, u32[]{:S(2)}, u32[]{:S(2)}) collective-permute-start(bf16[1,2,2,2,256,128]{5,4,3,1,2,0:T(8,128)(2,1)S(1)} %get-tuple-element.39), channel_id=1, source_target_pairs={{496,242},{498,496},{256,2},{258,256},{497,243},{499,497},{257,3},... | collective-permute-start | bytes 1572872 | tf_op jit(solution)/shard_map/ppermute | solution.py:24
  23.2 1.1 fusion.69
  24.5 0.7 slice_bitcast_fusion.6
  25.3 0.8 pad_maximum_fusion
  26.1 2.9 %collective-permute-start.4 = (bf16[2,1,2,1,2,256,128]{6,5,4,2,3,1,0:T(8,128)(2,1)}, bf16[2,1,2,1,2,256,128]{6,5,4,2,3,1,0:T(8,128)(2,1)}, u32[]{:S(2)}, u32[]{:S(2)}) collective-permute-start(bf16[2,1,2,1,2,256,128]{6,5,4,2,3,1,0:T(8,128)(2,1)} %pad_maximum_fusion), channel_id=1, source_target_pairs={{0,1},{1,0},{2,3},{3,2},{4,5},{5,4},{6,7},{7,6},{8,9},{9,8},{10,11... | collective-permute-start | bytes 1572872 | tf_op jit(solution)/shard_map/ppermute | solution.py:24
  29.0 0.8 fusion.68
  29.8 4.5 %collective-permute-start.3 = (bf16[1,1,2,2,256,128]{5,4,3,2,1,0:T(8,128)(2,1)}, bf16[1,1,2,2,256,128]{5,4,3,2,1,0:T(8,128)(2,1)}, u32[]{:S(2)}, u32[]{:S(2)}) collective-permute-start(bf16[1,1,2,2,256,128]{5,4,3,2,1,0:T(8,128)(2,1)} %get-tuple-element.29), channel_id=1, source_target_pairs={{0,14},{2,0},{4,2},{6,4},{8,6},{10,8},{12,10},{14,12},{1,15},{3,1}... | collective-permute-start | bytes 786440 | tf_op jit(solution)/shard_map/ppermute | solution.py:24
  34.6 1.0 fusion.67
  35.6 0.6 copy-done.3
  36.2 1.1 slice_bitcast_fusion.10
  37.9 1.3 %collective-permute-start.1 = (bf16[1,2,2,2,256,128]{5,4,3,1,2,0:T(8,128)(2,1)}, bf16[1,2,2,2,256,128]{5,4,3,1,2,0:T(8,128)(2,1)}, u32[]{:S(2)}, u32[]{:S(2)}) collective-permute-start(bf16[1,2,2,2,256,128]{5,4,3,1,2,0:T(8,128)(2,1)} %collective-permute-done), channel_id=1, source_target_pairs={{242,0},{496,2},{2,240},{256,242},{243,1},{497,3},{3,241},{257,243... | collective-permute-start | bytes 1572872 | tf_op jit(solution)/shard_map/ppermute | solution.py:24
  39.2 0.9 fusion.72
  40.1 4.2 %collective-permute-start.6 = (bf16[1,1,2,2,256,128]{5,4,3,2,1,0:T(8,128)(2,1)}, bf16[1,1,2,2,256,128]{5,4,3,2,1,0:T(8,128)(2,1)S(1)}, u32[]{:S(2)}, u32[]{:S(2)}) collective-permute-start(bf16[1,1,2,2,256,128]{5,4,3,2,1,0:T(8,128)(2,1)} %get-tuple-element.42), channel_id=1, source_target_pairs={{0,2},{2,4},{4,6},{6,8},{8,10},{10,12},{12,14},{14,0},{1,3},{3,5},... | collective-permute-start | bytes 786440 | tf_op jit(solution)/shard_map/ppermute | solution.py:24
  44.3 1.1 slice_bitcast_fusion.5
  45.7 9.7 %collective-permute-done.1 = bf16[1,2,2,2,256,128]{5,4,3,1,2,0:T(8,128)(2,1)} collective-permute-done((bf16[1,2,2,2,256,128]{5,4,3,1,2,0:T(8,128)(2,1)}, bf16[1,2,2,2,256,128]{5,4,3,1,2,0:T(8,128)(2,1)}, u32[]{:S(2)}, u32[]{:S(2)}) %collective-permute-start.1) | collective-permute-done | bytes 524320 | tf_op jit(solution)/shard_map/ppermute | solution.py:24
  55.4 1.3 %select_bitcast_fusion = (bf16[2,2,2,256,128]{4,3,2,0,1:T(8,128)(2,1)S(1)}, f32[1,2,2,2,256,128]{5,4,3,1,2,0:T(8,128)S(1)}) fusion(bf16[1,2,2,2,256,128]{5,4,3,1,2,0:T(8,128)(2,1)} %collective-permute-done.1, bf16[1,2,2,2,256,128]{5,4,3,1,2,0:T(8,128)(2,1)} %collective-permute-done.2, pred[]{:T(512)S(6)} %eq.12, ...), kind=kLoop, calls=%fused_computation.58 | loop fusion | flops 786432 | bytes 3145730 | tf_op jit(solution)/shard_map/reshape.9
  57.1 0.6 copy-done.10
  57.7 1.4 %fusion.2 = f32[2,2,2,256,128]{4,3,2,1,0:T(8,128)S(1)} fusion(f32[2,2,2,256,128]{4,3,2,1,0:T(8,128)S(1)} %fusion.27, f32[2,2,2,256,128]{4,3,2,1,0:T(8,128)S(1)} %convolution_add_fusion.6, bf16[1,1,2,2,256,128]{5,4,3,2,1,0:T(8,128)(2,1)} %collective-permute-done.3, bf16[1,1,2,2,256,128]{5,4,3,2,1,0:T(8,128)(2,1)S(1)} %copy-done.10, ...), kind=kOutput, calls=%fused_computation.8 | convolution fusion | flops 67895296 | bytes 3932160 | tf_op jit(solution)/shard_map/tzyxij,tzyxrj->tzyxri/dot_general | solution.py:8
  59.1 2.7 %collective-permute-done.6 = bf16[1,1,2,2,256,128]{5,4,3,2,1,0:T(8,128)(2,1)S(1)} collective-permute-done((bf16[1,1,2,2,256,128]{5,4,3,2,1,0:T(8,128)(2,1)}, bf16[1,1,2,2,256,128]{5,4,3,2,1,0:T(8,128)(2,1)S(1)}, u32[]{:S(2)}, u32[]{:S(2)}) %collective-permute-start.6) | collective-permute-done | bytes 262176 | tf_op jit(solution)/shard_map/ppermute | solution.py:24
  61.8 0.5 fusion.15
  62.4 0.3 fusion.7
  62.9 1.5 %collective-permute-start.12 = (bf16[1,2,2,2,256,128]{5,4,3,1,2,0:T(8,128)(2,1)S(1)}, bf16[1,2,2,2,256,128]{5,4,3,1,2,0:T(8,128)(2,1)S(1)}, u32[]{:S(2)}, u32[]{:S(2)}) collective-permute-start(bf16[1,2,2,2,256,128]{5,4,3,1,2,0:T(8,128)(2,1)S(1)} %fusion.7), channel_id=1, source_target_pairs={{0,16},{16,32},{32,48},{48,64},{64,80},{80,96},{96,112},{112,128},... | collective-permute-start | bytes 1572872 | tf_op jit(solution)/shard_map/ppermute | solution.py:24
  64.4 0.7 collective-permute-start.7
  65.1 5.0 %collective-permute-start.9 = (bf16[1,2,2,2,256,128]{5,4,3,1,2,0:T(8,128)(2,1)S(1)}, bf16[1,2,2,2,256,128]{5,4,3,1,2,0:T(8,128)(2,1)S(1)}, u32[]{:S(2)}, u32[]{:S(2)}) collective-permute-start(bf16[1,2,2,2,256,128]{5,4,3,1,2,0:T(8,128)(2,1)S(1)} %get-tuple-element.18), channel_id=1, source_target_pairs={{0,496},{16,0},{32,16},{48,32},{64,48},{80,64},{96,80},{112,96},{1... | collective-permute-start | bytes 1572872 | tf_op jit(solution)/shard_map/ppermute | solution.py:24
  70.1 0.3 fusion.8
  70.5 2.9 %collective-permute-start.11 = (bf16[2,1,2,1,2,256,128]{6,5,4,2,3,1,0:T(8,128)(2,1)S(1)}, bf16[2,1,2,1,2,256,128]{6,5,4,2,3,1,0:T(8,128)(2,1)S(1)}, u32[]{:S(2)}, u32[]{:S(2)}) collective-permute-start(bf16[2,1,2,1,2,256,128]{6,5,4,2,3,1,0:T(8,128)(2,1)S(1)} %pad_maximum_fusion.1), channel_id=1, source_target_pairs={{0,1},{1,0},{2,3},{3,2},{4,5},{5,4},{6,7},{7,6},{8,9},{9,8},{10,11... | collective-permute-start | bytes 1572872 | tf_op jit(solution)/shard_map/ppermute | solution.py:24
  73.4 0.3 fusion.10
  73.8 0.9 copy-done.4
  75.0 1.3 %collective-permute-start.8 = (bf16[1,2,2,2,256,128]{5,4,3,1,2,0:T(8,128)(2,1)S(1)}, bf16[1,2,2,2,256,128]{5,4,3,1,2,0:T(8,128)(2,1)S(1)}, u32[]{:S(2)}, u32[]{:S(2)}) collective-permute-start(bf16[1,2,2,2,256,128]{5,4,3,1,2,0:T(8,128)(2,1)S(1)} %collective-permute-done.7), channel_id=1, source_target_pairs={{242,0},{496,2},{2,240},{256,242},{243,1},{497,3},{3,241},{257,243... | collective-permute-start | bytes 1572872 | tf_op jit(solution)/shard_map/ppermute | solution.py:24
  76.4 6.2 %collective-permute-start.10 = (bf16[1,1,2,2,256,128]{5,4,3,2,1,0:T(8,128)(2,1)S(1)}, bf16[1,1,2,2,256,128]{5,4,3,2,1,0:T(8,128)(2,1)S(1)}, u32[]{:S(2)}, u32[]{:S(2)}) collective-permute-start(bf16[1,1,2,2,256,128]{5,4,3,2,1,0:T(8,128)(2,1)S(1)} %get-tuple-element.17), channel_id=1, source_target_pairs={{0,14},{2,0},{4,2},{6,4},{8,6},{10,8},{12,10},{14,12},{1,15},{3,1}... | collective-permute-start | bytes 786440 | tf_op jit(solution)/shard_map/ppermute | solution.py:24
  82.9 2.1 %collective-permute-start.13 = (bf16[1,1,2,2,256,128]{5,4,3,1,2,0:T(8,128)(2,1)S(1)}, bf16[1,1,2,2,256,128]{5,4,3,1,2,0:T(8,128)(2,1)S(1)}, u32[]{:S(2)}, u32[]{:S(2)}) collective-permute-start(bf16[1,1,2,2,256,128]{5,4,3,1,2,0:T(8,128)(2,1)S(1)} %get-tuple-element.24), channel_id=1, source_target_pairs={{0,2},{2,4},{4,6},{6,8},{8,10},{10,12},{12,14},{14,0},{1,3},{3,5},... | collective-permute-start | bytes 786440 | tf_op jit(solution)/shard_map/ppermute | solution.py:24
  85.0 7.3 %collective-permute-done.8 = bf16[1,2,2,2,256,128]{5,4,3,1,2,0:T(8,128)(2,1)S(1)} collective-permute-done((bf16[1,2,2,2,256,128]{5,4,3,1,2,0:T(8,128)(2,1)S(1)}, bf16[1,2,2,2,256,128]{5,4,3,1,2,0:T(8,128)(2,1)S(1)}, u32[]{:S(2)}, u32[]{:S(2)}) %collective-permute-start.8) | collective-permute-done | bytes 524320 | tf_op jit(solution)/shard_map/ppermute | solution.py:24
  92.6 6.7 %collective-permute-done.10 = bf16[1,1,2,2,256,128]{5,4,3,2,1,0:T(8,128)(2,1)S(1)} collective-permute-done((bf16[1,1,2,2,256,128]{5,4,3,2,1,0:T(8,128)(2,1)S(1)}, bf16[1,1,2,2,256,128]{5,4,3,2,1,0:T(8,128)(2,1)S(1)}, u32[]{:S(2)}, u32[]{:S(2)}) %collective-permute-start.10) | collective-permute-done | bytes 262176 | tf_op jit(solution)/shard_map/ppermute | solution.py:24
  99.2 0.3 convolution_add_fusion.2
  99.5 0.6 copy-done.8
  100.5 4.5 %collective-permute-done.13 = bf16[1,1,2,2,256,128]{5,4,3,1,2,0:T(8,128)(2,1)S(1)} collective-permute-done((bf16[1,1,2,2,256,128]{5,4,3,1,2,0:T(8,128)(2,1)S(1)}, bf16[1,1,2,2,256,128]{5,4,3,1,2,0:T(8,128)(2,1)S(1)}, u32[]{:S(2)}, u32[]{:S(2)}) %collective-permute-start.13) | collective-permute-done | bytes 262176 | tf_op jit(solution)/shard_map/ppermute | solution.py:24
  105.0 0.6 add_convert_fusion
  105.6 0.4 copy-done.18
  106.3 1.2 broadcast_in_dim.2
  107.5 3.9 %all-to-all-start = ((bf16[16,256,128]{2,1,0:T(8,128)(2,1)}), bf16[16,256,128]{2,1,0:T(8,128)(2,1)S(1)}, u32[]{:S(2)}, u32[]{:S(2)}) async-start(bf16[16,256,128]{2,1,0:T(8,128)(2,1)} %broadcast_in_dim.2), calls=%async_computation | async-start | bytes 2097152 | tf_op jit(solution)/shard_map/all_to_all | solution.py:111
  111.4 0.8 copy.32
  112.2 14.9 %all-to-all-done = bf16[16,256,128]{2,1,0:T(8,128)(2,1)S(1)} async-done(((bf16[16,256,128]{2,1,0:T(8,128)(2,1)}), bf16[16,256,128]{2,1,0:T(8,128)(2,1)S(1)}, u32[]{:S(2)}, u32[]{:S(2)}) %all-to-all-start) | async-done | bytes 1048608 | tf_op jit(solution)/shard_map/all_to_all | solution.py:111
  127.2 1.0 copy.121
  (63 shorter events, 3.8 us)
Async XLA Ops:
  0.6 36.9 %copy-start = (bf16[1,2,2,2,128,128]{5,4,3,2,1,0:T(8,128)(2,1)S(1)}, bf16[1,2,2,2,128,128]{5,4,3,2,1,0:T(8,128)(2,1)}, u32[]{:S(2)}) copy-start(bf16[1,2,2,2,128,128]{5,4,3,2,1,0:T(8,128)(2,1)} %param.6) | copy-start | bytes 786436
  0.6 2.2 %copy-start.1 = (bf16[1,2,2,2,256,128]{5,4,3,2,1,0:T(8,128)(2,1)S(1)}, bf16[1,2,2,2,256,128]{5,4,3,2,1,0:T(8,128)(2,1)}, u32[]{:S(2)}) copy-start(bf16[1,2,2,2,256,128]{5,4,3,2,1,0:T(8,128)(2,1)} %param.5) | copy-start | bytes 1572868
  3.9 41.8 %collective-permute-start.5 = (bf16[1,2,2,2,256,128]{5,4,3,1,2,0:T(8,128)(2,1)}, bf16[1,2,2,2,256,128]{5,4,3,1,2,0:T(8,128)(2,1)}, u32[]{:S(2)}, u32[]{:S(2)}) collective-permute-start(bf16[1,2,2,2,256,128]{5,4,3,1,2,0:T(8,128)(2,1)} %fusion.3), channel_id=1, source_target_pairs={{0,16},{16,32},{32,48},{48,64},{64,80},{80,96},{96,112},{112,128},... | collective-permute-start | bytes 1572872 | tf_op jit(solution)/shard_map/ppermute | solution.py:24
  10.0 14.3 %copy-start.2 = (bf16[4,1,2,2,2,128,128]{6,5,4,3,2,1,0:T(8,128)(2,1)S(1)}, bf16[4,1,2,2,2,128,128]{6,5,4,3,2,1,0:T(8,128)(2,1)}, u32[]{:S(2)}) copy-start(bf16[4,1,2,2,2,128,128]{6,5,4,3,2,1,0:T(8,128)(2,1)} %param.8) | copy-start | bytes 3145732
  10.0 35.7 %collective-permute-start.2 = (bf16[1,2,2,2,256,128]{5,4,3,1,2,0:T(8,128)(2,1)}, bf16[1,2,2,2,256,128]{5,4,3,1,2,0:T(8,128)(2,1)}, u32[]{:S(2)}, u32[]{:S(2)}) collective-permute-start(bf16[1,2,2,2,256,128]{5,4,3,1,2,0:T(8,128)(2,1)} %get-tuple-element.38), channel_id=1, source_target_pairs={{0,496},{16,0},{32,16},{48,32},{64,48},{80,64},{96,80},{112,96},{1... | collective-permute-start | bytes 1572872 | tf_op jit(solution)/shard_map/ppermute | solution.py:24
  21.7 16.2 %collective-permute-start = (bf16[1,2,2,2,256,128]{5,4,3,1,2,0:T(8,128)(2,1)S(1)}, bf16[1,2,2,2,256,128]{5,4,3,1,2,0:T(8,128)(2,1)}, u32[]{:S(2)}, u32[]{:S(2)}) collective-permute-start(bf16[1,2,2,2,256,128]{5,4,3,1,2,0:T(8,128)(2,1)S(1)} %get-tuple-element.39), channel_id=1, source_target_pairs={{496,242},{498,496},{256,2},{258,256},{497,243},{499,497},{257,3},... | collective-permute-start | bytes 1572872 | tf_op jit(solution)/shard_map/ppermute | solution.py:24
  26.1 13.9 %collective-permute-start.4 = (bf16[2,1,2,1,2,256,128]{6,5,4,2,3,1,0:T(8,128)(2,1)}, bf16[2,1,2,1,2,256,128]{6,5,4,2,3,1,0:T(8,128)(2,1)}, u32[]{:S(2)}, u32[]{:S(2)}) collective-permute-start(bf16[2,1,2,1,2,256,128]{6,5,4,2,3,1,0:T(8,128)(2,1)} %pad_maximum_fusion), channel_id=1, source_target_pairs={{0,1},{1,0},{2,3},{3,2},{4,5},{5,4},{6,7},{7,6},{8,9},{9,8},{10,11... | collective-permute-start | bytes 1572872 | tf_op jit(solution)/shard_map/ppermute | solution.py:24
  29.8 27.2 %collective-permute-start.3 = (bf16[1,1,2,2,256,128]{5,4,3,2,1,0:T(8,128)(2,1)}, bf16[1,1,2,2,256,128]{5,4,3,2,1,0:T(8,128)(2,1)}, u32[]{:S(2)}, u32[]{:S(2)}) collective-permute-start(bf16[1,1,2,2,256,128]{5,4,3,2,1,0:T(8,128)(2,1)} %get-tuple-element.29), channel_id=1, source_target_pairs={{0,14},{2,0},{4,2},{6,4},{8,6},{10,8},{12,10},{14,12},{1,15},{3,1}... | collective-permute-start | bytes 786440 | tf_op jit(solution)/shard_map/ppermute | solution.py:24
  34.6 1.6 %copy-start.3 = (bf16[4,1,2,2,2,128,128]{6,5,4,3,2,1,0:T(8,128)(2,1)S(1)}, bf16[4,1,2,2,2,128,128]{6,5,4,3,2,1,0:T(8,128)(2,1)}, u32[]{:S(2)}) copy-start(bf16[4,1,2,2,2,128,128]{6,5,4,3,2,1,0:T(8,128)(2,1)} %param.7) | copy-start | bytes 3145732
  37.9 17.5 %collective-permute-start.1 = (bf16[1,2,2,2,256,128]{5,4,3,1,2,0:T(8,128)(2,1)}, bf16[1,2,2,2,256,128]{5,4,3,1,2,0:T(8,128)(2,1)}, u32[]{:S(2)}, u32[]{:S(2)}) collective-permute-start(bf16[1,2,2,2,256,128]{5,4,3,1,2,0:T(8,128)(2,1)} %collective-permute-done), channel_id=1, source_target_pairs={{242,0},{496,2},{2,240},{256,242},{243,1},{497,3},{3,241},{257,243... | collective-permute-start | bytes 1572872 | tf_op jit(solution)/shard_map/ppermute | solution.py:24
  40.1 21.7 %collective-permute-start.6 = (bf16[1,1,2,2,256,128]{5,4,3,2,1,0:T(8,128)(2,1)}, bf16[1,1,2,2,256,128]{5,4,3,2,1,0:T(8,128)(2,1)S(1)}, u32[]{:S(2)}, u32[]{:S(2)}) collective-permute-start(bf16[1,1,2,2,256,128]{5,4,3,2,1,0:T(8,128)(2,1)} %get-tuple-element.42), channel_id=1, source_target_pairs={{0,2},{2,4},{4,6},{6,8},{8,10},{10,12},{12,14},{14,0},{1,3},{3,5},... | collective-permute-start | bytes 786440 | tf_op jit(solution)/shard_map/ppermute | solution.py:24
  56.7 1.0 copy-start.10
  57.7 4.1 %copy-start.11 = (bf16[1,2,1,2,256,128]{5,4,3,2,1,0:T(8,128)(2,1)S(1)}, bf16[1,2,1,2,256,128]{5,4,3,2,1,0:T(8,128)(2,1)}, u32[]{:S(2)}) copy-start(bf16[1,2,1,2,256,128]{5,4,3,2,1,0:T(8,128)(2,1)} %get-tuple-element.41) | copy-start | bytes 786436
  57.7 4.1 %copy-start.12 = (bf16[1,1,2,2,256,128]{5,4,3,2,1,0:T(8,128)(2,1)S(1)}, bf16[1,1,2,2,256,128]{5,4,3,2,1,0:T(8,128)(2,1)}, u32[]{:S(2)}) copy-start(bf16[1,1,2,2,256,128]{5,4,3,2,1,0:T(8,128)(2,1)} %get-tuple-element.43) | copy-start | bytes 786436
  57.7 4.1 %copy-start.14 = (bf16[1,2,2,1,256,128]{5,4,3,2,1,0:T(8,128)(2,1)S(1)}, bf16[1,2,2,1,256,128]{5,4,3,2,1,0:T(8,128)(2,1)}, u32[]{:S(2)}) copy-start(bf16[1,2,2,1,256,128]{5,4,3,2,1,0:T(8,128)(2,1)} %get-tuple-element.26) | copy-start | bytes 786436
  57.7 4.1 %copy-start.15 = (bf16[1,2,2,1,256,128]{5,4,3,2,1,0:T(8,128)(2,1)S(1)}, bf16[1,2,2,1,256,128]{5,4,3,2,1,0:T(8,128)(2,1)}, u32[]{:S(2)}) copy-start(bf16[1,2,2,1,256,128]{5,4,3,2,1,0:T(8,128)(2,1)} %get-tuple-element.27) | copy-start | bytes 786436
  57.7 4.1 %copy-start.16 = (bf16[1,2,2,1,256,128]{5,4,3,2,1,0:T(8,128)(2,1)S(1)}, bf16[1,2,2,1,256,128]{5,4,3,2,1,0:T(8,128)(2,1)}, u32[]{:S(2)}) copy-start(bf16[1,2,2,1,256,128]{5,4,3,2,1,0:T(8,128)(2,1)} %get-tuple-element.44) | copy-start | bytes 786436
  57.7 4.1 %copy-start.17 = (bf16[1,2,2,1,256,128]{5,4,3,2,1,0:T(8,128)(2,1)S(1)}, bf16[1,2,2,1,256,128]{5,4,3,2,1,0:T(8,128)(2,1)}, u32[]{:S(2)}) copy-start(bf16[1,2,2,1,256,128]{5,4,3,2,1,0:T(8,128)(2,1)} %get-tuple-element.45) | copy-start | bytes 786436
  62.9 7.2 %copy-start.6 = (bf16[2,2,2,128,128]{4,3,2,1,0:T(8,128)(2,1)S(1)}, bf16[2,2,2,128,128]{4,3,2,1,0:T(8,128)(2,1)}, u32[]{:S(2)}) copy-start(bf16[2,2,2,128,128]{4,3,2,1,0:T(8,128)(2,1)} %get-tuple-element.9) | copy-start | bytes 786436
  62.9 42.1 %collective-permute-start.12 = (bf16[1,2,2,2,256,128]{5,4,3,1,2,0:T(8,128)(2,1)S(1)}, bf16[1,2,2,2,256,128]{5,4,3,1,2,0:T(8,128)(2,1)S(1)}, u32[]{:S(2)}, u32[]{:S(2)}) collective-permute-start(bf16[1,2,2,2,256,128]{5,4,3,1,2,0:T(8,128)(2,1)S(1)} %fusion.7), channel_id=1, source_target_pairs={{0,16},{16,32},{32,48},{48,64},{64,80},{80,96},{96,112},{112,128},... | collective-permute-start | bytes 1572872 | tf_op jit(solution)/shard_map/ppermute | solution.py:24
  64.4 10.6 %collective-permute-start.7 = (bf16[1,2,2,2,256,128]{5,4,3,1,2,0:T(8,128)(2,1)S(1)}, bf16[1,2,2,2,256,128]{5,4,3,1,2,0:T(8,128)(2,1)S(1)}, u32[]{:S(2)}, u32[]{:S(2)}) collective-permute-start(bf16[1,2,2,2,256,128]{5,4,3,1,2,0:T(8,128)(2,1)S(1)} %get-tuple-element.19), channel_id=1, source_target_pairs={{496,242},{498,496},{256,2},{258,256},{497,243},{499,497},{257,3},... | collective-permute-start | bytes 1572872 | tf_op jit(solution)/shard_map/ppermute | solution.py:24
  65.1 19.9 %collective-permute-start.9 = (bf16[1,2,2,2,256,128]{5,4,3,1,2,0:T(8,128)(2,1)S(1)}, bf16[1,2,2,2,256,128]{5,4,3,1,2,0:T(8,128)(2,1)S(1)}, u32[]{:S(2)}, u32[]{:S(2)}) collective-permute-start(bf16[1,2,2,2,256,128]{5,4,3,1,2,0:T(8,128)(2,1)S(1)} %get-tuple-element.18), channel_id=1, source_target_pairs={{0,496},{16,0},{32,16},{48,32},{64,48},{80,64},{96,80},{112,96},{1... | collective-permute-start | bytes 1572872 | tf_op jit(solution)/shard_map/ppermute | solution.py:24
  70.4 3.0 %copy-start.5 = (bf16[2,2,2,128,128]{4,3,2,1,0:T(8,128)(2,1)S(1)}, bf16[2,2,2,128,128]{4,3,2,1,0:T(8,128)(2,1)}, u32[]{:S(2)}) copy-start(bf16[2,2,2,128,128]{4,3,2,1,0:T(8,128)(2,1)} %get-tuple-element.8) | copy-start | bytes 786436
  70.5 12.4 %collective-permute-start.11 = (bf16[2,1,2,1,2,256,128]{6,5,4,2,3,1,0:T(8,128)(2,1)S(1)}, bf16[2,1,2,1,2,256,128]{6,5,4,2,3,1,0:T(8,128)(2,1)S(1)}, u32[]{:S(2)}, u32[]{:S(2)}) collective-permute-start(bf16[2,1,2,1,2,256,128]{6,5,4,2,3,1,0:T(8,128)(2,1)S(1)} %pad_maximum_fusion.1), channel_id=1, source_target_pairs={{0,1},{1,0},{2,3},{3,2},{4,5},{5,4},{6,7},{7,6},{8,9},{9,8},{10,11... | collective-permute-start | bytes 1572872 | tf_op jit(solution)/shard_map/ppermute | solution.py:24
  73.7 1.0 copy-start.4
  75.0 17.2 %collective-permute-start.8 = (bf16[1,2,2,2,256,128]{5,4,3,1,2,0:T(8,128)(2,1)S(1)}, bf16[1,2,2,2,256,128]{5,4,3,1,2,0:T(8,128)(2,1)S(1)}, u32[]{:S(2)}, u32[]{:S(2)}) collective-permute-start(bf16[1,2,2,2,256,128]{5,4,3,1,2,0:T(8,128)(2,1)S(1)} %collective-permute-done.7), channel_id=1, source_target_pairs={{242,0},{496,2},{2,240},{256,242},{243,1},{497,3},{3,241},{257,243... | collective-permute-start | bytes 1572872 | tf_op jit(solution)/shard_map/ppermute | solution.py:24
  76.4 22.9 %collective-permute-start.10 = (bf16[1,1,2,2,256,128]{5,4,3,2,1,0:T(8,128)(2,1)S(1)}, bf16[1,1,2,2,256,128]{5,4,3,2,1,0:T(8,128)(2,1)S(1)}, u32[]{:S(2)}, u32[]{:S(2)}) collective-permute-start(bf16[1,1,2,2,256,128]{5,4,3,2,1,0:T(8,128)(2,1)S(1)} %get-tuple-element.17), channel_id=1, source_target_pairs={{0,14},{2,0},{4,2},{6,4},{8,6},{10,8},{12,10},{14,12},{1,15},{3,1}... | collective-permute-start | bytes 786440 | tf_op jit(solution)/shard_map/ppermute | solution.py:24
  82.9 9.4 %copy-start.7 = (bf16[2,2,2,128,128]{4,3,2,1,0:T(8,128)(2,1)S(1)}, bf16[2,2,2,128,128]{4,3,2,1,0:T(8,128)(2,1)}, u32[]{:S(2)}) copy-start(bf16[2,2,2,128,128]{4,3,2,1,0:T(8,128)(2,1)} %get-tuple-element.6) | copy-start | bytes 786436
  82.9 22.1 %collective-permute-start.13 = (bf16[1,1,2,2,256,128]{5,4,3,1,2,0:T(8,128)(2,1)S(1)}, bf16[1,1,2,2,256,128]{5,4,3,1,2,0:T(8,128)(2,1)S(1)}, u32[]{:S(2)}, u32[]{:S(2)}) collective-permute-start(bf16[1,1,2,2,256,128]{5,4,3,1,2,0:T(8,128)(2,1)S(1)} %get-tuple-element.24), channel_id=1, source_target_pairs={{0,2},{2,4},{4,6},{6,8},{8,10},{10,12},{12,14},{14,0},{1,3},{3,5},... | collective-permute-start | bytes 786440 | tf_op jit(solution)/shard_map/ppermute | solution.py:24
  92.3 7.0 %copy-start.9 = (bf16[2,2,2,128,128]{4,3,2,1,0:T(8,128)(2,1)S(1)}, bf16[2,2,2,128,128]{4,3,2,1,0:T(8,128)(2,1)}, u32[]{:S(2)}) copy-start(bf16[2,2,2,128,128]{4,3,2,1,0:T(8,128)(2,1)} %get-tuple-element.5) | copy-start | bytes 786436
  99.2 1.0 copy-start.8
  100.2 4.8 %copy-start.13 = (bf16[2,2,2,128,128]{4,3,2,1,0:T(8,128)(2,1)S(1)}, bf16[2,2,2,128,128]{4,3,2,1,0:T(8,128)(2,1)}, u32[]{:S(2)}) copy-start(bf16[2,2,2,128,128]{4,3,2,1,0:T(8,128)(2,1)} %get-tuple-element.4) | copy-start | bytes 786436
  105.0 1.0 copy-start.18
  107.5 19.7 %all-to-all-start = ((bf16[16,256,128]{2,1,0:T(8,128)(2,1)}), bf16[16,256,128]{2,1,0:T(8,128)(2,1)S(1)}, u32[]{:S(2)}, u32[]{:S(2)}) async-start(bf16[16,256,128]{2,1,0:T(8,128)(2,1)} %broadcast_in_dim.2), calls=%async_computation | async-start | bytes 2097152 | tf_op jit(solution)/shard_map/all_to_all | solution.py:111

commit v3 on v1

--- a/solution.py
+++ b/solution.py
@@ -58,10 +58,14 @@
 
 
 def gather_pieces(piece):
-    count = lax.axis_size("gz") * lax.axis_size("gy")
-    copies = jnp.broadcast_to(piece[None], (count, *piece.shape))
-    gathered = lax.all_to_all(copies, ("gz", "gy"), 0, 0, tiled=True)
-    return gathered.reshape(1, count, *piece.shape)
+    nz = lax.axis_size("gz")
+    assert lax.axis_size("gy") == 2
+    copies = jnp.broadcast_to(piece[None], (nz, *piece.shape))
+    column = lax.all_to_all(copies, "gz", 0, 0, tiled=True)
+    partner = lax.ppermute(column, "gy", ring(2, 1))
+    first = lax.axis_index("gy") == 0
+    full = jnp.where(first, jnp.stack([column, partner], axis=1), jnp.stack([partner, column], axis=1))
+    return full.reshape(1, 2 * nz, *piece.shape)
 
 
 def per_device_body(source_field, clover, forward, backward, restrict_blocks):

time: 106 us -> 102 us (0.962)
  waiting for transfers between devices: 45.3 us -> 31.2 us
  blocking collectives: 0 us -> 12.7 us
  local copies, waits for them, and re-layouts: 6.26 us -> 4.19 us
  starting transfers between devices: 45.5 us -> 44.1 us
  other arithmetic: 0.1 us -> 1.17 us
    all_to_all x1 -> x0, waiting for transfers between devices: 14.8 us -> none  [gather_pieces(): gathered = lax.all_to_all(copies, ('gz', 'gy'), 0, 0, tiled=True)]
    all_to_all x0 -> x1, blocking collectives: none -> 12.7 us  [gather_pieces(): column = lax.all_to_all(copies, 'gz', 0, 0, tiled=True)]
    all_to_all x1 -> x0, starting transfers between devices: 5.59 us -> none  [gather_pieces(): gathered = lax.all_to_all(copies, ('gz', 'gy'), 0, 0, tiled=True)]
    ppermute x0 -> x1, starting transfers between devices: none -> 4.19 us  [gather_pieces(): partner = lax.ppermute(column, 'gy', ring(2, 1))]
    broadcast_in_dim x1, local copies, waits for them, and re-layouts: 1.17 us -> 0.07 us  [gather_pieces(): copies = jnp.broadcast_to(piece[None], (nz, *piece.shape))]
    select_n x0 -> x1, other arithmetic: none -> 1.07 us  [gather_pieces(): jnp.where(first, jnp.stack([column, partner], axis=1), jnp.stack([partner...]
    unnamed x14 -> x13, local copies, waits for them, and re-layouts: 4.46 us -> 3.49 us
where the time goes in v3:
time: 102 us
  starting transfers between devices  44.1 us (43%)
  waiting for transfers between devices  31.2 us (31%)
  blocking collectives  12.7 us (12%)
  matrix products  7.08 us (7%)
  local copies, waits for them, and re-layouts  4.19 us (4%)
  other arithmetic  1.17 us (1%)
  between operations  1.11 us (1%)
    ppermute x4, waiting for transfers between devices, neighbours(): got_p = lax.ppermute(last, axis, ring(count, 1))  30.5 us
    ppermute x4, starting transfers between devices, neighbours(): got_v = lax.ppermute(first, axis, ring(count, -1))  23.5 us
    all_to_all x1, blocking collectives, gather_pieces(): column = lax.all_to_all(copies, 'gz', 0, 0, tiled=True)  12.7 us
    ppermute x4, starting transfers between devices, neighbours(): got_p = lax.ppermute(last, axis, ring(count, 1))  10.1 us
    dot_general x18, matrix products, apply_block(): jnp.einsum('tzyxij,tzyxrj->tzyxri', blocks, vector, preferred_element_typ...  6.79 us
    ppermute x2, starting transfers between devices, neighbours(): both = lax.ppermute(jnp.stack([first, last]), axis, ring(2, 1))  6.32 us
    ppermute x1, starting transfers between devices, gather_pieces(): partner = lax.ppermute(column, 'gy', ring(2, 1))  4.19 us
    unnamed x13, local copies, waits for them, and re-layouts  3.49 us
  transfers between devices with their start and end apart: 11, of which 4 were waited for; matrix products, arithmetic and copies ran while one was open for 8% of the time, Pallas kernels for 0%

profile of v3, /device:TPU:1, one launch (start us, length us, event | category | flops | bytes accessed | tf_op | source)
XLA Modules:
  0.0 101.6 jit_solution(13951291356161858035)
XLA Ops:
  0.6 0.0 copy-start
  0.7 14.5 %collective-permute-start = (bf16[1,2,2,2,256,128]{5,4,3,2,1,0:T(8,128)(2,1)}, bf16[1,2,2,2,256,128]{5,4,3,2,1,0:T(8,128)(2,1)S(1)}, u32[]{:S(2)}, u32[]{:S(2)}) collective-permute-start(bf16[1,2,2,2,256,128]{5,4,3,2,1,0:T(8,128)(2,1)} %param.5), channel_id=1, source_target_pairs={{0,496},{16,0},{32,16},{48,32},{64,48},{80,64},{96,80},{112,96},{1... | collective-permute-start | bytes 1572872 | tf_op jit(solution)/shard_map/ppermute | solution.py:32
  15.2 1.1 %slice_bitcast_fusion.15 = (bf16[1,2,1,2,256,128]{5,4,3,1,2,0:T(8,128)(2,1)S(1)}, bf16[1,1,2,1,2,256,128]{6,5,4,2,3,1,0:T(8,128)(2,1)S(1)}) fusion(bf16[1,2,2,2,256,128]{5,4,3,2,1,0:T(8,128)(2,1)} %param.5), kind=kLoop, calls=%fused_computation.89 | loop fusion | bytes 1048576
  16.3 1.2 %fusion.3 = bf16[1,2,2,2,256,128]{5,4,3,2,1,0:T(8,128)(2,1)S(1)} fusion(bf16[1,2,2,2,256,128]{5,4,3,2,1,0:T(8,128)(2,1)S(1)} %copy-done.1, bf16[4,1,2,2,2,128,128]{6,5,4,3,2,1,0:T(8,128)(2,1)} %param.8), kind=kOutput, calls=%fused_computation.18 | convolution fusion | flops 67371008 | bytes 1310720 | tf_op jit(solution)/shard_map/tzyxij,tzyxrj->tzyxri/dot_general | solution.py:8
  17.6 0.1 pad_maximum_fusion
  17.6 3.0 %collective-permute-start.2 = (bf16[2,1,2,1,2,256,128]{6,5,4,2,3,1,0:T(8,128)(2,1)S(1)}, bf16[2,1,2,1,2,256,128]{6,5,4,2,3,1,0:T(8,128)(2,1)S(1)}, u32[]{:S(2)}, u32[]{:S(2)}) collective-permute-start(bf16[2,1,2,1,2,256,128]{6,5,4,2,3,1,0:T(8,128)(2,1)S(1)} %pad_maximum_fusion), channel_id=1, source_target_pairs={{0,1},{1,0},{2,3},{3,2},{4,5},{5,4},{6,7},{7,6},{8,9},{9,8},{10,11... | collective-permute-start | bytes 1572872 | tf_op jit(solution)/shard_map/ppermute | solution.py:29
  20.7 4.7 %collective-permute-start.1 = (bf16[1,1,2,2,256,128]{5,4,3,2,1,0:T(8,128)(2,1)S(1)}, bf16[1,1,2,2,256,128]{5,4,3,2,1,0:T(8,128)(2,1)S(1)}, u32[]{:S(2)}, u32[]{:S(2)}) collective-permute-start(bf16[1,1,2,2,256,128]{5,4,3,2,1,0:T(8,128)(2,1)S(1)} %get-tuple-element.29), channel_id=1, source_target_pairs={{0,14},{2,0},{4,2},{6,4},{8,6},{10,8},{12,10},{14,12},{1,15},{3,1}... | collective-permute-start | bytes 786440 | tf_op jit(solution)/shard_map/ppermute | solution.py:32
  25.4 0.3 fusion.5
  25.7 1.9 %collective-permute-start.4 = (bf16[1,1,2,2,256,128]{5,4,3,2,1,0:T(8,128)(2,1)S(1)}, bf16[1,1,2,2,256,128]{5,4,3,2,1,0:T(8,128)(2,1)S(1)}, u32[]{:S(2)}, u32[]{:S(2)}) collective-permute-start(bf16[1,1,2,2,256,128]{5,4,3,2,1,0:T(8,128)(2,1)S(1)} %get-tuple-element.38), channel_id=1, source_target_pairs={{0,2},{2,4},{4,6},{6,8},{8,10},{10,12},{12,14},{14,0},{1,3},{3,5},... | collective-permute-start | bytes 786440 | tf_op jit(solution)/shard_map/ppermute | solution.py:33
  27.7 0.3 fusion.4
  28.0 1.9 %collective-permute-start.3 = (bf16[1,2,2,2,256,128]{5,4,3,2,1,0:T(8,128)(2,1)S(1)}, bf16[1,2,2,2,256,128]{5,4,3,2,1,0:T(8,128)(2,1)S(1)}, u32[]{:S(2)}, u32[]{:S(2)}) collective-permute-start(bf16[1,2,2,2,256,128]{5,4,3,2,1,0:T(8,128)(2,1)S(1)} %fusion.4), channel_id=1, source_target_pairs={{0,16},{16,32},{32,48},{48,64},{64,80},{80,96},{96,112},{112,128},... | collective-permute-start | bytes 1572872 | tf_op jit(solution)/shard_map/ppermute | solution.py:33
  29.9 0.1 slice_bitcast_fusion.8
  30.0 0.3 fusion.23
  30.3 0.3 fusion.6
  30.6 0.0 copy-start.3
  30.6 0.1 fusion.57
  30.7 1.1 %copy-done.3 = bf16[4,1,2,2,2,128,128]{6,5,4,3,2,1,0:T(8,128)(2,1)S(1)} copy-done((bf16[4,1,2,2,2,128,128]{6,5,4,3,2,1,0:T(8,128)(2,1)S(1)}, bf16[4,1,2,2,2,128,128]{6,5,4,3,2,1,0:T(8,128)(2,1)}, u32[]{:S(2)}) %copy-start.3) | copy-done | bytes 1048600
  31.8 0.1 slice_bitcast_fusion.11
  32.0 0.3 convolution_add_fusion.6
  32.3 0.3 fusion.31
  32.6 0.3 fusion.2
  32.9 16.8 %collective-permute-done.4 = bf16[1,1,2,2,256,128]{5,4,3,2,1,0:T(8,128)(2,1)S(1)} collective-permute-done((bf16[1,1,2,2,256,128]{5,4,3,2,1,0:T(8,128)(2,1)S(1)}, bf16[1,1,2,2,256,128]{5,4,3,2,1,0:T(8,128)(2,1)S(1)}, u32[]{:S(2)}, u32[]{:S(2)}) %collective-permute-start.4) | collective-permute-done | bytes 262176 | tf_op jit(solution)/shard_map/ppermute | solution.py:33
  49.8 0.5 add_convert_fusion.1
  50.3 1.9 %collective-permute-start.5 = (bf16[1,2,2,2,256,128]{5,4,3,2,1,0:T(8,128)(2,1)S(1)}, bf16[1,2,2,2,256,128]{5,4,3,2,1,0:T(8,128)(2,1)S(1)}, u32[]{:S(2)}, u32[]{:S(2)}) collective-permute-start(bf16[1,2,2,2,256,128]{5,4,3,2,1,0:T(8,128)(2,1)S(1)} %add_convert_fusion.1), channel_id=1, source_target_pairs={{0,496},{16,0},{32,16},{48,32},{64,48},{80,64},{96,80},{112,96},{1... | collective-permute-start | bytes 1572872 | tf_op jit(solution)/shard_map/ppermute | solution.py:32
  52.3 2.4 %collective-permute-start.6 = (bf16[1,1,2,2,256,128]{5,4,3,2,1,0:T(8,128)(2,1)S(1)}, bf16[1,1,2,2,256,128]{5,4,3,2,1,0:T(8,128)(2,1)S(1)}, u32[]{:S(2)}, u32[]{:S(2)}) collective-permute-start(bf16[1,1,2,2,256,128]{5,4,3,2,1,0:T(8,128)(2,1)S(1)} %get-tuple-element.19), channel_id=1, source_target_pairs={{0,14},{2,0},{4,2},{6,4},{8,6},{10,8},{12,10},{14,12},{1,15},{3,1}... | collective-permute-start | bytes 786440 | tf_op jit(solution)/shard_map/ppermute | solution.py:32
  54.7 0.3 fusion.7
  55.1 0.1 pad_maximum_fusion.1
  55.2 3.3 %collective-permute-start.7 = (bf16[2,1,2,1,2,256,128]{6,5,4,2,3,1,0:T(8,128)(2,1)S(1)}, bf16[2,1,2,1,2,256,128]{6,5,4,2,3,1,0:T(8,128)(2,1)S(1)}, u32[]{:S(2)}, u32[]{:S(2)}) collective-permute-start(bf16[2,1,2,1,2,256,128]{6,5,4,2,3,1,0:T(8,128)(2,1)S(1)} %pad_maximum_fusion.1), channel_id=1, source_target_pairs={{0,1},{1,0},{2,3},{3,2},{4,5},{5,4},{6,7},{7,6},{8,9},{9,8},{10,11... | collective-permute-start | bytes 1572872 | tf_op jit(solution)/shard_map/ppermute | solution.py:29
  58.5 0.3 fusion.9
  58.8 2.6 %collective-permute-start.9 = (bf16[1,1,2,2,256,128]{5,4,3,1,2,0:T(8,128)(2,1)S(1)}, bf16[1,1,2,2,256,128]{5,4,3,1,2,0:T(8,128)(2,1)S(1)}, u32[]{:S(2)}, u32[]{:S(2)}) collective-permute-start(bf16[1,1,2,2,256,128]{5,4,3,1,2,0:T(8,128)(2,1)S(1)} %get-tuple-element.24), channel_id=1, source_target_pairs={{0,2},{2,4},{4,6},{6,8},{8,10},{10,12},{12,14},{14,0},{1,3},{3,5},... | collective-permute-start | bytes 786440 | tf_op jit(solution)/shard_map/ppermute | solution.py:33
  61.5 0.3 fusion.10
  61.8 0.3 fusion.8
  62.1 3.6 %collective-permute-start.8 = (bf16[1,2,2,2,256,128]{5,4,3,1,2,0:T(8,128)(2,1)S(1)}, bf16[1,2,2,2,256,128]{5,4,3,1,2,0:T(8,128)(2,1)S(1)}, u32[]{:S(2)}, u32[]{:S(2)}) collective-permute-start(bf16[1,2,2,2,256,128]{5,4,3,1,2,0:T(8,128)(2,1)S(1)} %fusion.8), channel_id=1, source_target_pairs={{0,16},{16,32},{32,48},{48,64},{64,80},{80,96},{96,112},{112,128},... | collective-permute-start | bytes 1572872 | tf_op jit(solution)/shard_map/ppermute | solution.py:33
  65.8 0.3 fusion.37
  66.1 0.3 convolution_add_fusion.3
  66.4 0.3 convolution_add_fusion.2
  66.8 0.3 convolution_add_fusion.1
  67.1 3.6 %collective-permute-done.9 = bf16[1,1,2,2,256,128]{5,4,3,1,2,0:T(8,128)(2,1)S(1)} collective-permute-done((bf16[1,1,2,2,256,128]{5,4,3,1,2,0:T(8,128)(2,1)S(1)}, bf16[1,1,2,2,256,128]{5,4,3,1,2,0:T(8,128)(2,1)S(1)}, u32[]{:S(2)}, u32[]{:S(2)}) %collective-permute-start.9) | collective-permute-done | bytes 262176 | tf_op jit(solution)/shard_map/ppermute | solution.py:33
  70.7 10.1 %collective-permute-done.8 = bf16[1,2,2,2,256,128]{5,4,3,1,2,0:T(8,128)(2,1)S(1)} collective-permute-done((bf16[1,2,2,2,256,128]{5,4,3,1,2,0:T(8,128)(2,1)S(1)}, bf16[1,2,2,2,256,128]{5,4,3,1,2,0:T(8,128)(2,1)S(1)}, u32[]{:S(2)}, u32[]{:S(2)}) %collective-permute-start.8) | collective-permute-done | bytes 524320 | tf_op jit(solution)/shard_map/ppermute | solution.py:33
  80.8 0.5 add_convert_fusion
  81.3 0.4 copy-done.4
  81.7 0.3 fusion.11
  82.0 0.1 broadcast_in_dim.2
  82.1 12.7 %all_to_all.5 = bf16[8,256,128]{2,1,0:T(8,128)(2,1)S(1)} all-to-all(bf16[8,256,128]{2,1,0:T(8,128)(2,1)S(1)} %broadcast_in_dim.2), channel_id=1, replica_groups=mesh['ta'=32,'gz'=8,'gy'=2] {'gz'}, dimensions={0} | all-to-all | bytes 1048576 | tf_op jit(solution)/shard_map/all_to_all | solution.py:64
  94.8 4.2 %collective-permute-start.10 = (bf16[8,256,128]{2,1,0:T(8,128)(2,1)S(1)}, bf16[8,256,128]{2,1,0:T(8,128)(2,1)S(1)}, u32[]{:S(2)}, u32[]{:S(2)}) collective-permute-start(bf16[8,256,128]{2,1,0:T(8,128)(2,1)S(1)} %all_to_all.5), channel_id=1, source_target_pairs={{0,1},{1,0},{2,3},{3,2},{4,5},{5,4},{6,7},{7,6},{8,9},{9,8},{10,11... | collective-permute-start | bytes 1572872 | tf_op jit(solution)/shard_map/ppermute | solution.py:65
  99.0 0.8 copy.24
  99.8 0.7 collective-permute-done.10
  100.5 1.1 %maximum_select_fusion = bf16[8,2,256,128]{3,2,1,0:T(8,128)(2,1)} fusion(bf16[8,1,256,128]{3,2,1,0:T(8,128)(2,1)S(1)} %bitcast.154, bf16[8,1,256,128]{3,2,1,0:T(8,128)(2,1)S(1)} %bitcast.152, pred[]{:T(512)S(6)} %eq.3), kind=kLoop, calls=%fused_computation.28 | loop fusion | flops 1572864 | bytes 2097153 | tf_op jit(solution)/shard_map/jit(_where)/select_n | solution.py:67
  (24 shorter events, 0.4 us)
Async XLA Ops:
  0.6 29.4 %copy-start = (bf16[1,2,2,2,128,128]{5,4,3,2,1,0:T(8,128)(2,1)S(1)}, bf16[1,2,2,2,128,128]{5,4,3,2,1,0:T(8,128)(2,1)}, u32[]{:S(2)}) copy-start(bf16[1,2,2,2,128,128]{5,4,3,2,1,0:T(8,128)(2,1)} %param.6) | copy-start | bytes 786436
  0.6 15.6 %copy-start.1 = (bf16[1,2,2,2,256,128]{5,4,3,2,1,0:T(8,128)(2,1)S(1)}, bf16[1,2,2,2,256,128]{5,4,3,2,1,0:T(8,128)(2,1)}, u32[]{:S(2)}) copy-start(bf16[1,2,2,2,256,128]{5,4,3,2,1,0:T(8,128)(2,1)} %param.5) | copy-start | bytes 1572868
  0.7 31.3 %collective-permute-start = (bf16[1,2,2,2,256,128]{5,4,3,2,1,0:T(8,128)(2,1)}, bf16[1,2,2,2,256,128]{5,4,3,2,1,0:T(8,128)(2,1)S(1)}, u32[]{:S(2)}, u32[]{:S(2)}) collective-permute-start(bf16[1,2,2,2,256,128]{5,4,3,2,1,0:T(8,128)(2,1)} %param.5), channel_id=1, source_target_pairs={{0,496},{16,0},{32,16},{48,32},{64,48},{80,64},{96,80},{112,96},{1... | collective-permute-start | bytes 1572872 | tf_op jit(solution)/shard_map/ppermute | solution.py:32
  17.6 7.8 %copy-start.2 = (bf16[4,1,2,2,2,128,128]{6,5,4,3,2,1,0:T(8,128)(2,1)S(1)}, bf16[4,1,2,2,2,128,128]{6,5,4,3,2,1,0:T(8,128)(2,1)}, u32[]{:S(2)}) copy-start(bf16[4,1,2,2,2,128,128]{6,5,4,3,2,1,0:T(8,128)(2,1)} %param.8) | copy-start | bytes 3145732
  17.6 14.6 %collective-permute-start.2 = (bf16[2,1,2,1,2,256,128]{6,5,4,2,3,1,0:T(8,128)(2,1)S(1)}, bf16[2,1,2,1,2,256,128]{6,5,4,2,3,1,0:T(8,128)(2,1)S(1)}, u32[]{:S(2)}, u32[]{:S(2)}) collective-permute-start(bf16[2,1,2,1,2,256,128]{6,5,4,2,3,1,0:T(8,128)(2,1)S(1)} %pad_maximum_fusion), channel_id=1, source_target_pairs={{0,1},{1,0},{2,3},{3,2},{4,5},{5,4},{6,7},{7,6},{8,9},{9,8},{10,11... | collective-permute-start | bytes 1572872 | tf_op jit(solution)/shard_map/ppermute | solution.py:29
  20.7 11.9 %collective-permute-start.1 = (bf16[1,1,2,2,256,128]{5,4,3,2,1,0:T(8,128)(2,1)S(1)}, bf16[1,1,2,2,256,128]{5,4,3,2,1,0:T(8,128)(2,1)S(1)}, u32[]{:S(2)}, u32[]{:S(2)}) collective-permute-start(bf16[1,1,2,2,256,128]{5,4,3,2,1,0:T(8,128)(2,1)S(1)} %get-tuple-element.29), channel_id=1, source_target_pairs={{0,14},{2,0},{4,2},{6,4},{8,6},{10,8},{12,10},{14,12},{1,15},{3,1}... | collective-permute-start | bytes 786440 | tf_op jit(solution)/shard_map/ppermute | solution.py:32
  25.7 24.0 %collective-permute-start.4 = (bf16[1,1,2,2,256,128]{5,4,3,2,1,0:T(8,128)(2,1)S(1)}, bf16[1,1,2,2,256,128]{5,4,3,2,1,0:T(8,128)(2,1)S(1)}, u32[]{:S(2)}, u32[]{:S(2)}) collective-permute-start(bf16[1,1,2,2,256,128]{5,4,3,2,1,0:T(8,128)(2,1)S(1)} %get-tuple-element.38), channel_id=1, source_target_pairs={{0,2},{2,4},{4,6},{6,8},{8,10},{10,12},{12,14},{14,0},{1,3},{3,5},... | collective-permute-start | bytes 786440 | tf_op jit(solution)/shard_map/ppermute | solution.py:33
  28.0 21.8 %collective-permute-start.3 = (bf16[1,2,2,2,256,128]{5,4,3,2,1,0:T(8,128)(2,1)S(1)}, bf16[1,2,2,2,256,128]{5,4,3,2,1,0:T(8,128)(2,1)S(1)}, u32[]{:S(2)}, u32[]{:S(2)}) collective-permute-start(bf16[1,2,2,2,256,128]{5,4,3,2,1,0:T(8,128)(2,1)S(1)} %fusion.4), channel_id=1, source_target_pairs={{0,16},{16,32},{32,48},{48,64},{64,80},{80,96},{96,112},{112,128},... | collective-permute-start | bytes 1572872 | tf_op jit(solution)/shard_map/ppermute | solution.py:33
  30.6 1.2 %copy-start.3 = (bf16[4,1,2,2,2,128,128]{6,5,4,3,2,1,0:T(8,128)(2,1)S(1)}, bf16[4,1,2,2,2,128,128]{6,5,4,3,2,1,0:T(8,128)(2,1)}, u32[]{:S(2)}) copy-start(bf16[4,1,2,2,2,128,128]{6,5,4,3,2,1,0:T(8,128)(2,1)} %param.7) | copy-start | bytes 3145732
  50.3 15.8 %collective-permute-start.5 = (bf16[1,2,2,2,256,128]{5,4,3,2,1,0:T(8,128)(2,1)S(1)}, bf16[1,2,2,2,256,128]{5,4,3,2,1,0:T(8,128)(2,1)S(1)}, u32[]{:S(2)}, u32[]{:S(2)}) collective-permute-start(bf16[1,2,2,2,256,128]{5,4,3,2,1,0:T(8,128)(2,1)S(1)} %add_convert_fusion.1), channel_id=1, source_target_pairs={{0,496},{16,0},{32,16},{48,32},{64,48},{80,64},{96,80},{112,96},{1... | collective-permute-start | bytes 1572872 | tf_op jit(solution)/shard_map/ppermute | solution.py:32
  52.3 14.1 %collective-permute-start.6 = (bf16[1,1,2,2,256,128]{5,4,3,2,1,0:T(8,128)(2,1)S(1)}, bf16[1,1,2,2,256,128]{5,4,3,2,1,0:T(8,128)(2,1)S(1)}, u32[]{:S(2)}, u32[]{:S(2)}) collective-permute-start(bf16[1,1,2,2,256,128]{5,4,3,2,1,0:T(8,128)(2,1)S(1)} %get-tuple-element.19), channel_id=1, source_target_pairs={{0,14},{2,0},{4,2},{6,4},{8,6},{10,8},{12,10},{14,12},{1,15},{3,1}... | collective-permute-start | bytes 786440 | tf_op jit(solution)/shard_map/ppermute | solution.py:32
  55.2 11.6 %collective-permute-start.7 = (bf16[2,1,2,1,2,256,128]{6,5,4,2,3,1,0:T(8,128)(2,1)S(1)}, bf16[2,1,2,1,2,256,128]{6,5,4,2,3,1,0:T(8,128)(2,1)S(1)}, u32[]{:S(2)}, u32[]{:S(2)}) collective-permute-start(bf16[2,1,2,1,2,256,128]{6,5,4,2,3,1,0:T(8,128)(2,1)S(1)} %pad_maximum_fusion.1), channel_id=1, source_target_pairs={{0,1},{1,0},{2,3},{3,2},{4,5},{5,4},{6,7},{7,6},{8,9},{9,8},{10,11... | collective-permute-start | bytes 1572872 | tf_op jit(solution)/shard_map/ppermute | solution.py:29
  58.8 11.9 %collective-permute-start.9 = (bf16[1,1,2,2,256,128]{5,4,3,1,2,0:T(8,128)(2,1)S(1)}, bf16[1,1,2,2,256,128]{5,4,3,1,2,0:T(8,128)(2,1)S(1)}, u32[]{:S(2)}, u32[]{:S(2)}) collective-permute-start(bf16[1,1,2,2,256,128]{5,4,3,1,2,0:T(8,128)(2,1)S(1)} %get-tuple-element.24), channel_id=1, source_target_pairs={{0,2},{2,4},{4,6},{6,8},{8,10},{10,12},{12,14},{14,0},{1,3},{3,5},... | collective-permute-start | bytes 786440 | tf_op jit(solution)/shard_map/ppermute | solution.py:33
  62.1 18.7 %collective-permute-start.8 = (bf16[1,2,2,2,256,128]{5,4,3,1,2,0:T(8,128)(2,1)S(1)}, bf16[1,2,2,2,256,128]{5,4,3,1,2,0:T(8,128)(2,1)S(1)}, u32[]{:S(2)}, u32[]{:S(2)}) collective-permute-start(bf16[1,2,2,2,256,128]{5,4,3,1,2,0:T(8,128)(2,1)S(1)} %fusion.8), channel_id=1, source_target_pairs={{0,16},{16,32},{32,48},{48,64},{64,80},{80,96},{96,112},{112,128},... | collective-permute-start | bytes 1572872 | tf_op jit(solution)/shard_map/ppermute | solution.py:33
  80.8 1.0 copy-start.4
  94.8 5.7 %collective-permute-start.10 = (bf16[8,256,128]{2,1,0:T(8,128)(2,1)S(1)}, bf16[8,256,128]{2,1,0:T(8,128)(2,1)S(1)}, u32[]{:S(2)}, u32[]{:S(2)}) collective-permute-start(bf16[8,256,128]{2,1,0:T(8,128)(2,1)S(1)} %all_to_all.5), channel_id=1, source_target_pairs={{0,1},{1,0},{2,3},{3,2},{4,5},{5,4},{6,7},{7,6},{8,9},{9,8},{10,11... | collective-permute-start | bytes 1572872 | tf_op jit(solution)/shard_map/ppermute | solution.py:65

commit v4 on v3

--- a/solution.py
+++ b/solution.py
@@ -68,14 +68,22 @@
     return full.reshape(1, 2 * nz, *piece.shape)
 
 
+HALVES = 2
+
+
 def per_device_body(source_field, clover, forward, backward, restrict_blocks):
     first_image = operate(source_field, clover, forward, backward)
-    second_image = operate(first_image, clover, forward, backward)
-    partial_sum = jnp.einsum(
-        "tzyxij,tzyxrj->ri", restrict_blocks, second_image, preferred_element_type=jnp.float32
-    )
-    restricted = gather_pieces(partial_sum.astype(jnp.bfloat16))
-    return (second_image, restricted)
+    rows = first_image.shape[4] // HALVES
+    images, pieces = [], []
+    for h in range(HALVES):
+        part = lax.slice_in_dim(first_image, h * rows, (h + 1) * rows, axis=4)
+        image = operate(part, clover, forward, backward)
+        partial_sum = jnp.einsum(
+            "tzyxij,tzyxrj->ri", restrict_blocks, image, preferred_element_type=jnp.float32
+        )
+        pieces.append(gather_pieces(partial_sum.astype(jnp.bfloat16)))
+        images.append(image)
+    return jnp.concatenate(images, axis=4), jnp.concatenate(pieces, axis=2)
 
 
 def solution(mesh):

time: 102 us -> 123 us (1.21)
  starting transfers between devices: 44.1 us -> 71.1 us
  blocking collectives: 12.7 us -> 0 us
  local copies, waits for them, and re-layouts: 4.19 us -> 9.49 us
  matrix products: 7.08 us -> 11.8 us
  waiting for transfers between devices: 31.2 us -> 27.1 us
    all_to_all x1 -> x0, blocking collectives: 12.7 us -> none  [gather_pieces(): column = lax.all_to_all(copies, 'gz', 0, 0, tiled=True)]
    ppermute x4 -> x6, waiting for transfers between devices: 30.5 us -> 19.6 us  [neighbours(): got_p = lax.ppermute(last, axis, ring(count, 1))]
    ppermute x4 -> x6, starting transfers between devices: 23.5 us -> 33.6 us  [neighbours(): got_v = lax.ppermute(first, axis, ring(count, -1))]
    all_to_all x0 -> x2, starting transfers between devices: none -> 8.25 us  [gather_pieces(): column = lax.all_to_all(copies, 'gz', 0, 0, tiled=True)]
    all_to_all x0 -> x2, waiting for transfers between devices: none -> 7.3 us  [gather_pieces(): column = lax.all_to_all(copies, 'gz', 0, 0, tiled=True)]
    dot_general x18 -> x27, matrix products: 6.79 us -> 11.4 us  [apply_block(): jnp.einsum('tzyxij,tzyxrj->tzyxri', blocks, vector, preferred_element_typ...]
    ppermute x4 -> x6, starting transfers between devices: 10.1 us -> 13.9 us  [neighbours(): got_p = lax.ppermute(last, axis, ring(count, 1))]
    ppermute x2 -> x3, starting transfers between devices: 6.32 us -> 9.37 us  [neighbours(): both = lax.ppermute(jnp.stack([first, last]), axis, ring(2, 1))]
  transfers between devices with their start and end apart: 11 -> 19, of which waited for: 4 -> 5; matrix products, arithmetic and copies ran while one was open for 8% -> 11% of each run, Pallas kernels for 0% -> 0%
where the time goes in v4:
time: 123 us; the launch traced here: 122 us
  starting transfers between devices  71.1 us (58%)
  waiting for transfers between devices  27.1 us (22%)
  matrix products  11.8 us (10%)
  local copies, waits for them, and re-layouts  9.49 us (8%)
  between operations  1.37 us (1%)
  other arithmetic  1.3 us (1%)
    ppermute x6, starting transfers between devices, neighbours(): got_v = lax.ppermute(first, axis, ring(count, -1))  33.6 us
    ppermute x6, waiting for transfers between devices, neighbours(): got_p = lax.ppermute(last, axis, ring(count, 1))  19.6 us
    ppermute x6, starting transfers between devices, neighbours(): got_p = lax.ppermute(last, axis, ring(count, 1))  13.9 us
    dot_general x27, matrix products, apply_block(): jnp.einsum('tzyxij,tzyxrj->tzyxri', blocks, vector, preferred_element_typ...  11.4 us
    ppermute x3, starting transfers between devices, neighbours(): both = lax.ppermute(jnp.stack([first, last]), axis, ring(2, 1))  9.37 us
    all_to_all x2, starting transfers between devices, gather_pieces(): column = lax.all_to_all(copies, 'gz', 0, 0, tiled=True)  8.25 us
    all_to_all x2, waiting for transfers between devices, gather_pieces(): column = lax.all_to_all(copies, 'gz', 0, 0, tiled=True)  7.3 us
    ppermute x2, starting transfers between devices, gather_pieces(): partner = lax.ppermute(column, 'gy', ring(2, 1))  5.94 us
  transfers between devices with their start and end apart: 19, of which 5 were waited for; matrix products, arithmetic and copies ran while one was open for 11% of the time, Pallas kernels for 0%

profile of v4, /device:TPU:1, one launch (start us, length us, event | category | flops | bytes accessed | tf_op | source)
XLA Modules:
  0.0 122.2 jit_solution(5395302973935044170)
XLA Ops:
  0.7 14.5 %collective-permute-start = (bf16[1,2,2,2,256,128]{5,4,3,2,1,0:T(8,128)(2,1)}, bf16[1,2,2,2,256,128]{5,4,3,2,1,0:T(8,128)(2,1)S(1)}, u32[]{:S(2)}, u32[]{:S(2)}) collective-permute-start(bf16[1,2,2,2,256,128]{5,4,3,2,1,0:T(8,128)(2,1)} %param.5), channel_id=1, source_target_pairs={{0,496},{16,0},{32,16},{48,32},{64,48},{80,64},{96,80},{112,96},{1... | collective-permute-start | bytes 1572872 | tf_op jit(solution)/shard_map/ppermute | solution.py:32
  15.2 1.1 slice_bitcast_fusion.10
  16.3 1.2 %fusion.2 = bf16[1,2,2,2,256,128]{5,4,3,2,1,0:T(8,128)(2,1)S(1)} fusion(bf16[1,2,2,2,256,128]{5,4,3,2,1,0:T(8,128)(2,1)S(1)} %copy-done.1, bf16[4,1,2,2,2,128,128]{6,5,4,3,2,1,0:T(8,128)(2,1)} %param.8), kind=kOutput, calls=%fused_computation.9 | convolution fusion | flops 67371008 | bytes 1310720 | tf_op jit(solution)/shard_map/tzyxij,tzyxrj->tzyxri/dot_general | solution.py:8
  17.6 3.0 %collective-permute-start.2 = (bf16[2,1,2,1,2,256,128]{6,5,4,2,3,1,0:T(8,128)(2,1)S(1)}, bf16[2,1,2,1,2,256,128]{6,5,4,2,3,1,0:T(8,128)(2,1)S(1)}, u32[]{:S(2)}, u32[]{:S(2)}) collective-permute-start(bf16[2,1,2,1,2,256,128]{6,5,4,2,3,1,0:T(8,128)(2,1)S(1)} %pad_maximum_fusion.1), channel_id=1, source_target_pairs={{0,1},{1,0},{2,3},{3,2},{4,5},{5,4},{6,7},{7,6},{8,9},{9,8},{10,11... | collective-permute-start | bytes 1572872 | tf_op jit(solution)/shard_map/ppermute | solution.py:29
  20.7 4.7 %collective-permute-start.1 = (bf16[1,1,2,2,256,128]{5,4,3,2,1,0:T(8,128)(2,1)S(1)}, bf16[1,1,2,2,256,128]{5,4,3,2,1,0:T(8,128)(2,1)S(1)}, u32[]{:S(2)}, u32[]{:S(2)}) collective-permute-start(bf16[1,1,2,2,256,128]{5,4,3,2,1,0:T(8,128)(2,1)S(1)} %get-tuple-element.31), channel_id=1, source_target_pairs={{0,14},{2,0},{4,2},{6,4},{8,6},{10,8},{12,10},{14,12},{1,15},{3,1}... | collective-permute-start | bytes 786440 | tf_op jit(solution)/shard_map/ppermute | solution.py:32
  25.7 1.9 %collective-permute-start.4 = (bf16[1,1,2,2,256,128]{5,4,3,2,1,0:T(8,128)(2,1)S(1)}, bf16[1,1,2,2,256,128]{5,4,3,2,1,0:T(8,128)(2,1)S(1)}, u32[]{:S(2)}, u32[]{:S(2)}) collective-permute-start(bf16[1,1,2,2,256,128]{5,4,3,2,1,0:T(8,128)(2,1)S(1)} %get-tuple-element.40), channel_id=1, source_target_pairs={{0,2},{2,4},{4,6},{6,8},{8,10},{10,12},{12,14},{14,0},{1,3},{3,5},... | collective-permute-start | bytes 786440 | tf_op jit(solution)/shard_map/ppermute | solution.py:33
  28.0 1.9 %collective-permute-start.3 = (bf16[1,2,2,2,256,128]{5,4,3,2,1,0:T(8,128)(2,1)S(1)}, bf16[1,2,2,2,256,128]{5,4,3,2,1,0:T(8,128)(2,1)S(1)}, u32[]{:S(2)}, u32[]{:S(2)}) collective-permute-start(bf16[1,2,2,2,256,128]{5,4,3,2,1,0:T(8,128)(2,1)S(1)} %fusion.3), channel_id=1, source_target_pairs={{0,16},{16,32},{32,48},{48,64},{64,80},{80,96},{96,112},{112,128},... | collective-permute-start | bytes 1572872 | tf_op jit(solution)/shard_map/ppermute | solution.py:33
  30.7 1.1 copy-done.3
  32.6 0.3 fusion.1
  32.9 16.8 %collective-permute-done.4 = bf16[1,1,2,2,256,128]{5,4,3,2,1,0:T(8,128)(2,1)S(1)} collective-permute-done((bf16[1,1,2,2,256,128]{5,4,3,2,1,0:T(8,128)(2,1)S(1)}, bf16[1,1,2,2,256,128]{5,4,3,2,1,0:T(8,128)(2,1)S(1)}, u32[]{:S(2)}, u32[]{:S(2)}) %collective-permute-start.4) | collective-permute-done | bytes 262176 | tf_op jit(solution)/shard_map/ppermute | solution.py:33
  49.8 0.5 add_convert_fusion
  50.5 0.7 fusion.85
  51.2 0.7 fusion.84
  52.0 0.3 fusion.65
  52.3 0.3 fusion.8
  52.6 0.3 fusion.11
  53.2 0.3 fusion.15
  53.5 0.3 fusion.10
  54.2 0.3 fusion.9
  54.5 0.3 fusion.13
  54.8 1.9 %collective-permute-start.5 = (bf16[1,2,2,2,128,128]{5,4,3,2,1,0:T(8,128)(2,1)S(1)}, bf16[1,2,2,2,128,128]{5,4,3,2,1,0:T(8,128)(2,1)S(1)}, u32[]{:S(2)}, u32[]{:S(2)}) collective-permute-start(bf16[1,2,2,2,128,128]{5,4,3,2,1,0:T(8,128)(2,1)S(1)} %get-tuple-element.24), channel_id=1, source_target_pairs={{0,496},{16,0},{32,16},{48,32},{64,48},{80,64},{96,80},{112,96},{1... | collective-permute-start | bytes 786440 | tf_op jit(solution)/shard_map/ppermute | solution.py:32
  56.7 2.4 %collective-permute-start.6 = (bf16[1,1,2,2,128,128]{5,4,3,2,1,0:T(8,128)(2,1)S(1)}, bf16[1,1,2,2,128,128]{5,4,3,2,1,0:T(8,128)(2,1)S(1)}, u32[]{:S(2)}, u32[]{:S(2)}) collective-permute-start(bf16[1,1,2,2,128,128]{5,4,3,2,1,0:T(8,128)(2,1)S(1)} %get-tuple-element.23), channel_id=1, source_target_pairs={{0,14},{2,0},{4,2},{6,4},{8,6},{10,8},{12,10},{14,12},{1,15},{3,1}... | collective-permute-start | bytes 393224 | tf_op jit(solution)/shard_map/ppermute | solution.py:32
  59.2 3.3 %collective-permute-start.7 = (bf16[2,1,2,1,2,128,128]{6,5,4,2,3,1,0:T(8,128)(2,1)S(1)}, bf16[2,1,2,1,2,128,128]{6,5,4,2,3,1,0:T(8,128)(2,1)S(1)}, u32[]{:S(2)}, u32[]{:S(2)}) collective-permute-start(bf16[2,1,2,1,2,128,128]{6,5,4,2,3,1,0:T(8,128)(2,1)S(1)} %pad_maximum_fusion.3), channel_id=1, source_target_pairs={{0,1},{1,0},{2,3},{3,2},{4,5},{5,4},{6,7},{7,6},{8,9},{9,8},{10,11... | collective-permute-start | bytes 786440 | tf_op jit(solution)/shard_map/ppermute | solution.py:29
  62.5 2.6 %collective-permute-start.9 = (bf16[1,1,2,2,128,128]{5,4,3,1,2,0:T(8,128)(2,1)S(1)}, bf16[1,1,2,2,128,128]{5,4,3,1,2,0:T(8,128)(2,1)S(1)}, u32[]{:S(2)}, u32[]{:S(2)}) collective-permute-start(bf16[1,1,2,2,128,128]{5,4,3,1,2,0:T(8,128)(2,1)S(1)} %get-tuple-element.48), channel_id=1, source_target_pairs={{0,2},{2,4},{4,6},{6,8},{8,10},{10,12},{12,14},{14,0},{1,3},{3,5},... | collective-permute-start | bytes 393224 | tf_op jit(solution)/shard_map/ppermute | solution.py:33
  65.2 3.6 %collective-permute-start.8 = (bf16[1,2,2,2,128,128]{5,4,3,1,2,0:T(8,128)(2,1)S(1)}, bf16[1,2,2,2,128,128]{5,4,3,1,2,0:T(8,128)(2,1)S(1)}, u32[]{:S(2)}, u32[]{:S(2)}) collective-permute-start(bf16[1,2,2,2,128,128]{5,4,3,1,2,0:T(8,128)(2,1)S(1)} %fusion.9), channel_id=1, source_target_pairs={{0,16},{16,32},{32,48},{48,64},{64,80},{80,96},{96,112},{112,128},... | collective-permute-start | bytes 786440 | tf_op jit(solution)/shard_map/ppermute | solution.py:33
  68.8 0.7 slice_bitcast_fusion.15
  69.5 0.7 fusion.93
  70.3 0.7 fusion.94
  71.3 5.3 %collective-permute-start.10 = (bf16[1,2,2,2,128,128]{5,4,3,2,1,0:T(8,128)(2,1)S(1)}, bf16[1,2,2,2,128,128]{5,4,3,2,1,0:T(8,128)(2,1)}, u32[]{:S(2)}, u32[]{:S(2)}) collective-permute-start(bf16[1,2,2,2,128,128]{5,4,3,2,1,0:T(8,128)(2,1)S(1)} %get-tuple-element.27), channel_id=1, source_target_pairs={{0,496},{16,0},{32,16},{48,32},{64,48},{80,64},{96,80},{112,96},{1... | collective-permute-start | bytes 786440 | tf_op jit(solution)/shard_map/ppermute | solution.py:32
  76.9 4.8 %collective-permute-start.11 = (bf16[1,1,2,2,128,128]{5,4,3,2,1,0:T(8,128)(2,1)}, bf16[1,1,2,2,128,128]{5,4,3,2,1,0:T(8,128)(2,1)S(1)}, u32[]{:S(2)}, u32[]{:S(2)}) collective-permute-start(bf16[1,1,2,2,128,128]{5,4,3,2,1,0:T(8,128)(2,1)} %get-tuple-element.21), channel_id=1, source_target_pairs={{0,14},{2,0},{4,2},{6,4},{8,6},{10,8},{12,10},{14,12},{1,15},{3,1}... | collective-permute-start | bytes 393224 | tf_op jit(solution)/shard_map/ppermute | solution.py:32
  82.0 3.0 %collective-permute-start.12 = (bf16[2,1,2,1,2,128,128]{6,5,4,2,3,1,0:T(8,128)(2,1)S(1)}, bf16[2,1,2,1,2,128,128]{6,5,4,2,3,1,0:T(8,128)(2,1)S(1)}, u32[]{:S(2)}, u32[]{:S(2)}) collective-permute-start(bf16[2,1,2,1,2,128,128]{6,5,4,2,3,1,0:T(8,128)(2,1)S(1)} %pad_maximum_fusion.4), channel_id=1, source_target_pairs={{0,1},{1,0},{2,3},{3,2},{4,5},{5,4},{6,7},{7,6},{8,9},{9,8},{10,11... | collective-permute-start | bytes 786440 | tf_op jit(solution)/shard_map/ppermute | solution.py:29
  85.4 1.9 %collective-permute-start.14 = (bf16[1,1,2,2,128,128]{5,4,3,1,2,0:T(8,128)(2,1)}, bf16[1,1,2,2,128,128]{5,4,3,1,2,0:T(8,128)(2,1)}, u32[]{:S(2)}, u32[]{:S(2)}) collective-permute-start(bf16[1,1,2,2,128,128]{5,4,3,1,2,0:T(8,128)(2,1)} %get-tuple-element.56), channel_id=1, source_target_pairs={{0,2},{2,4},{4,6},{6,8},{8,10},{10,12},{12,14},{14,0},{1,3},{3,5},... | collective-permute-start | bytes 393224 | tf_op jit(solution)/shard_map/ppermute | solution.py:33
  87.3 1.9 %collective-permute-start.13 = (bf16[1,2,2,2,128,128]{5,4,3,1,2,0:T(8,128)(2,1)S(1)}, bf16[1,2,2,2,128,128]{5,4,3,1,2,0:T(8,128)(2,1)}, u32[]{:S(2)}, u32[]{:S(2)}) collective-permute-start(bf16[1,2,2,2,128,128]{5,4,3,1,2,0:T(8,128)(2,1)S(1)} %fusion.13), channel_id=1, source_target_pairs={{0,16},{16,32},{32,48},{48,64},{64,80},{80,96},{96,112},{112,128},... | collective-permute-start | bytes 786440 | tf_op jit(solution)/shard_map/ppermute | solution.py:33
  89.3 0.4 add_convert_fusion.2
  89.6 0.6 copy-done.12
  90.4 0.7 broadcast_in_dim.4
  91.2 4.8 %all-to-all-start = ((bf16[8,128,128]{2,1,0:T(8,128)(2,1)}), bf16[8,128,128]{2,1,0:T(8,128)(2,1)S(1)}, u32[]{:S(2)}, u32[]{:S(2)}) async-start(bf16[8,128,128]{2,1,0:T(8,128)(2,1)} %broadcast_in_dim.4), calls=%async_computation | async-start | bytes 524288 | tf_op jit(solution)/shard_map/all_to_all | solution.py:64
  96.0 1.2 %convolution_add_fusion.6 = f32[2,2,2,128,128]{4,3,2,0,1:T(8,128)S(1)} fusion(f32[2,2,2,128,128]{4,3,2,0,1:T(8,128)S(1)} %fusion.63, bf16[2,2,2,128,128]{4,3,2,1,0:T(8,128)(2,1)S(1)} %get-tuple-element.6, bf16[1,2,2,2,128,128]{5,4,3,2,1,0:T(8,128)(2,1)} %collective-permute-done.10), kind=kOutput, calls=%fused_computation.17 | convolution fusion | flops 33685504 | bytes 1572864 | tf_op jit(solution)/shard_map/tzyxij,tzyxrj->tzyxri/dot_general | solution.py:8
  98.0 2.8 %collective-permute-done.13 = bf16[1,2,2,2,128,128]{5,4,3,1,2,0:T(8,128)(2,1)} collective-permute-done((bf16[1,2,2,2,128,128]{5,4,3,1,2,0:T(8,128)(2,1)S(1)}, bf16[1,2,2,2,128,128]{5,4,3,1,2,0:T(8,128)(2,1)}, u32[]{:S(2)}, u32[]{:S(2)}) %collective-permute-start.13) | collective-permute-done | bytes 262176 | tf_op jit(solution)/shard_map/ppermute | solution.py:33
  100.9 1.4 %add_convert_fusion.1 = bf16[1,2,2,2,128,128]{5,4,3,1,2,0:T(8,128)(2,1)S(1)} fusion(bf16[1,2,2,2,128,128]{5,4,3,1,2,0:T(8,128)(2,1)} %collective-permute-done.13, bf16[1,1,2,2,128,128]{5,4,3,1,2,0:T(8,128)(2,1)S(1)} %copy-done.9, bf16[1,1,2,2,128,128]{5,4,3,1,2,0:T(8,128)(2,1)} %collective-permute-done.14, ...), kind=kOutput, calls=%fused_computation.65 | convolution fusion | flops 35389440 | bytes 2359296 | tf_op jit(solution)/shard_map/tzyxij,tzyxrj->tzyxri/dot_general | solution.py:8
  102.5 3.2 %all-to-all-done = bf16[8,128,128]{2,1,0:T(8,128)(2,1)S(1)} async-done(((bf16[8,128,128]{2,1,0:T(8,128)(2,1)}), bf16[8,128,128]{2,1,0:T(8,128)(2,1)S(1)}, u32[]{:S(2)}, u32[]{:S(2)}) %all-to-all-start) | async-done | bytes 262176 | tf_op jit(solution)/shard_map/all_to_all | solution.py:64
  105.7 0.7 broadcast_in_dim.5
  106.4 3.4 %all-to-all-start.1 = ((bf16[8,128,128]{2,1,0:T(8,128)(2,1)}), bf16[8,128,128]{2,1,0:T(8,128)(2,1)S(1)}, u32[]{:S(2)}, u32[]{:S(2)}) async-start(bf16[8,128,128]{2,1,0:T(8,128)(2,1)} %broadcast_in_dim.5), calls=%async_computation.1 | async-start | bytes 524288 | tf_op jit(solution)/shard_map/all_to_all | solution.py:64
  109.8 2.4 %collective-permute-start.15 = (bf16[8,128,128]{2,1,0:T(8,128)(2,1)S(1)}, bf16[8,128,128]{2,1,0:T(8,128)(2,1)S(1)}, u32[]{:S(2)}, u32[]{:S(2)}) collective-permute-start(bf16[8,128,128]{2,1,0:T(8,128)(2,1)S(1)} %all-to-all-done), channel_id=1, source_target_pairs={{0,1},{1,0},{2,3},{3,2},{4,5},{5,4},{6,7},{7,6},{8,9},{9,8},{10,11... | collective-permute-start | bytes 786440 | tf_op jit(solution)/shard_map/ppermute | solution.py:65
  112.3 4.1 %all-to-all-done.1 = bf16[8,128,128]{2,1,0:T(8,128)(2,1)S(1)} async-done(((bf16[8,128,128]{2,1,0:T(8,128)(2,1)}), bf16[8,128,128]{2,1,0:T(8,128)(2,1)S(1)}, u32[]{:S(2)}, u32[]{:S(2)}) %all-to-all-start.1) | async-done | bytes 262176 | tf_op jit(solution)/shard_map/all_to_all | solution.py:64
  116.4 3.5 %collective-permute-start.16 = (bf16[8,128,128]{2,1,0:T(8,128)(2,1)S(1)}, bf16[8,128,128]{2,1,0:T(8,128)(2,1)S(1)}, u32[]{:S(2)}, u32[]{:S(2)}) collective-permute-start(bf16[8,128,128]{2,1,0:T(8,128)(2,1)S(1)} %all-to-all-done.1), channel_id=1, source_target_pairs={{0,1},{1,0},{2,3},{3,2},{4,5},{5,4},{6,7},{7,6},{8,9},{9,8},{10,11... | collective-permute-start | bytes 786440 | tf_op jit(solution)/shard_map/ppermute | solution.py:65
  120.0 0.8 copy.38
  121.1 1.1 pad_maximum_fusion
  (77 shorter events, 5.9 us)
Async XLA Ops:
  0.6 29.4 %copy-start = (bf16[1,2,2,2,128,128]{5,4,3,2,1,0:T(8,128)(2,1)S(1)}, bf16[1,2,2,2,128,128]{5,4,3,2,1,0:T(8,128)(2,1)}, u32[]{:S(2)}) copy-start(bf16[1,2,2,2,128,128]{5,4,3,2,1,0:T(8,128)(2,1)} %param.6) | copy-start | bytes 786436
  0.6 15.6 %copy-start.1 = (bf16[1,2,2,2,256,128]{5,4,3,2,1,0:T(8,128)(2,1)S(1)}, bf16[1,2,2,2,256,128]{5,4,3,2,1,0:T(8,128)(2,1)}, u32[]{:S(2)}) copy-start(bf16[1,2,2,2,256,128]{5,4,3,2,1,0:T(8,128)(2,1)} %param.5) | copy-start | bytes 1572868
  0.7 31.3 %collective-permute-start = (bf16[1,2,2,2,256,128]{5,4,3,2,1,0:T(8,128)(2,1)}, bf16[1,2,2,2,256,128]{5,4,3,2,1,0:T(8,128)(2,1)S(1)}, u32[]{:S(2)}, u32[]{:S(2)}) collective-permute-start(bf16[1,2,2,2,256,128]{5,4,3,2,1,0:T(8,128)(2,1)} %param.5), channel_id=1, source_target_pairs={{0,496},{16,0},{32,16},{48,32},{64,48},{80,64},{96,80},{112,96},{1... | collective-permute-start | bytes 1572872 | tf_op jit(solution)/shard_map/ppermute | solution.py:32
  17.6 7.8 %copy-start.2 = (bf16[4,1,2,2,2,128,128]{6,5,4,3,2,1,0:T(8,128)(2,1)S(1)}, bf16[4,1,2,2,2,128,128]{6,5,4,3,2,1,0:T(8,128)(2,1)}, u32[]{:S(2)}) copy-start(bf16[4,1,2,2,2,128,128]{6,5,4,3,2,1,0:T(8,128)(2,1)} %param.8) | copy-start | bytes 3145732
  17.6 14.6 %collective-permute-start.2 = (bf16[2,1,2,1,2,256,128]{6,5,4,2,3,1,0:T(8,128)(2,1)S(1)}, bf16[2,1,2,1,2,256,128]{6,5,4,2,3,1,0:T(8,128)(2,1)S(1)}, u32[]{:S(2)}, u32[]{:S(2)}) collective-permute-start(bf16[2,1,2,1,2,256,128]{6,5,4,2,3,1,0:T(8,128)(2,1)S(1)} %pad_maximum_fusion.1), channel_id=1, source_target_pairs={{0,1},{1,0},{2,3},{3,2},{4,5},{5,4},{6,7},{7,6},{8,9},{9,8},{10,11... | collective-permute-start | bytes 1572872 | tf_op jit(solution)/shard_map/ppermute | solution.py:29
  20.7 11.9 %collective-permute-start.1 = (bf16[1,1,2,2,256,128]{5,4,3,2,1,0:T(8,128)(2,1)S(1)}, bf16[1,1,2,2,256,128]{5,4,3,2,1,0:T(8,128)(2,1)S(1)}, u32[]{:S(2)}, u32[]{:S(2)}) collective-permute-start(bf16[1,1,2,2,256,128]{5,4,3,2,1,0:T(8,128)(2,1)S(1)} %get-tuple-element.31), channel_id=1, source_target_pairs={{0,14},{2,0},{4,2},{6,4},{8,6},{10,8},{12,10},{14,12},{1,15},{3,1}... | collective-permute-start | bytes 786440 | tf_op jit(solution)/shard_map/ppermute | solution.py:32
  25.7 24.0 %collective-permute-start.4 = (bf16[1,1,2,2,256,128]{5,4,3,2,1,0:T(8,128)(2,1)S(1)}, bf16[1,1,2,2,256,128]{5,4,3,2,1,0:T(8,128)(2,1)S(1)}, u32[]{:S(2)}, u32[]{:S(2)}) collective-permute-start(bf16[1,1,2,2,256,128]{5,4,3,2,1,0:T(8,128)(2,1)S(1)} %get-tuple-element.40), channel_id=1, source_target_pairs={{0,2},{2,4},{4,6},{6,8},{8,10},{10,12},{12,14},{14,0},{1,3},{3,5},... | collective-permute-start | bytes 786440 | tf_op jit(solution)/shard_map/ppermute | solution.py:33
  28.0 21.8 %collective-permute-start.3 = (bf16[1,2,2,2,256,128]{5,4,3,2,1,0:T(8,128)(2,1)S(1)}, bf16[1,2,2,2,256,128]{5,4,3,2,1,0:T(8,128)(2,1)S(1)}, u32[]{:S(2)}, u32[]{:S(2)}) collective-permute-start(bf16[1,2,2,2,256,128]{5,4,3,2,1,0:T(8,128)(2,1)S(1)} %fusion.3), channel_id=1, source_target_pairs={{0,16},{16,32},{32,48},{48,64},{64,80},{80,96},{96,112},{112,128},... | collective-permute-start | bytes 1572872 | tf_op jit(solution)/shard_map/ppermute | solution.py:33
  30.6 1.2 %copy-start.3 = (bf16[4,1,2,2,2,128,128]{6,5,4,3,2,1,0:T(8,128)(2,1)S(1)}, bf16[4,1,2,2,2,128,128]{6,5,4,3,2,1,0:T(8,128)(2,1)}, u32[]{:S(2)}) copy-start(bf16[4,1,2,2,2,128,128]{6,5,4,3,2,1,0:T(8,128)(2,1)} %param.7) | copy-start | bytes 3145732
  31.9 57.3 %copy-start.4 = (bf16[2,2,2,128,128]{4,3,2,1,0:T(8,128)(2,1)}, bf16[2,2,2,128,128]{4,3,2,1,0:T(8,128)(2,1)S(1)}, u32[]{:S(2)}) copy-start(bf16[2,2,2,128,128]{4,3,2,1,0:T(8,128)(2,1)S(1)} %get-tuple-element.4) | copy-start | bytes 786436
  54.8 16.5 %collective-permute-start.5 = (bf16[1,2,2,2,128,128]{5,4,3,2,1,0:T(8,128)(2,1)S(1)}, bf16[1,2,2,2,128,128]{5,4,3,2,1,0:T(8,128)(2,1)S(1)}, u32[]{:S(2)}, u32[]{:S(2)}) collective-permute-start(bf16[1,2,2,2,128,128]{5,4,3,2,1,0:T(8,128)(2,1)S(1)} %get-tuple-element.24), channel_id=1, source_target_pairs={{0,496},{16,0},{32,16},{48,32},{64,48},{80,64},{96,80},{112,96},{1... | collective-permute-start | bytes 786440 | tf_op jit(solution)/shard_map/ppermute | solution.py:32
  56.7 20.2 %collective-permute-start.6 = (bf16[1,1,2,2,128,128]{5,4,3,2,1,0:T(8,128)(2,1)S(1)}, bf16[1,1,2,2,128,128]{5,4,3,2,1,0:T(8,128)(2,1)S(1)}, u32[]{:S(2)}, u32[]{:S(2)}) collective-permute-start(bf16[1,1,2,2,128,128]{5,4,3,2,1,0:T(8,128)(2,1)S(1)} %get-tuple-element.23), channel_id=1, source_target_pairs={{0,14},{2,0},{4,2},{6,4},{8,6},{10,8},{12,10},{14,12},{1,15},{3,1}... | collective-permute-start | bytes 393224 | tf_op jit(solution)/shard_map/ppermute | solution.py:32
  59.2 22.8 %collective-permute-start.7 = (bf16[2,1,2,1,2,128,128]{6,5,4,2,3,1,0:T(8,128)(2,1)S(1)}, bf16[2,1,2,1,2,128,128]{6,5,4,2,3,1,0:T(8,128)(2,1)S(1)}, u32[]{:S(2)}, u32[]{:S(2)}) collective-permute-start(bf16[2,1,2,1,2,128,128]{6,5,4,2,3,1,0:T(8,128)(2,1)S(1)} %pad_maximum_fusion.3), channel_id=1, source_target_pairs={{0,1},{1,0},{2,3},{3,2},{4,5},{5,4},{6,7},{7,6},{8,9},{9,8},{10,11... | collective-permute-start | bytes 786440 | tf_op jit(solution)/shard_map/ppermute | solution.py:29
  62.5 22.8 %collective-permute-start.9 = (bf16[1,1,2,2,128,128]{5,4,3,1,2,0:T(8,128)(2,1)S(1)}, bf16[1,1,2,2,128,128]{5,4,3,1,2,0:T(8,128)(2,1)S(1)}, u32[]{:S(2)}, u32[]{:S(2)}) collective-permute-start(bf16[1,1,2,2,128,128]{5,4,3,1,2,0:T(8,128)(2,1)S(1)} %get-tuple-element.48), channel_id=1, source_target_pairs={{0,2},{2,4},{4,6},{6,8},{8,10},{10,12},{12,14},{14,0},{1,3},{3,5},... | collective-permute-start | bytes 393224 | tf_op jit(solution)/shard_map/ppermute | solution.py:33
  65.2 22.1 %collective-permute-start.8 = (bf16[1,2,2,2,128,128]{5,4,3,1,2,0:T(8,128)(2,1)S(1)}, bf16[1,2,2,2,128,128]{5,4,3,1,2,0:T(8,128)(2,1)S(1)}, u32[]{:S(2)}, u32[]{:S(2)}) collective-permute-start(bf16[1,2,2,2,128,128]{5,4,3,1,2,0:T(8,128)(2,1)S(1)} %fusion.9), channel_id=1, source_target_pairs={{0,16},{16,32},{32,48},{48,64},{64,80},{80,96},{96,112},{112,128},... | collective-permute-start | bytes 786440 | tf_op jit(solution)/shard_map/ppermute | solution.py:33
  71.3 24.7 %collective-permute-start.10 = (bf16[1,2,2,2,128,128]{5,4,3,2,1,0:T(8,128)(2,1)S(1)}, bf16[1,2,2,2,128,128]{5,4,3,2,1,0:T(8,128)(2,1)}, u32[]{:S(2)}, u32[]{:S(2)}) collective-permute-start(bf16[1,2,2,2,128,128]{5,4,3,2,1,0:T(8,128)(2,1)S(1)} %get-tuple-element.27), channel_id=1, source_target_pairs={{0,496},{16,0},{32,16},{48,32},{64,48},{80,64},{96,80},{112,96},{1... | collective-permute-start | bytes 786440 | tf_op jit(solution)/shard_map/ppermute | solution.py:32
  76.9 20.4 %collective-permute-start.11 = (bf16[1,1,2,2,128,128]{5,4,3,2,1,0:T(8,128)(2,1)}, bf16[1,1,2,2,128,128]{5,4,3,2,1,0:T(8,128)(2,1)S(1)}, u32[]{:S(2)}, u32[]{:S(2)}) collective-permute-start(bf16[1,1,2,2,128,128]{5,4,3,2,1,0:T(8,128)(2,1)} %get-tuple-element.21), channel_id=1, source_target_pairs={{0,14},{2,0},{4,2},{6,4},{8,6},{10,8},{12,10},{14,12},{1,15},{3,1}... | collective-permute-start | bytes 393224 | tf_op jit(solution)/shard_map/ppermute | solution.py:32
  82.0 15.7 %collective-permute-start.12 = (bf16[2,1,2,1,2,128,128]{6,5,4,2,3,1,0:T(8,128)(2,1)S(1)}, bf16[2,1,2,1,2,128,128]{6,5,4,2,3,1,0:T(8,128)(2,1)S(1)}, u32[]{:S(2)}, u32[]{:S(2)}) collective-permute-start(bf16[2,1,2,1,2,128,128]{6,5,4,2,3,1,0:T(8,128)(2,1)S(1)} %pad_maximum_fusion.4), channel_id=1, source_target_pairs={{0,1},{1,0},{2,3},{3,2},{4,5},{5,4},{6,7},{7,6},{8,9},{9,8},{10,11... | collective-permute-start | bytes 786440 | tf_op jit(solution)/shard_map/ppermute | solution.py:29
  85.4 12.6 %collective-permute-start.14 = (bf16[1,1,2,2,128,128]{5,4,3,1,2,0:T(8,128)(2,1)}, bf16[1,1,2,2,128,128]{5,4,3,1,2,0:T(8,128)(2,1)}, u32[]{:S(2)}, u32[]{:S(2)}) collective-permute-start(bf16[1,1,2,2,128,128]{5,4,3,1,2,0:T(8,128)(2,1)} %get-tuple-element.56), channel_id=1, source_target_pairs={{0,2},{2,4},{4,6},{6,8},{8,10},{10,12},{12,14},{14,0},{1,3},{3,5},... | collective-permute-start | bytes 393224 | tf_op jit(solution)/shard_map/ppermute | solution.py:33
  87.3 13.5 %collective-permute-start.13 = (bf16[1,2,2,2,128,128]{5,4,3,1,2,0:T(8,128)(2,1)S(1)}, bf16[1,2,2,2,128,128]{5,4,3,1,2,0:T(8,128)(2,1)}, u32[]{:S(2)}, u32[]{:S(2)}) collective-permute-start(bf16[1,2,2,2,128,128]{5,4,3,1,2,0:T(8,128)(2,1)S(1)} %fusion.13), channel_id=1, source_target_pairs={{0,16},{16,32},{32,48},{48,64},{64,80},{80,96},{96,112},{112,128},... | collective-permute-start | bytes 786440 | tf_op jit(solution)/shard_map/ppermute | solution.py:33
  89.3 1.0 copy-start.12
  91.2 14.5 %all-to-all-start = ((bf16[8,128,128]{2,1,0:T(8,128)(2,1)}), bf16[8,128,128]{2,1,0:T(8,128)(2,1)S(1)}, u32[]{:S(2)}, u32[]{:S(2)}) async-start(bf16[8,128,128]{2,1,0:T(8,128)(2,1)} %broadcast_in_dim.4), calls=%async_computation | async-start | bytes 524288 | tf_op jit(solution)/shard_map/all_to_all | solution.py:64
  97.6 3.2 %copy-start.5 = (bf16[2,2,2,128,128]{4,3,2,1,0:T(8,128)(2,1)S(1)}, bf16[2,2,2,128,128]{4,3,2,1,0:T(8,128)(2,1)}, u32[]{:S(2)}) copy-start(bf16[2,2,2,128,128]{4,3,2,1,0:T(8,128)(2,1)} %copy-done.4) | copy-start | bytes 786436
  97.6 3.2 %copy-start.6 = (bf16[1,2,1,2,128,128]{5,4,3,1,2,0:T(8,128)(2,1)S(1)}, bf16[1,2,1,2,128,128]{5,4,3,1,2,0:T(8,128)(2,1)}, u32[]{:S(2)}) copy-start(bf16[1,2,1,2,128,128]{5,4,3,1,2,0:T(8,128)(2,1)} %get-tuple-element.55) | copy-start | bytes 393220
  97.6 3.2 %copy-start.7 = (bf16[1,2,2,1,128,128]{5,4,3,1,2,0:T(8,128)(2,1)S(1)}, bf16[1,2,2,1,128,128]{5,4,3,1,2,0:T(8,128)(2,1)}, u32[]{:S(2)}) copy-start(bf16[1,2,2,1,128,128]{5,4,3,1,2,0:T(8,128)(2,1)} %get-tuple-element.52) | copy-start | bytes 393220
  97.6 3.2 %copy-start.8 = (bf16[1,2,2,1,128,128]{5,4,3,1,2,0:T(8,128)(2,1)S(1)}, bf16[1,2,2,1,128,128]{5,4,3,1,2,0:T(8,128)(2,1)}, u32[]{:S(2)}) copy-start(bf16[1,2,2,1,128,128]{5,4,3,1,2,0:T(8,128)(2,1)} %get-tuple-element.53) | copy-start | bytes 393220
  97.6 3.2 %copy-start.9 = (bf16[1,1,2,2,128,128]{5,4,3,1,2,0:T(8,128)(2,1)S(1)}, bf16[1,1,2,2,128,128]{5,4,3,1,2,0:T(8,128)(2,1)}, u32[]{:S(2)}) copy-start(bf16[1,1,2,2,128,128]{5,4,3,1,2,0:T(8,128)(2,1)} %get-tuple-element.57) | copy-start | bytes 393220
  97.6 3.2 %copy-start.10 = (bf16[1,2,2,1,128,128]{5,4,3,2,1,0:T(8,128)(2,1)S(1)}, bf16[1,2,2,1,128,128]{5,4,3,2,1,0:T(8,128)(2,1)}, u32[]{:S(2)}) copy-start(bf16[1,2,2,1,128,128]{5,4,3,2,1,0:T(8,128)(2,1)} %get-tuple-element.13) | copy-start | bytes 393220
  97.7 3.2 %copy-start.11 = (bf16[1,2,2,1,128,128]{5,4,3,2,1,0:T(8,128)(2,1)S(1)}, bf16[1,2,2,1,128,128]{5,4,3,2,1,0:T(8,128)(2,1)}, u32[]{:S(2)}) copy-start(bf16[1,2,2,1,128,128]{5,4,3,2,1,0:T(8,128)(2,1)} %get-tuple-element.15) | copy-start | bytes 393220
  100.8 1.4 %copy-start.13 = (bf16[1,2,2,2,128,128]{5,4,3,2,1,0:T(8,128)(2,1)S(1)}, bf16[1,2,2,2,128,128]{5,4,3,2,1,0:T(8,128)(2,1)}, u32[]{:S(2)}) copy-start(bf16[1,2,2,2,128,128]{5,4,3,2,1,0:T(8,128)(2,1)} %param.9) | copy-start | bytes 786436
  106.4 9.9 %all-to-all-start.1 = ((bf16[8,128,128]{2,1,0:T(8,128)(2,1)}), bf16[8,128,128]{2,1,0:T(8,128)(2,1)S(1)}, u32[]{:S(2)}, u32[]{:S(2)}) async-start(bf16[8,128,128]{2,1,0:T(8,128)(2,1)} %broadcast_in_dim.5), calls=%async_computation.1 | async-start | bytes 524288 | tf_op jit(solution)/shard_map/all_to_all | solution.py:64
  109.8 10.9 %collective-permute-start.15 = (bf16[8,128,128]{2,1,0:T(8,128)(2,1)S(1)}, bf16[8,128,128]{2,1,0:T(8,128)(2,1)S(1)}, u32[]{:S(2)}, u32[]{:S(2)}) collective-permute-start(bf16[8,128,128]{2,1,0:T(8,128)(2,1)S(1)} %all-to-all-done), channel_id=1, source_target_pairs={{0,1},{1,0},{2,3},{3,2},{4,5},{5,4},{6,7},{7,6},{8,9},{9,8},{10,11... | collective-permute-start | bytes 786440 | tf_op jit(solution)/shard_map/ppermute | solution.py:65
  116.4 4.7 %collective-permute-start.16 = (bf16[8,128,128]{2,1,0:T(8,128)(2,1)S(1)}, bf16[8,128,128]{2,1,0:T(8,128)(2,1)S(1)}, u32[]{:S(2)}, u32[]{:S(2)}) collective-permute-start(bf16[8,128,128]{2,1,0:T(8,128)(2,1)S(1)} %all-to-all-done.1), channel_id=1, source_target_pairs={{0,1},{1,0},{2,3},{3,2},{4,5},{5,4},{6,7},{7,6},{8,9},{9,8},{10,11... | collective-permute-start | bytes 786440 | tf_op jit(solution)/shard_map/ppermute | solution.py:65

commit v5 on v3

--- a/solution.py
+++ b/solution.py
@@ -62,9 +62,8 @@
     assert lax.axis_size("gy") == 2
     copies = jnp.broadcast_to(piece[None], (nz, *piece.shape))
     column = lax.all_to_all(copies, "gz", 0, 0, tiled=True)
-    partner = lax.ppermute(column, "gy", ring(2, 1))
-    first = lax.axis_index("gy") == 0
-    full = jnp.where(first, jnp.stack([column, partner], axis=1), jnp.stack([partner, column], axis=1))
+    both = jnp.broadcast_to(column[:, None], (nz, 2, *piece.shape))
+    full = lax.all_to_all(both, "gy", 1, 1, tiled=True)
     return full.reshape(1, 2 * nz, *piece.shape)
 
 

time: 102 us -> 104 us (1.020)
  waiting for transfers between devices: 31.2 us -> 38.4 us
  blocking collectives: 12.7 us -> 6.48 us
  local copies, waits for them, and re-layouts: 4.19 us -> 6.24 us
  other arithmetic: 1.17 us -> 0.1 us
    all_to_all x0 -> x1, waiting for transfers between devices: none -> 7.92 us  [gather_pieces(): column = lax.all_to_all(copies, 'gz', 0, 0, tiled=True)]
    all_to_all x1, blocking collectives: 12.7 us -> 6.48 us  [gather_pieces(): full = lax.all_to_all(both, 'gy', 1, 1, tiled=True)]
    ppermute x1 -> x0, starting transfers between devices: 4.19 us -> none  [gather_pieces(): partner = lax.ppermute(column, 'gy', ring(2, 1))]
    all_to_all x0 -> x1, starting transfers between devices: none -> 4.15 us  [gather_pieces(): column = lax.all_to_all(copies, 'gz', 0, 0, tiled=True)]
    select_n x1 -> x0, other arithmetic: 1.07 us -> none  [gather_pieces(): jnp.where(first, jnp.stack([column, partner], axis=1), jnp.stack([partner...]
    all_to_all x0 -> x1, local copies, waits for them, and re-layouts: none -> 1.04 us  [gather_pieces(): full = lax.all_to_all(both, 'gy', 1, 1, tiled=True)]
where the time goes in v5:
time: 104 us
  starting transfers between devices  44.1 us (42%)
  waiting for transfers between devices  38.4 us (37%)
  matrix products  7.06 us (7%)
  blocking collectives  6.48 us (6%)
  local copies, waits for them, and re-layouts  6.24 us (6%)
  between operations  1.09 us (1%)
    ppermute x4, waiting for transfers between devices, neighbours(): got_p = lax.ppermute(last, axis, ring(count, 1))  30.5 us
    ppermute x4, starting transfers between devices, neighbours(): got_v = lax.ppermute(first, axis, ring(count, -1))  23.5 us
    ppermute x4, starting transfers between devices, neighbours(): got_p = lax.ppermute(last, axis, ring(count, 1))  10.1 us
    all_to_all x1, waiting for transfers between devices, gather_pieces(): column = lax.all_to_all(copies, 'gz', 0, 0, tiled=True)  7.92 us
    dot_general x18, matrix products, apply_block(): jnp.einsum('tzyxij,tzyxrj->tzyxri', blocks, vector, preferred_element_typ...  6.77 us
    all_to_all x1, blocking collectives, gather_pieces(): full = lax.all_to_all(both, 'gy', 1, 1, tiled=True)  6.48 us
    ppermute x2, starting transfers between devices, neighbours(): both = lax.ppermute(jnp.stack([first, last]), axis, ring(2, 1))  6.34 us
    all_to_all x1, starting transfers between devices, gather_pieces(): column = lax.all_to_all(copies, 'gz', 0, 0, tiled=True)  4.15 us
  transfers between devices with their start and end apart: 11, of which 4 were waited for; matrix products, arithmetic and copies ran while one was open for 8% of the time, Pallas kernels for 0%

profile of v5, /device:TPU:1, one launch (start us, length us, event | category | flops | bytes accessed | tf_op | source)
XLA Modules:
  0.0 103.5 jit_solution(5658453789907203701)
XLA Ops:
  0.6 0.0 copy-start
  0.7 14.5 %collective-permute-start = (bf16[1,2,2,2,256,128]{5,4,3,2,1,0:T(8,128)(2,1)}, bf16[1,2,2,2,256,128]{5,4,3,2,1,0:T(8,128)(2,1)S(1)}, u32[]{:S(2)}, u32[]{:S(2)}) collective-permute-start(bf16[1,2,2,2,256,128]{5,4,3,2,1,0:T(8,128)(2,1)} %param.5), channel_id=1, source_target_pairs={{0,496},{16,0},{32,16},{48,32},{64,48},{80,64},{96,80},{112,96},{1... | collective-permute-start | bytes 1572872 | tf_op jit(solution)/shard_map/ppermute | solution.py:32
  15.2 1.1 %slice_bitcast_fusion.15 = (bf16[1,2,1,2,256,128]{5,4,3,1,2,0:T(8,128)(2,1)S(1)}, bf16[1,1,2,1,2,256,128]{6,5,4,2,3,1,0:T(8,128)(2,1)S(1)}) fusion(bf16[1,2,2,2,256,128]{5,4,3,2,1,0:T(8,128)(2,1)} %param.5), kind=kLoop, calls=%fused_computation.88 | loop fusion | bytes 1048576
  16.3 1.2 %fusion.3 = bf16[1,2,2,2,256,128]{5,4,3,2,1,0:T(8,128)(2,1)S(1)} fusion(bf16[1,2,2,2,256,128]{5,4,3,2,1,0:T(8,128)(2,1)S(1)} %copy-done.1, bf16[4,1,2,2,2,128,128]{6,5,4,3,2,1,0:T(8,128)(2,1)} %param.8), kind=kOutput, calls=%fused_computation.18 | convolution fusion | flops 67371008 | bytes 1310720 | tf_op jit(solution)/shard_map/tzyxij,tzyxrj->tzyxri/dot_general | solution.py:8
  17.6 0.1 pad_maximum_fusion
  17.6 3.0 %collective-permute-start.2 = (bf16[2,1,2,1,2,256,128]{6,5,4,2,3,1,0:T(8,128)(2,1)S(1)}, bf16[2,1,2,1,2,256,128]{6,5,4,2,3,1,0:T(8,128)(2,1)S(1)}, u32[]{:S(2)}, u32[]{:S(2)}) collective-permute-start(bf16[2,1,2,1,2,256,128]{6,5,4,2,3,1,0:T(8,128)(2,1)S(1)} %pad_maximum_fusion), channel_id=1, source_target_pairs={{0,1},{1,0},{2,3},{3,2},{4,5},{5,4},{6,7},{7,6},{8,9},{9,8},{10,11... | collective-permute-start | bytes 1572872 | tf_op jit(solution)/shard_map/ppermute | solution.py:29
  20.7 4.7 %collective-permute-start.1 = (bf16[1,1,2,2,256,128]{5,4,3,2,1,0:T(8,128)(2,1)S(1)}, bf16[1,1,2,2,256,128]{5,4,3,2,1,0:T(8,128)(2,1)S(1)}, u32[]{:S(2)}, u32[]{:S(2)}) collective-permute-start(bf16[1,1,2,2,256,128]{5,4,3,2,1,0:T(8,128)(2,1)S(1)} %get-tuple-element.33), channel_id=1, source_target_pairs={{0,14},{2,0},{4,2},{6,4},{8,6},{10,8},{12,10},{14,12},{1,15},{3,1}... | collective-permute-start | bytes 786440 | tf_op jit(solution)/shard_map/ppermute | solution.py:32
  25.4 0.3 fusion.5
  25.7 1.9 %collective-permute-start.4 = (bf16[1,1,2,2,256,128]{5,4,3,2,1,0:T(8,128)(2,1)S(1)}, bf16[1,1,2,2,256,128]{5,4,3,2,1,0:T(8,128)(2,1)S(1)}, u32[]{:S(2)}, u32[]{:S(2)}) collective-permute-start(bf16[1,1,2,2,256,128]{5,4,3,2,1,0:T(8,128)(2,1)S(1)} %get-tuple-element.42), channel_id=1, source_target_pairs={{0,2},{2,4},{4,6},{6,8},{8,10},{10,12},{12,14},{14,0},{1,3},{3,5},... | collective-permute-start | bytes 786440 | tf_op jit(solution)/shard_map/ppermute | solution.py:33
  27.7 0.3 fusion.4
  28.0 1.9 %collective-permute-start.3 = (bf16[1,2,2,2,256,128]{5,4,3,2,1,0:T(8,128)(2,1)S(1)}, bf16[1,2,2,2,256,128]{5,4,3,2,1,0:T(8,128)(2,1)S(1)}, u32[]{:S(2)}, u32[]{:S(2)}) collective-permute-start(bf16[1,2,2,2,256,128]{5,4,3,2,1,0:T(8,128)(2,1)S(1)} %fusion.4), channel_id=1, source_target_pairs={{0,16},{16,32},{32,48},{48,64},{64,80},{80,96},{96,112},{112,128},... | collective-permute-start | bytes 1572872 | tf_op jit(solution)/shard_map/ppermute | solution.py:33
  29.9 0.1 slice_bitcast_fusion.8
  30.0 0.3 fusion.23
  30.3 0.3 fusion.6
  30.6 0.1 fusion.57
  30.7 1.1 %copy-done.3 = bf16[4,1,2,2,2,128,128]{6,5,4,3,2,1,0:T(8,128)(2,1)S(1)} copy-done((bf16[4,1,2,2,2,128,128]{6,5,4,3,2,1,0:T(8,128)(2,1)S(1)}, bf16[4,1,2,2,2,128,128]{6,5,4,3,2,1,0:T(8,128)(2,1)}, u32[]{:S(2)}) %copy-start.3) | copy-done | bytes 1048600
  31.8 0.1 slice_bitcast_fusion.11
  32.0 0.3 convolution_add_fusion.6
  32.3 0.3 fusion.31
  32.6 0.3 fusion.2
  32.9 16.8 %collective-permute-done.4 = bf16[1,1,2,2,256,128]{5,4,3,2,1,0:T(8,128)(2,1)S(1)} collective-permute-done((bf16[1,1,2,2,256,128]{5,4,3,2,1,0:T(8,128)(2,1)S(1)}, bf16[1,1,2,2,256,128]{5,4,3,2,1,0:T(8,128)(2,1)S(1)}, u32[]{:S(2)}, u32[]{:S(2)}) %collective-permute-start.4) | collective-permute-done | bytes 262176 | tf_op jit(solution)/shard_map/ppermute | solution.py:33
  49.8 0.5 add_convert_fusion.1
  50.3 1.9 %collective-permute-start.5 = (bf16[1,2,2,2,256,128]{5,4,3,2,1,0:T(8,128)(2,1)S(1)}, bf16[1,2,2,2,256,128]{5,4,3,2,1,0:T(8,128)(2,1)S(1)}, u32[]{:S(2)}, u32[]{:S(2)}) collective-permute-start(bf16[1,2,2,2,256,128]{5,4,3,2,1,0:T(8,128)(2,1)S(1)} %add_convert_fusion.1), channel_id=1, source_target_pairs={{0,496},{16,0},{32,16},{48,32},{64,48},{80,64},{96,80},{112,96},{1... | collective-permute-start | bytes 1572872 | tf_op jit(solution)/shard_map/ppermute | solution.py:32
  52.3 2.4 %collective-permute-start.6 = (bf16[1,1,2,2,256,128]{5,4,3,2,1,0:T(8,128)(2,1)S(1)}, bf16[1,1,2,2,256,128]{5,4,3,2,1,0:T(8,128)(2,1)S(1)}, u32[]{:S(2)}, u32[]{:S(2)}) collective-permute-start(bf16[1,1,2,2,256,128]{5,4,3,2,1,0:T(8,128)(2,1)S(1)} %get-tuple-element.23), channel_id=1, source_target_pairs={{0,14},{2,0},{4,2},{6,4},{8,6},{10,8},{12,10},{14,12},{1,15},{3,1}... | collective-permute-start | bytes 786440 | tf_op jit(solution)/shard_map/ppermute | solution.py:32
  54.7 0.3 fusion.7
  55.1 0.1 pad_maximum_fusion.1
  55.1 3.3 %collective-permute-start.7 = (bf16[2,1,2,1,2,256,128]{6,5,4,2,3,1,0:T(8,128)(2,1)S(1)}, bf16[2,1,2,1,2,256,128]{6,5,4,2,3,1,0:T(8,128)(2,1)S(1)}, u32[]{:S(2)}, u32[]{:S(2)}) collective-permute-start(bf16[2,1,2,1,2,256,128]{6,5,4,2,3,1,0:T(8,128)(2,1)S(1)} %pad_maximum_fusion.1), channel_id=1, source_target_pairs={{0,1},{1,0},{2,3},{3,2},{4,5},{5,4},{6,7},{7,6},{8,9},{9,8},{10,11... | collective-permute-start | bytes 1572872 | tf_op jit(solution)/shard_map/ppermute | solution.py:29
  58.5 0.3 fusion.9
  58.8 2.6 %collective-permute-start.9 = (bf16[1,1,2,2,256,128]{5,4,3,1,2,0:T(8,128)(2,1)S(1)}, bf16[1,1,2,2,256,128]{5,4,3,1,2,0:T(8,128)(2,1)S(1)}, u32[]{:S(2)}, u32[]{:S(2)}) collective-permute-start(bf16[1,1,2,2,256,128]{5,4,3,1,2,0:T(8,128)(2,1)S(1)} %get-tuple-element.28), channel_id=1, source_target_pairs={{0,2},{2,4},{4,6},{6,8},{8,10},{10,12},{12,14},{14,0},{1,3},{3,5},... | collective-permute-start | bytes 786440 | tf_op jit(solution)/shard_map/ppermute | solution.py:33
  61.5 0.3 fusion.10
  61.8 0.3 fusion.8
  62.1 3.6 %collective-permute-start.8 = (bf16[1,2,2,2,256,128]{5,4,3,1,2,0:T(8,128)(2,1)S(1)}, bf16[1,2,2,2,256,128]{5,4,3,1,2,0:T(8,128)(2,1)S(1)}, u32[]{:S(2)}, u32[]{:S(2)}) collective-permute-start(bf16[1,2,2,2,256,128]{5,4,3,1,2,0:T(8,128)(2,1)S(1)} %fusion.8), channel_id=1, source_target_pairs={{0,16},{16,32},{32,48},{48,64},{64,80},{80,96},{96,112},{112,128},... | collective-permute-start | bytes 1572872 | tf_op jit(solution)/shard_map/ppermute | solution.py:33
  65.8 0.3 fusion.37
  66.1 0.3 convolution_add_fusion.3
  66.4 0.3 convolution_add_fusion.2
  66.8 0.3 convolution_add_fusion.1
  67.1 3.6 %collective-permute-done.9 = bf16[1,1,2,2,256,128]{5,4,3,1,2,0:T(8,128)(2,1)S(1)} collective-permute-done((bf16[1,1,2,2,256,128]{5,4,3,1,2,0:T(8,128)(2,1)S(1)}, bf16[1,1,2,2,256,128]{5,4,3,1,2,0:T(8,128)(2,1)S(1)}, u32[]{:S(2)}, u32[]{:S(2)}) %collective-permute-start.9) | collective-permute-done | bytes 262176 | tf_op jit(solution)/shard_map/ppermute | solution.py:33
  70.7 10.1 %collective-permute-done.8 = bf16[1,2,2,2,256,128]{5,4,3,1,2,0:T(8,128)(2,1)S(1)} collective-permute-done((bf16[1,2,2,2,256,128]{5,4,3,1,2,0:T(8,128)(2,1)S(1)}, bf16[1,2,2,2,256,128]{5,4,3,1,2,0:T(8,128)(2,1)S(1)}, u32[]{:S(2)}, u32[]{:S(2)}) %collective-permute-start.8) | collective-permute-done | bytes 524320 | tf_op jit(solution)/shard_map/ppermute | solution.py:33
  80.8 0.5 add_convert_fusion
  81.3 0.4 copy-done.4
  81.7 0.3 fusion.11
  82.0 0.9 broadcast_in_dim.4
  82.9 4.2 %all-to-all-start = ((bf16[8,256,128]{2,1,0:T(8,128)(2,1)}), bf16[8,256,128]{2,1,0:T(8,128)(2,1)S(1)}, u32[]{:S(2)}, u32[]{:S(2)}) async-start(bf16[8,256,128]{2,1,0:T(8,128)(2,1)} %broadcast_in_dim.4), calls=%async_computation | async-start | bytes 1048576 | tf_op jit(solution)/shard_map/all_to_all | solution.py:64
  87.0 0.8 copy.61
  87.9 7.9 %all-to-all-done = bf16[8,256,128]{2,1,0:T(8,128)(2,1)S(1)} async-done(((bf16[8,256,128]{2,1,0:T(8,128)(2,1)}), bf16[8,256,128]{2,1,0:T(8,128)(2,1)S(1)}, u32[]{:S(2)}, u32[]{:S(2)}) %all-to-all-start) | async-done | bytes 524320 | tf_op jit(solution)/shard_map/all_to_all | solution.py:64
  95.8 0.2 broadcast_in_dim.5
  96.0 6.5 %all_to_all.10 = bf16[8,2,256,128]{3,2,0,1:T(8,128)(2,1)S(1)} all-to-all(bf16[8,2,256,128]{3,2,0,1:T(8,128)(2,1)S(1)} %broadcast_in_dim.5), channel_id=1, replica_groups=mesh['ta'=32,'gz'=8,'gy'=2] {'gy'}, dimensions={1} | all-to-all | bytes 2097152 | tf_op jit(solution)/shard_map/all_to_all | solution.py:66
  102.5 1.0 %copy.60 = bf16[8,2,256,128]{3,2,1,0:T(8,128)(2,1)} copy(bf16[8,2,256,128]{3,2,0,1:T(8,128)(2,1)S(1)} %all_to_all.10) | data formatting | bytes 2097152 | tf_op jit(solution)/shard_map/all_to_all | solution.py:66
  (25 shorter events, 0.4 us)
Async XLA Ops:
  0.6 29.4 %copy-start = (bf16[1,2,2,2,128,128]{5,4,3,2,1,0:T(8,128)(2,1)S(1)}, bf16[1,2,2,2,128,128]{5,4,3,2,1,0:T(8,128)(2,1)}, u32[]{:S(2)}) copy-start(bf16[1,2,2,2,128,128]{5,4,3,2,1,0:T(8,128)(2,1)} %param.6) | copy-start | bytes 786436
  0.6 15.6 %copy-start.1 = (bf16[1,2,2,2,256,128]{5,4,3,2,1,0:T(8,128)(2,1)S(1)}, bf16[1,2,2,2,256,128]{5,4,3,2,1,0:T(8,128)(2,1)}, u32[]{:S(2)}) copy-start(bf16[1,2,2,2,256,128]{5,4,3,2,1,0:T(8,128)(2,1)} %param.5) | copy-start | bytes 1572868
  0.7 31.3 %collective-permute-start = (bf16[1,2,2,2,256,128]{5,4,3,2,1,0:T(8,128)(2,1)}, bf16[1,2,2,2,256,128]{5,4,3,2,1,0:T(8,128)(2,1)S(1)}, u32[]{:S(2)}, u32[]{:S(2)}) collective-permute-start(bf16[1,2,2,2,256,128]{5,4,3,2,1,0:T(8,128)(2,1)} %param.5), channel_id=1, source_target_pairs={{0,496},{16,0},{32,16},{48,32},{64,48},{80,64},{96,80},{112,96},{1... | collective-permute-start | bytes 1572872 | tf_op jit(solution)/shard_map/ppermute | solution.py:32
  17.6 7.8 %copy-start.2 = (bf16[4,1,2,2,2,128,128]{6,5,4,3,2,1,0:T(8,128)(2,1)S(1)}, bf16[4,1,2,2,2,128,128]{6,5,4,3,2,1,0:T(8,128)(2,1)}, u32[]{:S(2)}) copy-start(bf16[4,1,2,2,2,128,128]{6,5,4,3,2,1,0:T(8,128)(2,1)} %param.8) | copy-start | bytes 3145732
  17.6 14.6 %collective-permute-start.2 = (bf16[2,1,2,1,2,256,128]{6,5,4,2,3,1,0:T(8,128)(2,1)S(1)}, bf16[2,1,2,1,2,256,128]{6,5,4,2,3,1,0:T(8,128)(2,1)S(1)}, u32[]{:S(2)}, u32[]{:S(2)}) collective-permute-start(bf16[2,1,2,1,2,256,128]{6,5,4,2,3,1,0:T(8,128)(2,1)S(1)} %pad_maximum_fusion), channel_id=1, source_target_pairs={{0,1},{1,0},{2,3},{3,2},{4,5},{5,4},{6,7},{7,6},{8,9},{9,8},{10,11... | collective-permute-start | bytes 1572872 | tf_op jit(solution)/shard_map/ppermute | solution.py:29
  20.7 11.9 %collective-permute-start.1 = (bf16[1,1,2,2,256,128]{5,4,3,2,1,0:T(8,128)(2,1)S(1)}, bf16[1,1,2,2,256,128]{5,4,3,2,1,0:T(8,128)(2,1)S(1)}, u32[]{:S(2)}, u32[]{:S(2)}) collective-permute-start(bf16[1,1,2,2,256,128]{5,4,3,2,1,0:T(8,128)(2,1)S(1)} %get-tuple-element.33), channel_id=1, source_target_pairs={{0,14},{2,0},{4,2},{6,4},{8,6},{10,8},{12,10},{14,12},{1,15},{3,1}... | collective-permute-start | bytes 786440 | tf_op jit(solution)/shard_map/ppermute | solution.py:32
  25.7 24.0 %collective-permute-start.4 = (bf16[1,1,2,2,256,128]{5,4,3,2,1,0:T(8,128)(2,1)S(1)}, bf16[1,1,2,2,256,128]{5,4,3,2,1,0:T(8,128)(2,1)S(1)}, u32[]{:S(2)}, u32[]{:S(2)}) collective-permute-start(bf16[1,1,2,2,256,128]{5,4,3,2,1,0:T(8,128)(2,1)S(1)} %get-tuple-element.42), channel_id=1, source_target_pairs={{0,2},{2,4},{4,6},{6,8},{8,10},{10,12},{12,14},{14,0},{1,3},{3,5},... | collective-permute-start | bytes 786440 | tf_op jit(solution)/shard_map/ppermute | solution.py:33
  28.0 21.8 %collective-permute-start.3 = (bf16[1,2,2,2,256,128]{5,4,3,2,1,0:T(8,128)(2,1)S(1)}, bf16[1,2,2,2,256,128]{5,4,3,2,1,0:T(8,128)(2,1)S(1)}, u32[]{:S(2)}, u32[]{:S(2)}) collective-permute-start(bf16[1,2,2,2,256,128]{5,4,3,2,1,0:T(8,128)(2,1)S(1)} %fusion.4), channel_id=1, source_target_pairs={{0,16},{16,32},{32,48},{48,64},{64,80},{80,96},{96,112},{112,128},... | collective-permute-start | bytes 1572872 | tf_op jit(solution)/shard_map/ppermute | solution.py:33
  30.6 1.2 %copy-start.3 = (bf16[4,1,2,2,2,128,128]{6,5,4,3,2,1,0:T(8,128)(2,1)S(1)}, bf16[4,1,2,2,2,128,128]{6,5,4,3,2,1,0:T(8,128)(2,1)}, u32[]{:S(2)}) copy-start(bf16[4,1,2,2,2,128,128]{6,5,4,3,2,1,0:T(8,128)(2,1)} %param.7) | copy-start | bytes 3145732
  50.3 15.8 %collective-permute-start.5 = (bf16[1,2,2,2,256,128]{5,4,3,2,1,0:T(8,128)(2,1)S(1)}, bf16[1,2,2,2,256,128]{5,4,3,2,1,0:T(8,128)(2,1)S(1)}, u32[]{:S(2)}, u32[]{:S(2)}) collective-permute-start(bf16[1,2,2,2,256,128]{5,4,3,2,1,0:T(8,128)(2,1)S(1)} %add_convert_fusion.1), channel_id=1, source_target_pairs={{0,496},{16,0},{32,16},{48,32},{64,48},{80,64},{96,80},{112,96},{1... | collective-permute-start | bytes 1572872 | tf_op jit(solution)/shard_map/ppermute | solution.py:32
  52.3 14.1 %collective-permute-start.6 = (bf16[1,1,2,2,256,128]{5,4,3,2,1,0:T(8,128)(2,1)S(1)}, bf16[1,1,2,2,256,128]{5,4,3,2,1,0:T(8,128)(2,1)S(1)}, u32[]{:S(2)}, u32[]{:S(2)}) collective-permute-start(bf16[1,1,2,2,256,128]{5,4,3,2,1,0:T(8,128)(2,1)S(1)} %get-tuple-element.23), channel_id=1, source_target_pairs={{0,14},{2,0},{4,2},{6,4},{8,6},{10,8},{12,10},{14,12},{1,15},{3,1}... | collective-permute-start | bytes 786440 | tf_op jit(solution)/shard_map/ppermute | solution.py:32
  55.1 11.6 %collective-permute-start.7 = (bf16[2,1,2,1,2,256,128]{6,5,4,2,3,1,0:T(8,128)(2,1)S(1)}, bf16[2,1,2,1,2,256,128]{6,5,4,2,3,1,0:T(8,128)(2,1)S(1)}, u32[]{:S(2)}, u32[]{:S(2)}) collective-permute-start(bf16[2,1,2,1,2,256,128]{6,5,4,2,3,1,0:T(8,128)(2,1)S(1)} %pad_maximum_fusion.1), channel_id=1, source_target_pairs={{0,1},{1,0},{2,3},{3,2},{4,5},{5,4},{6,7},{7,6},{8,9},{9,8},{10,11... | collective-permute-start | bytes 1572872 | tf_op jit(solution)/shard_map/ppermute | solution.py:29
  58.8 11.9 %collective-permute-start.9 = (bf16[1,1,2,2,256,128]{5,4,3,1,2,0:T(8,128)(2,1)S(1)}, bf16[1,1,2,2,256,128]{5,4,3,1,2,0:T(8,128)(2,1)S(1)}, u32[]{:S(2)}, u32[]{:S(2)}) collective-permute-start(bf16[1,1,2,2,256,128]{5,4,3,1,2,0:T(8,128)(2,1)S(1)} %get-tuple-element.28), channel_id=1, source_target_pairs={{0,2},{2,4},{4,6},{6,8},{8,10},{10,12},{12,14},{14,0},{1,3},{3,5},... | collective-permute-start | bytes 786440 | tf_op jit(solution)/shard_map/ppermute | solution.py:33
  62.1 18.7 %collective-permute-start.8 = (bf16[1,2,2,2,256,128]{5,4,3,1,2,0:T(8,128)(2,1)S(1)}, bf16[1,2,2,2,256,128]{5,4,3,1,2,0:T(8,128)(2,1)S(1)}, u32[]{:S(2)}, u32[]{:S(2)}) collective-permute-start(bf16[1,2,2,2,256,128]{5,4,3,1,2,0:T(8,128)(2,1)S(1)} %fusion.8), channel_id=1, source_target_pairs={{0,16},{16,32},{32,48},{48,64},{64,80},{80,96},{96,112},{112,128},... | collective-permute-start | bytes 1572872 | tf_op jit(solution)/shard_map/ppermute | solution.py:33
  80.8 1.0 copy-start.4
  82.9 12.9 %all-to-all-start = ((bf16[8,256,128]{2,1,0:T(8,128)(2,1)}), bf16[8,256,128]{2,1,0:T(8,128)(2,1)S(1)}, u32[]{:S(2)}, u32[]{:S(2)}) async-start(bf16[8,256,128]{2,1,0:T(8,128)(2,1)} %broadcast_in_dim.4), calls=%async_computation | async-start | bytes 1048576 | tf_op jit(solution)/shard_map/all_to_all | solution.py:64
